TPU v7x, 256 devices: a whole 4x4x8 slice. The times are simulated.
256 devices in a mesh: ctx: 32 (over z, x), tp: 8 (over y, core).
Axes of the slice: x: 4, y: 4, z: 8, core: 2. Of those that a mesh axis runs over, the one named last changes fastest.
Arguments:
- activations: bfloat16 [8192, 4096], P('ctx'), may hold values from -38 to 38
- w_qkv: bfloat16 [4096, 6144], P(None, 'tp'), may hold values from -0.09375 to 0.09375
- matching: int32 [8, 32], P('tp'), may hold values from 0 to 31, each once within a row
- dropout_bits: int32 [8192, 512], P('ctx', 'tp'), may hold values from 0 to 65535
- out_grad: bfloat16 [8192, 2048], P('ctx', 'tp'), may hold values from -0.29882812 to 0.29882812
Outputs:
- attended: bfloat16 [8192, 2048], P('ctx', 'tp')
- input_grad: bfloat16 [8192, 4096], P('ctx', 'tp')
- weight_grad: bfloat16 [4096, 6144], P('ctx', 'tp')
Inputs may be any that keep to these rules, and one draw needn't show every extreme that they name: Each row of matching is a permutation of the 32 blocks.
All inputs are finite; a program needn't handle non-finite values.
Results may differ from a plain program's by a relative error of at most 0.019.
Values may be sent and summed in bfloat16 or wider, within the bound.
No kernel may reach another device: no remote copies, remote signals or barrier semaphores. Data moves between devices by JAX's collectives and lax.ppermute only.
A program may use at most 128 MiB of HBM per device.

v0:
```python
import jax
import jax.numpy as jnp
import numpy as np
from jax import lax
from jax.sharding import PartitionSpec as P

HD = 128
BLK = 256
HGROUP = 2
WORDS = 32


def unpack_bits(words):
    shifts = jnp.arange(16, dtype=jnp.int32)
    bits = jnp.bitwise_and(jnp.right_shift(words[..., None], shifts), 1)
    return bits.reshape(words.shape[:-1] + (words.shape[-1] * 16,)).astype(jnp.float32) * 2.0


def to_blocks(flat, width):
    row_total = flat.shape[0]
    head_count = flat.shape[1] // width
    return flat.reshape(row_total // BLK, BLK, head_count, width).transpose(2, 0, 1, 3)


def from_blocks(blocked):
    head_count, block_count, block_rows, width = blocked.shape
    return blocked.transpose(1, 2, 0, 3).reshape(block_count * block_rows, head_count * width)


def pick_rows(current, shard_rows, wanted_rows, first_row):
    row_count = shard_rows.shape[0]
    head_count = wanted_rows.shape[0]
    width = shard_rows.shape[1] // head_count
    by_head = shard_rows.reshape(row_count, head_count, width).transpose(1, 0, 2)
    offset = wanted_rows.reshape(head_count, -1) - first_row
    within = (offset >= 0) & (offset < row_count)
    picked = jnp.take_along_axis(by_head, jnp.clip(offset, 0, row_count - 1)[:, :, None], axis=1)
    merged = jnp.where(within[:, :, None], picked, current.reshape(head_count, -1, width))
    return merged.reshape(current.shape)


def per_device(activations, w_qkv, matching, dropout_bits, out_grad):
    f32 = jnp.float32
    local_tokens = activations.shape[0]
    head_count = out_grad.shape[1] // HD
    local_blocks = local_tokens // BLK
    score_scale = HD ** (-0.5)
    ctx_index = lax.axis_index("ctx")
    projected = jnp.dot(activations, w_qkv, preferred_element_type=f32).astype(jnp.bfloat16)
    projected = projected.reshape(local_tokens, head_count, 3, HD)
    query_flat = projected[:, :, 0].reshape(local_tokens, head_count * HD)
    key_flat = projected[:, :, 1].reshape(local_tokens, head_count * HD)
    value_flat = projected[:, :, 2].reshape(local_tokens, head_count * HD)
    query = to_blocks(query_flat, HD)
    key_own = to_blocks(key_flat, HD)
    value_own = to_blocks(value_flat, HD)
    head_match = matching[np.arange(head_count) // HGROUP]
    all_blocks = head_match.shape[1]
    matched = lax.dynamic_slice_in_dim(head_match, ctx_index * local_blocks, local_blocks, 1)
    in_block = jnp.arange(BLK, dtype=jnp.int32)
    key_rows = matched[:, :, None] * BLK + in_block
    empty_rows = jnp.zeros((head_count, local_blocks, BLK, HD), jnp.bfloat16)
    first_row = jnp.int32(0)
    key_far = pick_rows(
        empty_rows, lax.all_gather(key_flat, "ctx", axis=0, tiled=True), key_rows, first_row
    )
    value_far = pick_rows(
        empty_rows, lax.all_gather(value_flat, "ctx", axis=0, tiled=True), key_rows, first_row
    )
    keys = jnp.concatenate([key_own, key_far], 2)
    values = jnp.concatenate([value_own, value_far], 2)
    scores = jnp.einsum("hnqd,hnkd->hnqk", query, keys, preferred_element_type=f32) * score_scale
    row_max = jnp.max(scores, -1, keepdims=True)
    log_total = row_max + jnp.log(jnp.sum(jnp.exp(scores - row_max), -1, keepdims=True))
    probability = jnp.exp(scores - log_total)
    kept = unpack_bits(to_blocks(dropout_bits, WORDS))
    dropped = (probability * kept).astype(jnp.bfloat16)
    attended = jnp.einsum("hnqk,hnkd->hnqd", dropped, values, preferred_element_type=f32).astype(
        jnp.bfloat16
    )
    grad_out = to_blocks(out_grad, HD)
    grad_prob = jnp.einsum("hnqd,hnkd->hnqk", grad_out, values, preferred_element_type=f32) * kept
    row_delta = jnp.sum(probability * grad_prob, -1, keepdims=True)
    grad_score = (probability * (grad_prob - row_delta) * score_scale).astype(jnp.bfloat16)
    grad_query = jnp.einsum("hnqk,hnkd->hnqd", grad_score, keys, preferred_element_type=f32).astype(
        jnp.bfloat16
    )
    grad_keys = jnp.einsum("hnqk,hnqd->hnkd", grad_score, query, preferred_element_type=f32)
    grad_values = jnp.einsum("hnqk,hnqd->hnkd", dropped, grad_out, preferred_element_type=f32)
    inverse = (
        jnp.zeros_like(head_match)
        .at[np.arange(head_count)[:, None], head_match]
        .set(jnp.broadcast_to(jnp.arange(all_blocks, dtype=jnp.int32)[None, :], head_match.shape))
    )
    sources = lax.dynamic_slice_in_dim(inverse, ctx_index * local_blocks, local_blocks, 1)
    query_rows = sources[:, :, None] * BLK + in_block
    far_part = jnp.concatenate([grad_keys[:, :, BLK:], grad_values[:, :, BLK:]], -1).astype(
        jnp.bfloat16
    )
    far_flat = from_blocks(far_part)
    empty_terms = jnp.zeros((head_count, local_blocks, BLK, 2 * HD), jnp.bfloat16)
    returned = pick_rows(
        empty_terms, lax.all_gather(far_flat, "ctx", axis=0, tiled=True), query_rows, jnp.int32(0)
    )
    far_key = returned[..., :HD].astype(f32)
    far_value = returned[..., HD:].astype(f32)
    grad_key = (grad_keys[:, :, :BLK] + far_key).astype(jnp.bfloat16)
    grad_value = (grad_values[:, :, :BLK] + far_value).astype(jnp.bfloat16)
    stacked = jnp.stack([grad_query, grad_key, grad_value], 3)
    grad_qkv = stacked.transpose(1, 2, 0, 3, 4).reshape(local_tokens, head_count * 3 * HD)
    weight_grad = lax.psum_scatter(
        lax.dot_general(
            activations, grad_qkv, (((0,), (0,)), ((), ())), preferred_element_type=f32
        ).astype(jnp.bfloat16),
        "ctx",
        scatter_dimension=0,
        tiled=True,
    )
    input_grad = lax.psum_scatter(
        lax.dot_general(w_qkv, grad_qkv, (((1,), (1,)), ((), ())), preferred_element_type=f32),
        "tp",
        scatter_dimension=0,
        tiled=True,
    ).T.astype(jnp.bfloat16)
    return (from_blocks(attended), input_grad, weight_grad)


def solution(mesh):
    return jax.shard_map(
        per_device,
        mesh=mesh,
        in_specs=(P("ctx", None), P(None, "tp"), P("tp", None), P("ctx", "tp"), P("ctx", "tp")),
        out_specs=(P("ctx", "tp"), P("ctx", "tp"), P("ctx", "tp")),
        check_vma=False,
    )
```

profile of v0, /device:TPU:8, one launch (start us, length us, event | category | flops | bytes accessed | tf_op | source)
XLA Modules:
  0.0 628.7 jit_solution(16482032936210440719)
XLA Ops:
  7.2 0.0 all-gather.4.cloned.1.call-start
  7.3 1.5 copy-done
  8.8 4.6 convolution_convert_fusion.1
  13.3 0.2 copy.44
  13.5 0.7 fusion.41
  14.2 0.0 all-gather.4.cloned.1.call-update
  14.3 0.0 all-gather.6.cloned.1.call-start
  14.3 0.7 all-gather.6.cloned.1.call-update
  15.0 0.0 all-gather.8.cloned.1.call-start
  15.1 1.0 copy.74
  16.1 1.7 copy.73
  17.8 0.6 fusion.42
  18.4 0.6 or_bitcast_fusion
  19.1 0.1 shift_right_arithmetic.28
  19.1 0.1 copy.69
  19.2 0.8 copy.72
  20.0 0.1 shift_right_arithmetic.25
  20.1 1.4 copy.49
  21.5 0.6 and_bitcast_fusion
  22.1 0.6 compare_and_fusion.2
  22.7 77.1 %all-gather.4.cloned.1.call-done = bf16[8192,256]{0,1:T(8,128)(2,1)} async-done(((bf16[256,256]{0,1:T(8,128)(2,1)}), bf16[8192,256]{0,1:T(8,128)(2,1)}) %all-gather.4.cloned.1.call-update) | async-done | bytes 4194320 | tf_op jit(solution)/shard_map/all_gather | solution.py:65
  99.9 6.3 %copy.48 = bf16[8192,2,128]{2,0,1:T(8,128)(2,1)} copy(bf16[8192,2,128]{0,2,1:T(8,128)(2,1)} %bitcast.125) | data formatting | bytes 8388608 | tf_op jit(solution)/shard_map/reshape | solution.py:34
  106.2 80.0 %all-gather.6.cloned.1.call-done = bf16[8192,256]{0,1:T(8,128)(2,1)} async-done(((bf16[256,256]{0,1:T(8,128)(2,1)}), bf16[8192,256]{0,1:T(8,128)(2,1)}) %all-gather.6.cloned.1.call-update) | async-done | bytes 4194320 | tf_op jit(solution)/shard_map/all_gather | solution.py:68
  186.2 6.4 %copy.52 = bf16[8192,2,128]{2,0,1:T(8,128)(2,1)} copy(bf16[8192,2,128]{0,2,1:T(8,128)(2,1)} %bitcast.126) | data formatting | bytes 8388608 | tf_op jit(solution)/shard_map/reshape | solution.py:34
  192.6 6.7 %gather_fusion.1 = bf16[512,128]{1,0:T(8,128)(2,1)S(1)} fusion(bf16[2,8192,128]{2,1,0:T(8,128)(2,1)} %bitcast.123, s32[512]{0:T(512)S(1)} %bitcast.118), kind=kCustom, calls=%fused_computation.clone | custom fusion | bytes 266240 | tf_op jit(solution)/shard_map/jit(take_along_axis)/gather | solution.py:37
  199.3 6.7 %gather_fusion.2 = bf16[512,128]{1,0:T(8,128)(2,1)S(1)} fusion(bf16[2,8192,128]{2,1,0:T(8,128)(2,1)} %bitcast.124, s32[512]{0:T(512)S(1)} %bitcast.119), kind=kCustom, calls=%fused_computation.1.clone | custom fusion | bytes 266240 | tf_op jit(solution)/shard_map/jit(take_along_axis)/gather | solution.py:37
  206.0 0.2 fusion.25
  206.2 0.6 copy-done.4
  206.9 1.4 fusion.43
  208.2 0.3 exponential_reduce_fusion
  208.6 1.5 multiply_convert_fusion
  210.1 0.8 copy-done.1
  210.9 1.0 convolution_bitcast_fusion.2
  211.9 2.6 fusion.5
  214.5 5.2 convolution_bitcast_fusion.3
  219.7 1.0 slice.70
  220.7 1.0 slice.69
  221.7 0.7 pad_maximum_fusion
  222.4 0.0 all-gather.8.cloned.1.call-update
  222.4 0.2 reduce-scatter.5.cloned.1.call-start
  222.7 0.1 reshape.379
  222.8 0.1 reshape.381
  222.9 3.5 scatter_fusion
  226.3 0.2 multiply_reduce_fusion.1
  226.5 0.1 fusion.30
  226.6 0.1 compare_and_fusion.1
  226.7 4.6 fusion.7
  231.3 94.1 %all-gather.8.cloned.1.call-done = bf16[8192,512]{0,1:T(8,128)(2,1)} async-done(((bf16[256,512]{0,1:T(8,128)(2,1)}), bf16[8192,512]{0,1:T(8,128)(2,1)}) %all-gather.8.cloned.1.call-update) | async-done | bytes 8388624 | tf_op jit(solution)/shard_map/all_gather | solution.py:103
  325.4 12.0 %copy.59 = bf16[8192,2,256]{2,0,1:T(8,128)(2,1)} copy(bf16[8192,2,256]{0,2,1:T(8,128)(2,1)} %bitcast.122) | data formatting | bytes 16777216 | tf_op jit(solution)/shard_map/reshape | solution.py:34
  337.4 6.9 %gather_fusion = bf16[512,256]{1,0:T(8,128)(2,1)S(1)} fusion(bf16[2,8192,256]{2,1,0:T(8,128)(2,1)} %bitcast.121, s32[512]{0:T(512)S(1)} %bitcast.120), kind=kCustom, calls=%fused_computation.2 | custom fusion | bytes 528384 | tf_op jit(solution)/shard_map/jit(take_along_axis)/gather | solution.py:37
  344.3 0.1 copy.60
  344.5 1.0 fusion.21
  345.6 6.6 %convolution_bitcast_fusion = f32[4096,256]{0,1:T(8,128)} fusion(bf16[256,768]{0,1:T(8,128)(2,1)S(1)} %bitcast.128, bf16[4096,768]{1,0:T(8,128)(2,1)} %param.12), kind=kOutput, calls=%fused_computation.7 | convolution fusion | flops 1610612736 | bytes 10878976 | tf_op jit(solution)/shard_map/dot_general | solution.py:120
  352.2 0.0 reduce-scatter.5.cloned.1.call-update
  352.2 0.0 reduce-scatter.7.cloned.1.call-start
  352.3 4.5 fusion.1
  356.7 8.6 %copy.70 = bf16[4096,768]{1,0:T(8,128)(2,1)} copy(bf16[4096,768]{0,1:T(8,128)(2,1)} %fusion.1) | data formatting | bytes 12582912
  365.4 0.0 reduce-scatter.7.cloned.1.call-update
  365.4 1.0 copy-done.2
  366.4 0.3 convolution_convert_fusion.3
  366.7 0.8 copy.62
  367.5 20.7 %reduce-scatter.5.cloned.1.call-done = f32[512,256]{0,1:T(8,128)} async-done(((f32[4096,256]{0,1:T(8,128)}), f32[512,256]{0,1:T(8,128)}) %reduce-scatter.5.cloned.1.call-update) | async-done | bytes 524304 | tf_op jit(solution)/shard_map/reduce_scatter | solution.py:119
  388.2 1.8 convert_bitcast_fusion
  390.0 232.1 %reduce-scatter.7.cloned.1.call-done = bf16[128,768]{1,0:T(8,128)(2,1)} async-done(((bf16[4096,768]{1,0:T(8,128)(2,1)}), bf16[128,768]{1,0:T(8,128)(2,1)}) %reduce-scatter.7.cloned.1.call-update) | async-done | bytes 196624
  (24 shorter events, 0.2 us)
Async XLA Ops:
  7.2 1.6 copy-start
  7.2 10.6 %copy-start.7 = (s32[1,32]{1,0:T(1,128)S(1)}, s32[1,32]{1,0:T(1,128)}, u32[]{:S(2)}) copy-start(s32[1,32]{1,0:T(1,128)} %param.13) | copy-start | bytes 388
  7.2 11.9 %copy-start.5 = (bf16[256,256]{1,0:T(8,128)(2,1)S(1)}, bf16[256,256]{1,0:T(8,128)(2,1)}, u32[]{:S(2)}) copy-start(bf16[256,256]{1,0:T(8,128)(2,1)} %param.15) | copy-start | bytes 393220
  7.2 12.8 %copy-start.6 = (s32[256,64]{0,1:T(8,128)S(1)}, s32[256,64]{0,1:T(8,128)}, u32[]{:S(2)}) copy-start(s32[256,64]{0,1:T(8,128)} %param.14) | copy-start | bytes 196612
  7.2 92.7 %all-gather.4.cloned.1.call-start = ((), (), s32[]{:S(2)}) async-start(), calls=%async_computation.2 | async-start | bytes 4325376 | tf_op jit(solution)/shard_map/all_gather | solution.py:65
  14.3 172.0 %all-gather.6.cloned.1.call-start = ((), (), s32[]{:S(2)}) async-start(), calls=%async_computation.3 | async-start | bytes 4325376 | tf_op jit(solution)/shard_map/all_gather | solution.py:68
  15.0 310.4 %all-gather.8.cloned.1.call-start = ((), (), s32[]{:S(2)}) async-start(), calls=%async_computation.4 | async-start | bytes 8650752 | tf_op jit(solution)/shard_map/all_gather | solution.py:103
  206.2 0.7 copy-start.4
  210.1 0.8 copy-start.1
  222.4 165.8 %reduce-scatter.5.cloned.1.call-start = ((), (), s32[]{:S(2)}) async-start(), calls=%async_computation.5 | async-start | bytes 4718592 | tf_op jit(solution)/shard_map/reduce_scatter | solution.py:119
  325.4 19.1 %copy-start.3 = (f32[2,1,512,128]{2,3,0,1:T(8,128)S(1)}, f32[2,1,512,128]{2,3,0,1:T(8,128)}, u32[]{:S(2)}) copy-start(f32[2,1,512,128]{2,3,0,1:T(8,128)} %convolution_bitcast_fusion.2) | copy-start | bytes 1572868
  352.2 269.9 %reduce-scatter.7.cloned.1.call-start = ((), (), s32[]{:S(2)}) async-start(), calls=%async_computation.6 | async-start | bytes 6488064
  365.4 1.1 copy-start.2
Sparse Core Ops, SparseCore 0:
  14.4 85.4 all-gather.3
  102.9 83.2 all-gather.5
  222.5 102.8 all-gather.7
  352.4 35.8 reduce-scatter.4
  392.6 229.4 reduce-scatter.6
where the time goes:
time: 630 us; the launch traced here: 629 us
  waiting for transfers between devices  505 us (80%)
  local copies, waits for them, and re-layouts  70.1 us (11%)
  matrix products  30.7 us (5%)
  between operations  14 us (2%)
  other arithmetic  8.57 us (1%)
    unnamed x6, waiting for transfers between devices  233 us
    all_gather x1, waiting for transfers between devices, per_device(): lax.all_gather(far_flat, 'ctx', axis=0, tiled=True)  94.1 us
    all_gather x1, waiting for transfers between devices, per_device(): lax.all_gather(value_flat, 'ctx', axis=0, tiled=True)  80 us
    all_gather x1, waiting for transfers between devices, per_device(): lax.all_gather(key_flat, 'ctx', axis=0, tiled=True)  77.1 us
    reshape x3, local copies, waits for them, and re-layouts, pick_rows(): shard_rows.reshape(row_count, head_count, width).transpose(1, 0, 2)  24.7 us
    reduce_scatter x1, waiting for transfers between devices, per_device(): lax.psum_scatter(lax.dot_general(w_qkv, grad_qkv, (((1,), (1,)), ((), ())...  20.7 us
    gather x4, local copies, waits for them, and re-layouts, pick_rows(): jnp.take_along_axis(by_head, jnp.clip(offset, 0, row_count - 1)[:, :, Non...  20.4 us
    unnamed x23, local copies, waits for them, and re-layouts  16.8 us
  transfers between devices with their start and end apart: 5, of which 5 were waited for; matrix products, arithmetic and copies ran while one was open for 6% of the time, Pallas kernels for 0%

commit v1 on v0

v1 whole, which is shorter than its diff:
```python
import jax
import jax.numpy as jnp
import numpy as np
from jax import lax
from jax.sharding import Mesh, PartitionSpec as P

HD = 128
BLK = 256
HGROUP = 2
WORDS = 32


def unpack_bits(words):
    shifts = jnp.arange(16, dtype=jnp.int32)
    bits = jnp.bitwise_and(jnp.right_shift(words[..., None], shifts), 1)
    return bits.reshape(words.shape[:-1] + (words.shape[-1] * 16,)).astype(jnp.float32) * 2.0


def to_blocks(flat, width):
    row_total = flat.shape[0]
    head_count = flat.shape[1] // width
    return flat.reshape(row_total // BLK, BLK, head_count, width).transpose(2, 0, 1, 3)


def from_blocks(blocked):
    head_count, block_count, block_rows, width = blocked.shape
    return blocked.transpose(1, 2, 0, 3).reshape(block_count * block_rows, head_count * width)


CTX = ("z", "x")
TP = ("y", "c")


def route(payload, order):
    spread = lax.all_to_all(payload, CTX, 0, 0, tiled=True)
    chosen = jnp.take(spread, order, axis=0)
    return lax.all_to_all(chosen, CTX, 0, 0, tiled=True)


def to_pieces(blocked, pieces):
    lead = blocked.shape[:-2]
    rows, width = blocked.shape[-2:]
    split = blocked.reshape(lead + (pieces, rows // pieces, width))
    return jnp.moveaxis(split, len(lead), 0)


def from_pieces(spread):
    joined = jnp.moveaxis(spread, 0, -3)
    return joined.reshape(joined.shape[:-3] + (-1, joined.shape[-1]))


def ring_rs(chunks, axis, n):
    i = lax.axis_index(axis)
    if n == 2:
        other = lax.dynamic_index_in_dim(chunks, 1 - i, 0, keepdims=False)
        mine = lax.dynamic_index_in_dim(chunks, i, 0, keepdims=False)
        got = lax.ppermute(other, axis, [(0, 1), (1, 0)])
        return (got.astype(jnp.float32) + mine.astype(jnp.float32)).astype(chunks.dtype)
    half = chunks.shape[1] // 2
    cw = [(j, (j + 1) % n) for j in range(n)]
    ccw = [(j, (j - 1) % n) for j in range(n)]

    def take(k, part):
        block = lax.dynamic_index_in_dim(chunks, k % n, 0, keepdims=False)
        return block[:half] if part == 0 else block[half:]

    acc_a = take(i - 1 + n, 0)
    acc_b = take(i + 1, 1)
    for s in range(n - 1):
        got_a = lax.ppermute(acc_a, axis, cw)
        got_b = lax.ppermute(acc_b, axis, ccw)
        acc_a = (got_a.astype(jnp.float32) + take(i - s - 2 + 2 * n, 0).astype(jnp.float32)).astype(chunks.dtype)
        acc_b = (got_b.astype(jnp.float32) + take(i + s + 2, 1).astype(jnp.float32)).astype(chunks.dtype)
    return jnp.concatenate([acc_a, acc_b], 0)


def per_device(activations, w_qkv, matching, dropout_bits, out_grad):
    f32 = jnp.float32
    local_tokens = activations.shape[0]
    head_count = out_grad.shape[1] // HD
    score_scale = HD ** (-0.5)
    n_ctx = matching.shape[1]
    projected = jnp.dot(activations, w_qkv, preferred_element_type=f32).astype(jnp.bfloat16)
    projected = projected.reshape(local_tokens, head_count, 3, HD)
    query = to_blocks(projected[:, :, 0].reshape(local_tokens, head_count * HD), HD)
    key_own = to_blocks(projected[:, :, 1].reshape(local_tokens, head_count * HD), HD)
    value_own = to_blocks(projected[:, :, 2].reshape(local_tokens, head_count * HD), HD)
    order = matching[0]
    inverse = jnp.zeros_like(order).at[order].set(jnp.arange(n_ctx, dtype=order.dtype))
    own_kv = jnp.stack([key_own, value_own], 0)
    far_kv = from_pieces(route(to_pieces(own_kv, n_ctx), order))
    keys = jnp.concatenate([key_own, far_kv[0]], 2)
    values = jnp.concatenate([value_own, far_kv[1]], 2)
    scores = jnp.einsum("hnqd,hnkd->hnqk", query, keys, preferred_element_type=f32) * score_scale
    row_max = jnp.max(scores, -1, keepdims=True)
    log_total = row_max + jnp.log(jnp.sum(jnp.exp(scores - row_max), -1, keepdims=True))
    probability = jnp.exp(scores - log_total)
    kept = unpack_bits(to_blocks(dropout_bits, WORDS))
    dropped = (probability * kept).astype(jnp.bfloat16)
    attended = jnp.einsum("hnqk,hnkd->hnqd", dropped, values, preferred_element_type=f32).astype(
        jnp.bfloat16
    )
    grad_out = to_blocks(out_grad, HD)
    grad_prob = jnp.einsum("hnqd,hnkd->hnqk", grad_out, values, preferred_element_type=f32) * kept
    row_delta = jnp.sum(probability * grad_prob, -1, keepdims=True)
    grad_score = (probability * (grad_prob - row_delta) * score_scale).astype(jnp.bfloat16)
    grad_query = jnp.einsum("hnqk,hnkd->hnqd", grad_score, keys, preferred_element_type=f32).astype(
        jnp.bfloat16
    )
    grad_keys = jnp.einsum("hnqk,hnqd->hnkd", grad_score, query, preferred_element_type=f32)
    grad_values = jnp.einsum("hnqk,hnqd->hnkd", dropped, grad_out, preferred_element_type=f32)
    far_part = jnp.stack([grad_keys[:, :, BLK:], grad_values[:, :, BLK:]], 0).astype(jnp.bfloat16)
    returned = from_pieces(route(to_pieces(far_part, n_ctx), inverse))
    grad_key = (grad_keys[:, :, :BLK] + returned[0].astype(f32)).astype(jnp.bfloat16)
    grad_value = (grad_values[:, :, :BLK] + returned[1].astype(f32)).astype(jnp.bfloat16)
    stacked = jnp.stack([grad_query, grad_key, grad_value], 3)
    grad_qkv = stacked.transpose(1, 2, 0, 3, 4).reshape(local_tokens, head_count * 3 * HD)
    weight_part = lax.dot_general(
        activations, grad_qkv, (((0,), (0,)), ((), ())), preferred_element_type=f32
    ).astype(jnp.bfloat16)
    weight_grad = lax.psum_scatter(
        lax.psum_scatter(weight_part, "z", scatter_dimension=0, tiled=True),
        "x",
        scatter_dimension=0,
        tiled=True,
    )
    input_part = jnp.dot(grad_qkv, w_qkv.T, preferred_element_type=f32).astype(jnp.bfloat16)
    n_y = lax.psum(1, "y")
    width = input_part.shape[1] // (2 * n_y)
    by_core = input_part.reshape(local_tokens, n_y, 2, width).transpose(2, 1, 0, 3)
    core_sum = ring_rs(by_core, "c", 2)
    input_grad = ring_rs(core_sum, "y", n_y)
    return (from_blocks(attended), input_grad, weight_grad)


def solution(mesh):
    n_ctx, n_tp = mesh.devices.shape
    n_x = 4 if n_ctx % 4 == 0 else 1
    fine = Mesh(mesh.devices.reshape(n_ctx // n_x, n_x, n_tp // 2, 2), ("z", "x", "y", "c"))
    return jax.shard_map(
        per_device,
        mesh=fine,
        in_specs=(P(CTX, None), P(None, TP), P(TP, None), P(CTX, TP), P(CTX, TP)),
        out_specs=(P(CTX, TP), P(CTX, TP), P(CTX, TP)),
        check_vma=False,
    )
```

time: 630 us -> 225 us (0.36)
  waiting for transfers between devices: 505 us -> 90.8 us
  starting transfers between devices: 0.38 us -> 36.3 us
  local copies, waits for them, and re-layouts: 70.1 us -> 35.7 us
  other arithmetic: 8.57 us -> 15.2 us
    all_gather x3 -> x0, waiting for transfers between devices: 251 us -> none  [the longest x1 94.1 us: per_device(): lax.all_gather(far_flat, 'ctx', axis=0, tiled=True)]
    unnamed x6 -> x3, waiting for transfers between devices: 233 us -> 1.04 us
    all_to_all x0 -> x4, waiting for transfers between devices: none -> 39.1 us  [the longest x2 24.4 us: route(): spread = lax.all_to_all(payload, CTX, 0, 0, tiled=True)]
    all_to_all x0 -> x4, starting transfers between devices: none -> 25.1 us  [the longest x2 15.9 us: route(): spread = lax.all_to_all(payload, CTX, 0, 0, tiled=True)]
    reshape x3 -> x1, local copies, waits for them, and re-layouts: 24.7 us -> 4.66 us  [per_device(): input_part.reshape(local_tokens, n_y, 2, width).transpose(2, 1, 0, 3)]
    gather x4 -> x2, local copies, waits for them, and re-layouts: 20.4 us -> 2.84 us  [route(): chosen = jnp.take(spread, order, axis=0)]
    reduce_scatter x1, waiting for transfers between devices: 20.7 us -> 36.6 us  [per_device(): lax.psum_scatter(weight_part, 'z', scatter_dimension=0, tiled=True)]
    ppermute x0 -> x7, waiting for transfers between devices: none -> 14.1 us  [the longest x3 7.17 us: ring_rs(): got_a = lax.ppermute(acc_a, axis, cw)]
  transfers between devices with their start and end apart: 5 -> 13, of which waited for: 5 -> 11; matrix products, arithmetic and copies ran while one was open for 6% -> 19% of each run, Pallas kernels for 0% -> 0%
where the time goes in v1:
time: 225 us; the launch traced here: 224 us
  waiting for transfers between devices  90.8 us (40%)
  starting transfers between devices  36.3 us (16%)
  local copies, waits for them, and re-layouts  35.7 us (16%)
  matrix products  31.2 us (14%)
  other arithmetic  15.2 us (7%)
  between operations  14.4 us (6%)
    reduce_scatter x1, waiting for transfers between devices, per_device(): lax.psum_scatter(weight_part, 'z', scatter_dimension=0, tiled=True)  36.6 us
    all_to_all x2, waiting for transfers between devices, route(): spread = lax.all_to_all(payload, CTX, 0, 0, tiled=True)  24.4 us
    all_to_all x2, starting transfers between devices, route(): spread = lax.all_to_all(payload, CTX, 0, 0, tiled=True)  15.9 us
    all_to_all x2, waiting for transfers between devices, route(): return lax.all_to_all(chosen, CTX, 0, 0, tiled=True)  14.6 us
    all_to_all x2, starting transfers between devices, route(): return lax.all_to_all(chosen, CTX, 0, 0, tiled=True)  9.17 us
    dynamic_slice x1, local copies, waits for them, and re-layouts, ring_rs(): mine = lax.dynamic_index_in_dim(chunks, i, 0, keepdims=False)  7.92 us
    unnamed x25, local copies, waits for them, and re-layouts  7.3 us
    ppermute x3, waiting for transfers between devices, ring_rs(): got_a = lax.ppermute(acc_a, axis, cw)  7.17 us
  transfers between devices with their start and end apart: 13, of which 11 were waited for; matrix products, arithmetic and copies ran while one was open for 19% of the time, Pallas kernels for 0%

profile of v1, /device:TPU:8, one launch (start us, length us, event | category | flops | bytes accessed | tf_op | source)
XLA Modules:
  0.0 223.7 jit_solution(87690824138475214)
XLA Ops:
  7.2 1.6 copy-done
  8.8 4.6 %convolution_convert_fusion.2 = bf16[256,768]{1,0:T(8,128)(2,1)S(1)} fusion(bf16[256,4096]{1,0:T(8,128)(2,1)S(1)} %copy-done, bf16[4096,768]{1,0:T(8,128)(2,1)} %param.8), kind=kOutput, calls=%fused_computation.16 | convolution fusion | flops 1610809344 | bytes 8781824 | tf_op jit(solution)/shard_map/dot_general | solution.py:83
  13.9 0.7 copy.63
  14.6 11.3 %all-to-all-start = ((bf16[32,2,2,1,8,128]{5,4,2,1,3,0:T(8,128)(2,1)}), bf16[32,2,2,1,8,128]{5,4,2,1,3,0:T(8,128)(2,1)S(1)}, u32[]{:S(2)}, u32[]{:S(2)}) async-start(bf16[32,2,2,1,8,128]{5,4,2,1,3,0:T(8,128)(2,1)} %copy.63), calls=%async_computation | async-start | bytes 524288 | tf_op jit(solution)/shard_map/all_to_all | solution.py:35
  26.0 12.8 %all-to-all-done = bf16[32,2,2,1,8,128]{5,4,2,1,3,0:T(8,128)(2,1)S(1)} async-done(((bf16[32,2,2,1,8,128]{5,4,2,1,3,0:T(8,128)(2,1)}), bf16[32,2,2,1,8,128]{5,4,2,1,3,0:T(8,128)(2,1)S(1)}, u32[]{:S(2)}, u32[]{:S(2)}) %all-to-all-start) | async-done | bytes 262176 | tf_op jit(solution)/shard_map/all_to_all | solution.py:35
  38.7 0.6 gather_fusion
  39.3 0.8 fusion.29
  40.2 4.6 %all-to-all-start.1 = ((bf16[32,2,2,1,8,128]{5,4,2,1,3,0:T(8,128)(2,1)}), bf16[32,2,2,1,8,128]{5,4,2,1,3,0:T(8,128)(2,1)}, u32[]{:S(2)}, u32[]{:S(2)}) async-start(bf16[32,2,2,1,8,128]{5,4,2,1,3,0:T(8,128)(2,1)} %fusion.29), calls=%async_computation.1 | async-start | bytes 524288 | tf_op jit(solution)/shard_map/all_to_all | solution.py:37
  44.9 0.8 copy.97
  45.6 0.9 shift_right_arithmetic.25
  46.6 1.3 copy.66
  47.9 0.7 scatter_custom_fusion
  48.6 8.1 %all-to-all-done.1 = bf16[32,2,2,1,8,128]{5,4,2,1,3,0:T(8,128)(2,1)} async-done(((bf16[32,2,2,1,8,128]{5,4,2,1,3,0:T(8,128)(2,1)}), bf16[32,2,2,1,8,128]{5,4,2,1,3,0:T(8,128)(2,1)}, u32[]{:S(2)}, u32[]{:S(2)}) %all-to-all-start.1) | async-done | bytes 262176 | tf_op jit(solution)/shard_map/all_to_all | solution.py:37
  56.7 1.0 copy.116
  57.7 0.7 slice_bitcast_fusion.2
  58.3 0.8 copy.67
  59.1 1.4 fusion.52
  61.5 1.3 fusion.6
  62.7 1.1 convolution_bitcast_fusion.1
  63.8 5.2 %convolution_bitcast_fusion.2 = f32[2,1,512,128]{2,3,0,1:T(8,128)} fusion(f32[2,256,512]{2,1,0:T(8,128)} %fusion.6, f32[2,256,512]{2,1,0:T(8,128)S(1)} %get-tuple-element.27, f32[2,256]{1,0:T(2,128)S(1)} %log_add_fusion, bf16[256,2,1,128]{3,0,1,2:T(8,128)(2,1)} %copy.97), kind=kOutput, calls=%fused_computation.18 | convolution fusion | flops 68944896 | bytes 2754560 | tf_op jit(solution)/shard_map/hnqk,hnqd->hnkd/dot_general | solution.py:110
  69.0 1.0 slice.133
  70.0 0.8 copy.74
  70.8 1.0 slice.132
  71.7 0.8 copy.77
  72.5 1.0 maximum_bitcast_fusion.4
  73.5 0.7 copy.78
  74.3 4.6 %all-to-all-start.2 = ((bf16[32,2,2,1,8,128]{5,4,2,1,3,0:T(8,128)(2,1)}), bf16[32,2,2,1,8,128]{5,4,2,1,3,0:T(8,128)(2,1)}, u32[]{:S(2)}, u32[]{:S(2)}) async-start(bf16[32,2,2,1,8,128]{5,4,2,1,3,0:T(8,128)(2,1)} %copy.78), calls=%async_computation.2 | async-start | bytes 524288 | tf_op jit(solution)/shard_map/all_to_all | solution.py:35
  78.9 11.7 %all-to-all-done.2 = bf16[32,2,2,1,8,128]{5,4,2,1,3,0:T(8,128)(2,1)} async-done(((bf16[32,2,2,1,8,128]{5,4,2,1,3,0:T(8,128)(2,1)}), bf16[32,2,2,1,8,128]{5,4,2,1,3,0:T(8,128)(2,1)}, u32[]{:S(2)}, u32[]{:S(2)}) %all-to-all-start.2) | async-done | bytes 262176 | tf_op jit(solution)/shard_map/all_to_all | solution.py:35
  90.6 2.2 gather_fusion.1
  92.8 1.8 fusion.28
  94.6 4.6 %all-to-all-start.3 = ((bf16[32,2,2,1,8,128]{5,4,2,1,3,0:T(8,128)(2,1)}), bf16[32,2,2,1,8,128]{5,4,2,1,3,0:T(8,128)(2,1)}, u32[]{:S(2)}, u32[]{:S(2)}) async-start(bf16[32,2,2,1,8,128]{5,4,2,1,3,0:T(8,128)(2,1)} %fusion.28), calls=%async_computation.3 | async-start | bytes 524288 | tf_op jit(solution)/shard_map/all_to_all | solution.py:37
  99.2 5.1 %fusion.8 = bf16[2,1,256,1,128]{2,4,0,3,1:T(8,128)(2,1)} fusion(f32[2,256,512]{2,1,0:T(8,128)} %fusion.6, f32[2,256,512]{2,1,0:T(8,128)S(1)} %get-tuple-element.27, f32[2,256]{1,0:T(2,128)S(1)} %log_add_fusion, bf16[2,1,256,128]{3,2,0,1:T(8,128)(2,1)S(1)} %copy-done.6, bf16[2,1,256,128]{3,2,0,1:T(8,128)(2,1)S(1)} %bitcast.180), kind=kOutput, calls=%fused_computation.21 | convolution fusion | flops 69534720 | bytes 2492416 | tf_op jit(solution)/shard_map/hnqk,hnkd->hnqd/dot_general | solution.py:107
  104.3 6.5 %all-to-all-done.3 = bf16[32,2,2,1,8,128]{5,4,2,1,3,0:T(8,128)(2,1)} async-done(((bf16[32,2,2,1,8,128]{5,4,2,1,3,0:T(8,128)(2,1)}), bf16[32,2,2,1,8,128]{5,4,2,1,3,0:T(8,128)(2,1)}, u32[]{:S(2)}, u32[]{:S(2)}) %all-to-all-start.3) | async-done | bytes 262176 | tf_op jit(solution)/shard_map/all_to_all | solution.py:37
  110.9 1.0 copy.115
  111.9 0.7 fusion.33
  112.7 1.1 copy.82
  113.8 1.0 fusion.30
  115.0 4.5 %fusion.1 = bf16[4096,768]{0,1:T(8,128)(2,1)} fusion(bf16[256,768]{0,1:T(8,128)(2,1)S(1)} %bitcast.175, bf16[256,4096]{1,0:T(8,128)(2,1)S(1)} %copy-done), kind=kOutput, calls=%fused_computation.5 | convolution fusion | flops 1613758464 | bytes 8781824 | tf_op jit(solution)/shard_map/dot_general | solution.py:118
  119.7 6.0 %convolution_convert_fusion.1 = bf16[256,4096]{1,0:T(8,128)(2,1)} fusion(bf16[256,768]{0,1:T(8,128)(2,1)S(1)} %bitcast.176, bf16[4096,768]{1,0:T(8,128)(2,1)} %param.8), kind=kOutput, calls=%fused_computation.6 | convolution fusion | flops 1611661312 | bytes 8781824 | tf_op jit(solution)/shard_map/dot_general | solution.py:127
  125.7 4.7 %reshape.265 = bf16[256,4,2,512]{3,2,1,0:T(2,128)(2,1)} reshape(bf16[256,4096]{1,0:T(8,128)(2,1)} %convolution_convert_fusion.1) | data formatting | bytes 4194304 | tf_op jit(solution)/shard_map/reshape | solution.py:130
  130.4 7.9 %constant_dynamic-slice_fusion = (bf16[256,4,1,512]{3,2,1,0:T(2,128)(2,1)}, bf16[256,4,1,512]{3,2,1,0:T(2,128)(2,1)S(1)}) fusion(bf16[256,4,2,512]{3,2,1,0:T(2,128)(2,1)} %reshape.265, s32[]{:T(128)S(6)} %select_n.86, s32[]{:T(128)S(6)} %select_n.85), kind=kLoop, calls=%fused_computation.91 | loop fusion | bytes 4194312 | tf_op jit(solution)/shard_map/jit(dynamic_index_in_dim)/dynamic_slice | solution.py:56
  139.0 2.7 %collective-permute-done = bf16[4,256,512]{2,1,0:T(8,128)(2,1)} collective-permute-done((bf16[4,256,512]{2,1,0:T(8,128)(2,1)S(1)}, bf16[4,256,512]{2,1,0:T(8,128)(2,1)}, u32[]{:S(2)}, u32[]{:S(2)}) %collective-permute-start) | collective-permute-done | bytes 1048608 | tf_op jit(solution)/shard_map/ppermute | solution.py:57
  141.8 2.6 %fusion.2 = bf16[4,256,512]{2,1,0:T(8,128)(2,1)S(1)} fusion(bf16[4,256,512]{2,1,0:T(8,128)(2,1)} %collective-permute-done, bf16[256,4,1,512]{3,2,1,0:T(2,128)(2,1)} %get-tuple-element.13), kind=kLoop, calls=%fused_computation.8 | loop fusion | flops 2097152 | bytes 3145728 | tf_op jit(solution)/shard_map/convert_element_type | solution.py:58
  144.4 1.6 collective-permute-start.1
  146.0 4.1 %collective-permute-done.1 = bf16[128,512]{1,0:T(8,128)(2,1)} collective-permute-done((bf16[128,512]{1,0:T(8,128)(2,1)S(1)}, bf16[128,512]{1,0:T(8,128)(2,1)}, u32[]{:S(2)}, u32[]{:S(2)}) %collective-permute-start.1) | collective-permute-done | bytes 131104 | tf_op jit(solution)/shard_map/ppermute | solution.py:70
  150.1 1.6 fusion.27
  151.7 1.6 collective-permute-start.2
  153.3 36.6 %reduce-scatter.5.cloned.1.call-done = bf16[512,768]{0,1:T(8,128)(2,1)} async-done(((bf16[4096,768]{0,1:T(8,128)(2,1)}), bf16[512,768]{0,1:T(8,128)(2,1)}) %reduce-scatter.5.cloned.1.call-update) | async-done | bytes 786448 | tf_op jit(solution)/shard_map/reduce_scatter | solution.py:122
  189.9 2.3 %copy.95 = bf16[512,768]{1,0:T(8,128)(2,1)} copy(bf16[512,768]{0,1:T(8,128)(2,1)} %reduce-scatter.5.cloned.1.call-done) | data formatting | bytes 1572864
  192.3 0.6 collective-permute-start.4
  192.9 1.6 fusion.26
  194.5 1.5 collective-permute-start.3
  196.0 1.7 collective-permute-done.4
  197.6 3.1 %collective-permute-done.3 = bf16[128,512]{1,0:T(8,128)(2,1)} collective-permute-done((bf16[128,512]{1,0:T(8,128)(2,1)}, bf16[128,512]{1,0:T(8,128)(2,1)}, u32[]{:S(2)}, u32[]{:S(2)}) %collective-permute-start.3) | collective-permute-done | bytes 131104 | tf_op jit(solution)/shard_map/ppermute | solution.py:70
  200.7 1.0 fusion.25
  201.7 3.1 %collective-permute-start.5 = (bf16[128,512]{1,0:T(8,128)(2,1)S(1)}, bf16[128,512]{1,0:T(8,128)(2,1)S(1)}, u32[]{:S(2)}, u32[]{:S(2)}) collective-permute-start(bf16[128,512]{1,0:T(8,128)(2,1)S(1)} %get-tuple-element.16), channel_id=1, source_target_pairs={{0,6},{2,0},{4,2},{6,4},{1,7},{3,1},{5,3},{7,5},{8,14},{10,8},{12,... | collective-permute-start | bytes 393224 | tf_op jit(solution)/shard_map/ppermute | solution.py:71
  204.8 2.5 %collective-permute-done.5 = bf16[128,512]{1,0:T(8,128)(2,1)S(1)} collective-permute-done((bf16[128,512]{1,0:T(8,128)(2,1)S(1)}, bf16[128,512]{1,0:T(8,128)(2,1)S(1)}, u32[]{:S(2)}, u32[]{:S(2)}) %collective-permute-start.5) | collective-permute-done | bytes 131104 | tf_op jit(solution)/shard_map/ppermute | solution.py:71
  207.4 0.7 fusion.23
  208.0 2.4 %collective-permute-start.6 = (bf16[128,512]{1,0:T(8,128)(2,1)}, bf16[128,512]{1,0:T(8,128)(2,1)}, u32[]{:S(2)}, u32[]{:S(2)}) collective-permute-start(bf16[128,512]{1,0:T(8,128)(2,1)} %fusion.23), channel_id=1, source_target_pairs={{0,6},{2,0},{4,2},{6,4},{1,7},{3,1},{5,3},{7,5},{8,14},{10,8},{12,... | collective-permute-start | bytes 393224 | tf_op jit(solution)/shard_map/ppermute | solution.py:71
  210.5 2.0 convolution_convert_fusion.4
  212.5 1.7 copy.86
  214.2 0.9 fusion.22
  215.1 0.7 pad_maximum_fusion
  215.8 1.0 reduce-scatter.7.cloned.1.call-done
  (50 shorter events, 2.8 us)
Async XLA Ops:
  7.2 1.6 copy-start
  13.3 12.6 %copy-start.9 = (s32[1,32]{1,0:T(1,128)S(1)}, s32[1,32]{1,0:T(1,128)}, u32[]{:S(2)}) copy-start(s32[1,32]{1,0:T(1,128)} %param.9) | copy-start | bytes 388
  13.5 31.3 %copy-start.7 = (bf16[256,256]{1,0:T(8,128)(2,1)S(1)}, bf16[256,256]{1,0:T(8,128)(2,1)}, u32[]{:S(2)}) copy-start(bf16[256,256]{1,0:T(8,128)(2,1)} %param.11) | copy-start | bytes 393220
  14.6 24.1 %all-to-all-start = ((bf16[32,2,2,1,8,128]{5,4,2,1,3,0:T(8,128)(2,1)}), bf16[32,2,2,1,8,128]{5,4,2,1,3,0:T(8,128)(2,1)S(1)}, u32[]{:S(2)}, u32[]{:S(2)}) async-start(bf16[32,2,2,1,8,128]{5,4,2,1,3,0:T(8,128)(2,1)} %copy.63), calls=%async_computation | async-start | bytes 524288 | tf_op jit(solution)/shard_map/all_to_all | solution.py:35
  40.2 16.5 %all-to-all-start.1 = ((bf16[32,2,2,1,8,128]{5,4,2,1,3,0:T(8,128)(2,1)}), bf16[32,2,2,1,8,128]{5,4,2,1,3,0:T(8,128)(2,1)}, u32[]{:S(2)}, u32[]{:S(2)}) async-start(bf16[32,2,2,1,8,128]{5,4,2,1,3,0:T(8,128)(2,1)} %fusion.29), calls=%async_computation.1 | async-start | bytes 524288 | tf_op jit(solution)/shard_map/all_to_all | solution.py:37
  59.1 1.8 copy-start.1
  60.5 0.9 copy-start.4
  61.5 1.3 copy-start.2
  72.5 26.7 %copy-start.6 = (bf16[2,1,256,128]{3,2,0,1:T(8,128)(2,1)S(1)}, bf16[2,1,256,128]{3,2,0,1:T(8,128)(2,1)}, u32[]{:S(2)}) copy-start(bf16[2,1,256,128]{3,2,0,1:T(8,128)(2,1)} %get-tuple-element.25) | copy-start | bytes 393220
  74.3 16.3 %all-to-all-start.2 = ((bf16[32,2,2,1,8,128]{5,4,2,1,3,0:T(8,128)(2,1)}), bf16[32,2,2,1,8,128]{5,4,2,1,3,0:T(8,128)(2,1)}, u32[]{:S(2)}, u32[]{:S(2)}) async-start(bf16[32,2,2,1,8,128]{5,4,2,1,3,0:T(8,128)(2,1)} %copy.78), calls=%async_computation.2 | async-start | bytes 524288 | tf_op jit(solution)/shard_map/all_to_all | solution.py:35
  94.6 16.3 %all-to-all-start.3 = ((bf16[32,2,2,1,8,128]{5,4,2,1,3,0:T(8,128)(2,1)}), bf16[32,2,2,1,8,128]{5,4,2,1,3,0:T(8,128)(2,1)}, u32[]{:S(2)}, u32[]{:S(2)}) async-start(bf16[32,2,2,1,8,128]{5,4,2,1,3,0:T(8,128)(2,1)} %fusion.28), calls=%async_computation.3 | async-start | bytes 524288 | tf_op jit(solution)/shard_map/all_to_all | solution.py:37
  99.2 90.8 %reduce-scatter.5.cloned.1.call-start = ((), (), s32[]{:S(2)}) async-start(), calls=%async_computation.6 | async-start | bytes 7077888 | tf_op jit(solution)/shard_map/reduce_scatter | solution.py:122
  104.3 9.5 %copy-start.3 = (f32[2,1,512,128]{2,3,0,1:T(8,128)S(1)}, f32[2,1,512,128]{2,3,0,1:T(8,128)}, u32[]{:S(2)}) copy-start(f32[2,1,512,128]{2,3,0,1:T(8,128)} %convolution_bitcast_fusion.1) | copy-start | bytes 1572868
  104.3 10.5 %copy-start.8 = (bf16[2,1,256,1,128]{2,4,0,3,1:T(8,128)(2,1)S(1)}, bf16[2,1,256,1,128]{2,4,0,3,1:T(8,128)(2,1)}, u32[]{:S(2)}) copy-start(bf16[2,1,256,1,128]{2,4,0,3,1:T(8,128)(2,1)} %fusion.8) | copy-start | bytes 393220
  119.5 97.4 %reduce-scatter.7.cloned.1.call-start = ((), (), s32[]{:S(2)}) async-start(), calls=%async_computation.7 | async-start | bytes 983040
  138.9 2.9 %collective-permute-start = (bf16[4,256,512]{2,1,0:T(8,128)(2,1)S(1)}, bf16[4,256,512]{2,1,0:T(8,128)(2,1)}, u32[]{:S(2)}, u32[]{:S(2)}) collective-permute-start(bf16[4,256,512]{2,1,0:T(8,128)(2,1)S(1)} %bitcast.181), channel_id=1, source_target_pairs={{0,1},{1,0},{2,3},{3,2},{4,5},{5,4},{6,7},{7,6},{8,9},{9,8},{10,11... | collective-permute-start | bytes 3145736 | tf_op jit(solution)/shard_map/ppermute | solution.py:57
  144.4 5.7 %collective-permute-start.1 = (bf16[128,512]{1,0:T(8,128)(2,1)S(1)}, bf16[128,512]{1,0:T(8,128)(2,1)}, u32[]{:S(2)}, u32[]{:S(2)}) collective-permute-start(bf16[128,512]{1,0:T(8,128)(2,1)S(1)} %get-tuple-element.17), channel_id=1, source_target_pairs={{0,2},{2,4},{4,6},{6,0},{1,3},{3,5},{5,7},{7,1},{8,10},{10,12},{12... | collective-permute-start | bytes 393224 | tf_op jit(solution)/shard_map/ppermute | solution.py:70
  151.7 58.8 %copy-start.5 = (bf16[2,1,256,128]{2,3,0,1:T(8,128)(2,1)S(1)}, bf16[2,1,256,128]{2,3,0,1:T(8,128)(2,1)}, u32[]{:S(2)}) copy-start(bf16[2,1,256,128]{2,3,0,1:T(8,128)(2,1)} %copy.67) | copy-start | bytes 393220
  151.7 41.2 %collective-permute-start.2 = (bf16[128,512]{1,0:T(8,128)(2,1)}, bf16[128,512]{1,0:T(8,128)(2,1)}, u32[]{:S(2)}, u32[]{:S(2)}) collective-permute-start(bf16[128,512]{1,0:T(8,128)(2,1)} %fusion.27), channel_id=1, source_target_pairs={{0,2},{2,4},{4,6},{6,0},{1,3},{3,5},{5,7},{7,1},{8,10},{10,12},{12... | collective-permute-start | bytes 393224 | tf_op jit(solution)/shard_map/ppermute | solution.py:70
  192.3 5.4 %collective-permute-start.4 = (bf16[128,512]{1,0:T(8,128)(2,1)S(1)}, bf16[128,512]{1,0:T(8,128)(2,1)}, u32[]{:S(2)}, u32[]{:S(2)}) collective-permute-start(bf16[128,512]{1,0:T(8,128)(2,1)S(1)} %get-tuple-element.18), channel_id=1, source_target_pairs={{0,6},{2,0},{4,2},{6,4},{1,7},{3,1},{5,3},{7,5},{8,14},{10,8},{12,... | collective-permute-start | bytes 393224 | tf_op jit(solution)/shard_map/ppermute | solution.py:71
  194.5 6.2 %collective-permute-start.3 = (bf16[128,512]{1,0:T(8,128)(2,1)}, bf16[128,512]{1,0:T(8,128)(2,1)}, u32[]{:S(2)}, u32[]{:S(2)}) collective-permute-start(bf16[128,512]{1,0:T(8,128)(2,1)} %fusion.26), channel_id=1, source_target_pairs={{0,2},{2,4},{4,6},{6,0},{1,3},{3,5},{5,7},{7,1},{8,10},{10,12},{12... | collective-permute-start | bytes 393224 | tf_op jit(solution)/shard_map/ppermute | solution.py:70
  201.7 5.6 %collective-permute-start.5 = (bf16[128,512]{1,0:T(8,128)(2,1)S(1)}, bf16[128,512]{1,0:T(8,128)(2,1)S(1)}, u32[]{:S(2)}, u32[]{:S(2)}) collective-permute-start(bf16[128,512]{1,0:T(8,128)(2,1)S(1)} %get-tuple-element.16), channel_id=1, source_target_pairs={{0,6},{2,0},{4,2},{6,4},{1,7},{3,1},{5,3},{7,5},{8,14},{10,8},{12,... | collective-permute-start | bytes 393224 | tf_op jit(solution)/shard_map/ppermute | solution.py:71
  208.0 6.1 %collective-permute-start.6 = (bf16[128,512]{1,0:T(8,128)(2,1)}, bf16[128,512]{1,0:T(8,128)(2,1)}, u32[]{:S(2)}, u32[]{:S(2)}) collective-permute-start(bf16[128,512]{1,0:T(8,128)(2,1)} %fusion.23), channel_id=1, source_target_pairs={{0,6},{2,0},{4,2},{6,4},{1,7},{3,1},{5,3},{7,5},{8,14},{10,8},{12,... | collective-permute-start | bytes 393224 | tf_op jit(solution)/shard_map/ppermute | solution.py:71
Sparse Core Ops, SparseCore 0:
  119.6 70.2 reduce-scatter.4
  193.1 23.7 reduce-scatter.6

commit v2 on v1

--- a/solution.py
+++ b/solution.py
@@ -74,6 +74,17 @@
     return jnp.concatenate([acc_a, acc_b], 0)
 
 
+def weight_term(activations, cols):
+    return lax.dot_general(
+        activations, cols, (((0,), (0,)), ((), ())), preferred_element_type=jnp.float32
+    ).astype(jnp.bfloat16)
+
+
+def reduce_ctx(part):
+    part = lax.psum_scatter(part, "z", scatter_dimension=0, tiled=True)
+    return lax.psum_scatter(part, "x", scatter_dimension=0, tiled=True)
+
+
 def per_device(activations, w_qkv, matching, dropout_bits, out_grad):
     f32 = jnp.float32
     local_tokens = activations.shape[0]
@@ -115,20 +126,20 @@
     grad_value = (grad_values[:, :, :BLK] + returned[1].astype(f32)).astype(jnp.bfloat16)
     stacked = jnp.stack([grad_query, grad_key, grad_value], 3)
     grad_qkv = stacked.transpose(1, 2, 0, 3, 4).reshape(local_tokens, head_count * 3 * HD)
-    weight_part = lax.dot_general(
-        activations, grad_qkv, (((0,), (0,)), ((), ())), preferred_element_type=f32
-    ).astype(jnp.bfloat16)
-    weight_grad = lax.psum_scatter(
-        lax.psum_scatter(weight_part, "z", scatter_dimension=0, tiled=True),
-        "x",
-        scatter_dimension=0,
-        tiled=True,
-    )
-    input_part = jnp.dot(grad_qkv, w_qkv.T, preferred_element_type=f32).astype(jnp.bfloat16)
+    query_cols = grad_query.transpose(1, 2, 0, 3).reshape(local_tokens, head_count * HD)
+    kv_cols = jnp.stack([grad_key, grad_value], 3).transpose(1, 2, 0, 3, 4)
+    kv_cols = kv_cols.reshape(local_tokens, head_count * 2 * HD)
+    weight_q = reduce_ctx(weight_term(activations, query_cols))
+    weight_kv = reduce_ctx(weight_term(activations, kv_cols))
+    rows = weight_q.shape[0]
+    weight_grad = jnp.concatenate(
+        [weight_q.reshape(rows, head_count, 1, HD), weight_kv.reshape(rows, head_count, 2, HD)], 2
+    ).reshape(rows, head_count * 3 * HD)
     n_y = lax.psum(1, "y")
-    width = input_part.shape[1] // (2 * n_y)
-    by_core = input_part.reshape(local_tokens, n_y, 2, width).transpose(2, 1, 0, 3)
-    core_sum = ring_rs(by_core, "c", 2)
+    width = activations.shape[1] // (2 * n_y)
+    w_split = w_qkv.reshape(n_y, 2, width, w_qkv.shape[1])
+    by_core = jnp.einsum("tk,ycwk->cytw", grad_qkv, w_split, preferred_element_type=f32)
+    core_sum = ring_rs(by_core.astype(jnp.bfloat16), "c", 2)
     input_grad = ring_rs(core_sum, "y", n_y)
     return (from_blocks(attended), input_grad, weight_grad)
 

time: 225 us -> 239 us (1.062)
  blocking collectives: 0 us -> 18.2 us
  waiting for transfers between devices: 90.8 us -> 106 us
  starting transfers between devices: 36.3 us -> 25.2 us
  local copies, waits for them, and re-layouts: 35.7 us -> 28.5 us
    unnamed x3 -> x6, waiting for transfers between devices: 1.04 us -> 34 us
    all_to_all x0 -> x1, blocking collectives: none -> 18.2 us  [route(): return lax.all_to_all(chosen, CTX, 0, 0, tiled=True)]
    reduce_scatter x1 -> x2, waiting for transfers between devices: 36.6 us -> 23.9 us  [reduce_ctx(): part = lax.psum_scatter(part, 'z', scatter_dimension=0, tiled=True)]
    dynamic_slice x1 -> x0, local copies, waits for them, and re-layouts: 7.92 us -> none  [ring_rs(): mine = lax.dynamic_index_in_dim(chunks, i, 0, keepdims=False)]
    unnamed x25 -> x30, local copies, waits for them, and re-layouts: 7.3 us -> 14.6 us
    all_to_all x2 -> x1, waiting for transfers between devices: 14.6 us -> 8.28 us  [route(): return lax.all_to_all(chosen, CTX, 0, 0, tiled=True)]
    reshape x1 -> x0, local copies, waits for them, and re-layouts: 4.66 us -> none  [per_device(): input_part.reshape(local_tokens, n_y, 2, width).transpose(2, 1, 0, 3)]
    all_to_all x2 -> x1, starting transfers between devices: 9.17 us -> 4.59 us  [route(): return lax.all_to_all(chosen, CTX, 0, 0, tiled=True)]
  transfers between devices with their start and end apart: 13 -> 14, of which waited for: 11 -> 11; matrix products, arithmetic and copies ran while one was open for 19% -> 19% of each run, Pallas kernels for 0% -> 0%
where the time goes in v2:
time: 239 us; the launch traced here: 238 us
  waiting for transfers between devices  106 us (44%)
  matrix products  31.8 us (13%)
  local copies, waits for them, and re-layouts  28.5 us (12%)
  starting transfers between devices  25.2 us (11%)
  blocking collectives  18.2 us (8%)
  between operations  14.2 us (6%)
  other arithmetic  14.1 us (6%)
    unnamed x6, waiting for transfers between devices  34 us
    all_to_all x2, waiting for transfers between devices, route(): spread = lax.all_to_all(payload, CTX, 0, 0, tiled=True)  25.5 us
    reduce_scatter x2, waiting for transfers between devices, reduce_ctx(): part = lax.psum_scatter(part, 'z', scatter_dimension=0, tiled=True)  23.9 us
    all_to_all x1, blocking collectives, route(): return lax.all_to_all(chosen, CTX, 0, 0, tiled=True)  18.2 us
    all_to_all x2, starting transfers between devices, route(): spread = lax.all_to_all(payload, CTX, 0, 0, tiled=True)  15.2 us
    unnamed x30, local copies, waits for them, and re-layouts  14.6 us
    all_to_all x1, waiting for transfers between devices, route(): return lax.all_to_all(chosen, CTX, 0, 0, tiled=True)  8.28 us
    ppermute x3, waiting for transfers between devices, ring_rs(): got_a = lax.ppermute(acc_a, axis, cw)  6.46 us
  transfers between devices with their start and end apart: 14, of which 11 were waited for; matrix products, arithmetic and copies ran while one was open for 19% of the time, Pallas kernels for 0%

profile of v2, /device:TPU:8, one launch (start us, length us, event | category | flops | bytes accessed | tf_op | source)
XLA Modules:
  0.0 238.4 jit_solution(3142992319970020361)
XLA Ops:
  7.2 1.6 copy-done
  8.8 4.6 %convolution_convert_fusion.3 = bf16[256,768]{1,0:T(8,128)(2,1)S(1)} fusion(bf16[256,4096]{1,0:T(8,128)(2,1)S(1)} %copy-done, bf16[4096,768]{1,0:T(8,128)(2,1)} %param.8), kind=kOutput, calls=%fused_computation.18 | convolution fusion | flops 1610809344 | bytes 8781824 | tf_op jit(solution)/shard_map/dot_general | solution.py:94
  13.9 0.7 copy.61
  14.6 11.3 %all-to-all-start = ((bf16[32,2,2,1,8,128]{5,4,2,1,3,0:T(8,128)(2,1)}), bf16[32,2,2,1,8,128]{5,4,2,1,3,0:T(8,128)(2,1)S(1)}, u32[]{:S(2)}, u32[]{:S(2)}) async-start(bf16[32,2,2,1,8,128]{5,4,2,1,3,0:T(8,128)(2,1)} %copy.61), calls=%async_computation | async-start | bytes 524288 | tf_op jit(solution)/shard_map/all_to_all | solution.py:35
  26.0 12.8 %all-to-all-done = bf16[32,2,2,1,8,128]{5,4,2,1,3,0:T(8,128)(2,1)S(1)} async-done(((bf16[32,2,2,1,8,128]{5,4,2,1,3,0:T(8,128)(2,1)}), bf16[32,2,2,1,8,128]{5,4,2,1,3,0:T(8,128)(2,1)S(1)}, u32[]{:S(2)}, u32[]{:S(2)}) %all-to-all-start) | async-done | bytes 262176 | tf_op jit(solution)/shard_map/all_to_all | solution.py:35
  39.4 0.8 fusion.29
  40.2 4.6 %all-to-all-start.1 = ((bf16[32,2,2,1,8,128]{5,4,2,1,3,0:T(8,128)(2,1)}), bf16[32,2,2,1,8,128]{5,4,2,1,3,0:T(8,128)(2,1)}, u32[]{:S(2)}, u32[]{:S(2)}) async-start(bf16[32,2,2,1,8,128]{5,4,2,1,3,0:T(8,128)(2,1)} %fusion.29), calls=%async_computation.1 | async-start | bytes 524288 | tf_op jit(solution)/shard_map/all_to_all | solution.py:37
  45.0 0.8 copy.97
  45.8 1.1 shift_right_arithmetic.25
  46.8 1.6 copy.64
  48.4 8.3 %all-to-all-done.1 = bf16[32,2,2,1,8,128]{5,4,2,1,3,0:T(8,128)(2,1)} async-done(((bf16[32,2,2,1,8,128]{5,4,2,1,3,0:T(8,128)(2,1)}), bf16[32,2,2,1,8,128]{5,4,2,1,3,0:T(8,128)(2,1)}, u32[]{:S(2)}, u32[]{:S(2)}) %all-to-all-start.1) | async-done | bytes 262176 | tf_op jit(solution)/shard_map/all_to_all | solution.py:37
  56.7 1.0 copy.104
  57.7 0.7 slice_bitcast_fusion.2
  58.4 1.7 copy.65
  60.1 1.4 fusion.48
  61.4 1.0 copy-done.1
  62.7 1.3 fusion.7
  64.1 5.7 %convolution_convert_fusion.4 = bf16[2,256,128]{1,2,0:T(8,128)(2,1)} fusion(f32[2,256,512]{2,1,0:T(8,128)} %fusion.7, f32[2,256,512]{2,1,0:T(8,128)} %copy-done.1, f32[2,256]{1,0:T(2,128)S(1)} %log_add_fusion, bf16[2,1,256,128]{3,2,0,1:T(8,128)(2,1)} %get-tuple-element.23, bf16[2,1,256,128]{3,2,0,1:T(8,128)(2,1)S(1)} %bitcast.199), kind=kOutput, calls=%fused_computation.21 | convolution fusion | flops 69534720 | bytes 2492416 | tf_op jit(solution)/shard_map/hnqk,hnkd->hnqd/dot_general | solution.py:118
  69.8 3.0 %fusion.2 = bf16[4096,256]{0,1:T(8,128)(2,1)} fusion(bf16[256,256]{0,1:T(8,128)(2,1)} %bitcast.207, bf16[256,4096]{1,0:T(8,128)(2,1)S(1)} %copy-done), kind=kOutput, calls=%fused_computation.7 | convolution fusion | flops 537919488 | bytes 4325376 | tf_op jit(solution)/shard_map/dot_general | solution.py:78
  72.8 0.7 scatter_custom_fusion
  73.5 1.6 multiply_convert_fusion
  75.1 0.8 copy-done.2
  76.3 5.8 %convolution_bitcast_fusion.2 = f32[2,1,512,128]{2,3,0,1:T(8,128)} fusion(f32[2,256,512]{2,1,0:T(8,128)} %fusion.7, f32[2,256,512]{2,1,0:T(8,128)} %copy-done.1, f32[2,256]{1,0:T(2,128)S(1)} %log_add_fusion, bf16[256,2,1,128]{3,0,1,2:T(8,128)(2,1)S(1)} %copy-done.7), kind=kOutput, calls=%fused_computation.20 | convolution fusion | flops 68944896 | bytes 2754560 | tf_op jit(solution)/shard_map/hnqk,hnqd->hnkd/dot_general | solution.py:121
  82.1 1.0 slice.133
  83.2 0.7 copy.74
  83.9 3.9 %all-to-all-start.2 = ((bf16[32,2,2,1,8,128]{5,4,2,1,3,0:T(8,128)(2,1)}), bf16[32,2,2,1,8,128]{5,4,2,1,3,0:T(8,128)(2,1)S(1)}, u32[]{:S(2)}, u32[]{:S(2)}) async-start(bf16[32,2,2,1,8,128]{5,4,2,1,3,0:T(8,128)(2,1)} %copy.74), calls=%async_computation.2 | async-start | bytes 524288 | tf_op jit(solution)/shard_map/all_to_all | solution.py:35
  87.9 12.8 %all-to-all-done.2 = bf16[32,2,2,1,8,128]{5,4,2,1,3,0:T(8,128)(2,1)S(1)} async-done(((bf16[32,2,2,1,8,128]{5,4,2,1,3,0:T(8,128)(2,1)}), bf16[32,2,2,1,8,128]{5,4,2,1,3,0:T(8,128)(2,1)S(1)}, u32[]{:S(2)}, u32[]{:S(2)}) %all-to-all-start.2) | async-done | bytes 262176 | tf_op jit(solution)/shard_map/all_to_all | solution.py:35
  101.4 18.2 %all_to_all.20 = bf16[32,2,2,1,8,128]{5,4,2,1,3,0:T(8,128)(2,1)S(1)} all-to-all(bf16[32,2,2,1,8,128]{5,4,2,1,3,0:T(8,128)(2,1)S(1)} %fusion.28), channel_id=1, replica_groups=mesh['z'=8,'x'=4,'y'=4,'c'=2] {'z','x'}, dimensions={0} | all-to-all | bytes 524288 | tf_op jit(solution)/shard_map/all_to_all | solution.py:37
  119.7 0.7 fusion.33
  120.4 1.1 copy.77
  121.5 0.8 copy.78
  122.3 1.0 fusion.30
  123.3 1.0 fusion.31
  124.3 3.2 %fusion.1 = bf16[4096,512]{0,1:T(8,128)(2,1)} fusion(bf16[256,512]{0,1:T(8,128)(2,1)S(1)} %bitcast.201, bf16[256,4096]{1,0:T(8,128)(2,1)S(1)} %copy-done), kind=kOutput, calls=%fused_computation.5 | convolution fusion | flops 1075838976 | bytes 6553600 | tf_op jit(solution)/shard_map/dot_general | solution.py:78
  128.6 4.6 %convolution_convert_fusion.2 = bf16[256,4,2,512]{3,0,2,1:T(8,128)(2,1)S(1)} fusion(bf16[256,768,1,1]{0,1,3,2:T(8,128)(2,1)S(1)} %bitcast.212, bf16[4,2,512,768]{3,2,1,0:T(8,128)(2,1)} %bitcast.216), kind=kOutput, calls=%fused_computation.10 | convolution fusion | flops 1611661312 | bytes 8781824 | tf_op jit(solution)/shard_map/tk,ycwk->cytw/dot_general | solution.py:141
  133.2 1.3 copy-done.3
  134.8 2.7 %collective-permute-done = bf16[4,256,512]{2,1,0:T(8,128)(2,1)} collective-permute-done((bf16[4,256,512]{2,1,0:T(8,128)(2,1)S(1)}, bf16[4,256,512]{2,1,0:T(8,128)(2,1)}, u32[]{:S(2)}, u32[]{:S(2)}) %collective-permute-start) | collective-permute-done | bytes 1048608 | tf_op jit(solution)/shard_map/ppermute | solution.py:57
  137.5 1.8 fusion.3
  139.4 0.7 dynamic-slice_bitcast_fusion.8
  140.0 0.7 collective-permute-start.1
  140.8 1.8 copy.93
  142.7 3.2 %collective-permute-done.1 = bf16[128,512]{1,0:T(8,128)(2,1)} collective-permute-done((bf16[128,512]{1,0:T(8,128)(2,1)}, bf16[128,512]{1,0:T(8,128)(2,1)}, u32[]{:S(2)}, u32[]{:S(2)}) %collective-permute-start.1) | collective-permute-done | bytes 131104 | tf_op jit(solution)/shard_map/ppermute | solution.py:70
  145.9 1.6 fusion.27
  147.5 0.7 collective-permute-start.2
  148.2 1.3 collective-permute-start.4
  149.5 3.3 %collective-permute-done.2 = bf16[128,512]{1,0:T(8,128)(2,1)} collective-permute-done((bf16[128,512]{1,0:T(8,128)(2,1)}, bf16[128,512]{1,0:T(8,128)(2,1)}, u32[]{:S(2)}, u32[]{:S(2)}) %collective-permute-start.2) | collective-permute-done | bytes 131104 | tf_op jit(solution)/shard_map/ppermute | solution.py:70
  152.8 1.6 fusion.26
  154.4 0.7 collective-permute-start.3
  155.1 23.9 %reduce-scatter.11.cloned.1.call-done = bf16[512,512]{0,1:T(8,128)(2,1)} async-done(((bf16[4096,512]{0,1:T(8,128)(2,1)}), bf16[512,512]{0,1:T(8,128)(2,1)}) %reduce-scatter.11.cloned.1.call-update) | async-done | bytes 524304 | tf_op jit(solution)/shard_map/reduce_scatter | solution.py:84
  179.1 2.0 copy.95
  181.2 1.0 fusion.25
  182.8 4.6 %collective-permute-done.5 = bf16[128,512]{1,0:T(8,128)(2,1)S(1)} collective-permute-done((bf16[128,512]{1,0:T(8,128)(2,1)S(1)}, bf16[128,512]{1,0:T(8,128)(2,1)S(1)}, u32[]{:S(2)}, u32[]{:S(2)}) %collective-permute-start.5) | collective-permute-done | bytes 131104 | tf_op jit(solution)/shard_map/ppermute | solution.py:71
  187.5 0.7 fusion.23
  188.2 0.8 collective-permute-start.6
  189.0 2.0 convolution_convert_fusion.5
  191.0 1.7 copy.83
  192.6 0.8 collective-permute-done.6
  193.4 0.9 fusion.22
  194.4 0.7 pad_maximum_fusion
  195.1 8.5 %reduce-scatter.13.cloned.1.call-done = bf16[128,256]{1,0:T(8,128)(2,1)} async-done(((bf16[512,256]{1,0:T(8,128)(2,1)}), bf16[128,256]{1,0:T(8,128)(2,1)}) %reduce-scatter.13.cloned.1.call-update) | async-done | bytes 65552
  203.6 0.9 copy.94
  204.6 25.4 %reduce-scatter.15.cloned.1.call-done = bf16[128,512]{1,0:T(8,128)(2,1)} async-done(((bf16[512,512]{1,0:T(8,128)(2,1)}), bf16[128,512]{1,0:T(8,128)(2,1)}) %reduce-scatter.15.cloned.1.call-update) | async-done | bytes 131088
  230.0 1.0 copy.96
  231.0 0.8 copy.84
  (64 shorter events, 4.9 us)
Async XLA Ops:
  7.2 1.6 copy-start
  13.3 12.6 %copy-start.10 = (s32[1,32]{1,0:T(1,128)S(1)}, s32[1,32]{1,0:T(1,128)}, u32[]{:S(2)}) copy-start(s32[1,32]{1,0:T(1,128)} %param.9) | copy-start | bytes 388
  13.5 31.4 %copy-start.8 = (bf16[256,256]{1,0:T(8,128)(2,1)S(1)}, bf16[256,256]{1,0:T(8,128)(2,1)}, u32[]{:S(2)}) copy-start(bf16[256,256]{1,0:T(8,128)(2,1)} %param.11) | copy-start | bytes 393220
  13.6 32.2 %copy-start.9 = (s32[256,64]{0,1:T(8,128)S(1)}, s32[256,64]{0,1:T(8,128)}, u32[]{:S(2)}) copy-start(s32[256,64]{0,1:T(8,128)} %param.10) | copy-start | bytes 196612
  14.6 24.1 %all-to-all-start = ((bf16[32,2,2,1,8,128]{5,4,2,1,3,0:T(8,128)(2,1)}), bf16[32,2,2,1,8,128]{5,4,2,1,3,0:T(8,128)(2,1)S(1)}, u32[]{:S(2)}, u32[]{:S(2)}) async-start(bf16[32,2,2,1,8,128]{5,4,2,1,3,0:T(8,128)(2,1)} %copy.61), calls=%async_computation | async-start | bytes 524288 | tf_op jit(solution)/shard_map/all_to_all | solution.py:35
  40.2 16.5 %all-to-all-start.1 = ((bf16[32,2,2,1,8,128]{5,4,2,1,3,0:T(8,128)(2,1)}), bf16[32,2,2,1,8,128]{5,4,2,1,3,0:T(8,128)(2,1)}, u32[]{:S(2)}, u32[]{:S(2)}) async-start(bf16[32,2,2,1,8,128]{5,4,2,1,3,0:T(8,128)(2,1)} %fusion.29), calls=%async_computation.1 | async-start | bytes 524288 | tf_op jit(solution)/shard_map/all_to_all | solution.py:37
  44.8 96.0 %reduce-scatter.9.cloned.1.call-start = ((), (), s32[]{:S(2)}) async-start(), calls=%async_computation.8 | async-start | bytes 2359296 | tf_op jit(solution)/shard_map/reduce_scatter | solution.py:84
  60.1 2.7 %copy-start.4 = (bf16[2,1,256,128]{2,3,0,1:T(8,128)(2,1)S(1)}, bf16[2,1,256,128]{2,3,0,1:T(8,128)(2,1)}, u32[]{:S(2)}) copy-start(bf16[2,1,256,128]{2,3,0,1:T(8,128)(2,1)} %copy.65) | copy-start | bytes 393220
  61.4 1.0 copy-start.1
  73.5 2.8 %copy-start.7 = (bf16[256,2,1,128]{3,0,1,2:T(8,128)(2,1)S(1)}, bf16[256,2,1,128]{3,0,1,2:T(8,128)(2,1)}, u32[]{:S(2)}) copy-start(bf16[256,2,1,128]{3,0,1,2:T(8,128)(2,1)} %copy.97) | copy-start | bytes 393220
  75.1 0.8 copy-start.2
  83.9 16.7 %all-to-all-start.2 = ((bf16[32,2,2,1,8,128]{5,4,2,1,3,0:T(8,128)(2,1)}), bf16[32,2,2,1,8,128]{5,4,2,1,3,0:T(8,128)(2,1)S(1)}, u32[]{:S(2)}, u32[]{:S(2)}) async-start(bf16[32,2,2,1,8,128]{5,4,2,1,3,0:T(8,128)(2,1)} %copy.74), calls=%async_computation.2 | async-start | bytes 524288 | tf_op jit(solution)/shard_map/all_to_all | solution.py:35
  87.8 91.3 %reduce-scatter.11.cloned.1.call-start = ((), (), s32[]{:S(2)}) async-start(), calls=%async_computation.9 | async-start | bytes 4718592 | tf_op jit(solution)/shard_map/reduce_scatter | solution.py:84
  127.6 0.9 copy-start.6
  127.6 76.0 %reduce-scatter.13.cloned.1.call-start = ((), (), s32[]{:S(2)}) async-start(), calls=%async_computation.10 | async-start | bytes 327680
  133.2 1.4 copy-start.3
  134.6 2.9 %collective-permute-start = (bf16[4,256,512]{2,1,0:T(8,128)(2,1)S(1)}, bf16[4,256,512]{2,1,0:T(8,128)(2,1)}, u32[]{:S(2)}, u32[]{:S(2)}) collective-permute-start(bf16[4,256,512]{2,1,0:T(8,128)(2,1)S(1)} %dynamic-slice_bitcast_fusion), channel_id=1, source_target_pairs={{0,1},{1,0},{2,3},{3,2},{4,5},{5,4},{6,7},{7,6},{8,9},{9,8},{10,11... | collective-permute-start | bytes 3145736 | tf_op jit(solution)/shard_map/ppermute | solution.py:57
  140.0 5.9 %collective-permute-start.1 = (bf16[128,512]{1,0:T(8,128)(2,1)}, bf16[128,512]{1,0:T(8,128)(2,1)}, u32[]{:S(2)}, u32[]{:S(2)}) collective-permute-start(bf16[128,512]{1,0:T(8,128)(2,1)} %get-tuple-element.15), channel_id=1, source_target_pairs={{0,2},{2,4},{4,6},{6,0},{1,3},{3,5},{5,7},{7,1},{8,10},{10,12},{12... | collective-permute-start | bytes 393224 | tf_op jit(solution)/shard_map/ppermute | solution.py:70
  140.8 48.2 %copy-start.5 = (bf16[2,1,256,128]{2,3,0,1:T(8,128)(2,1)S(1)}, bf16[2,1,256,128]{2,3,0,1:T(8,128)(2,1)}, u32[]{:S(2)}) copy-start(bf16[2,1,256,128]{2,3,0,1:T(8,128)(2,1)} %copy.65) | copy-start | bytes 393220
  142.6 87.3 %reduce-scatter.15.cloned.1.call-start = ((), (), s32[]{:S(2)}) async-start(), calls=%async_computation.11 | async-start | bytes 655360
  147.5 5.3 %collective-permute-start.2 = (bf16[128,512]{1,0:T(8,128)(2,1)}, bf16[128,512]{1,0:T(8,128)(2,1)}, u32[]{:S(2)}, u32[]{:S(2)}) collective-permute-start(bf16[128,512]{1,0:T(8,128)(2,1)} %fusion.27), channel_id=1, source_target_pairs={{0,2},{2,4},{4,6},{6,0},{1,3},{3,5},{5,7},{7,1},{8,10},{10,12},{12... | collective-permute-start | bytes 393224 | tf_op jit(solution)/shard_map/ppermute | solution.py:70
  148.2 32.9 %collective-permute-start.4 = (bf16[128,512]{1,0:T(8,128)(2,1)S(1)}, bf16[128,512]{1,0:T(8,128)(2,1)}, u32[]{:S(2)}, u32[]{:S(2)}) collective-permute-start(bf16[128,512]{1,0:T(8,128)(2,1)S(1)} %get-tuple-element.16), channel_id=1, source_target_pairs={{0,6},{2,0},{4,2},{6,4},{1,7},{3,1},{5,3},{7,5},{8,14},{10,8},{12,... | collective-permute-start | bytes 393224 | tf_op jit(solution)/shard_map/ppermute | solution.py:71
  154.4 26.8 %collective-permute-start.3 = (bf16[128,512]{1,0:T(8,128)(2,1)}, bf16[128,512]{1,0:T(8,128)(2,1)}, u32[]{:S(2)}, u32[]{:S(2)}) collective-permute-start(bf16[128,512]{1,0:T(8,128)(2,1)} %fusion.26), channel_id=1, source_target_pairs={{0,2},{2,4},{4,6},{6,0},{1,3},{3,5},{5,7},{7,1},{8,10},{10,12},{12... | collective-permute-start | bytes 393224 | tf_op jit(solution)/shard_map/ppermute | solution.py:70
  182.2 5.3 %collective-permute-start.5 = (bf16[128,512]{1,0:T(8,128)(2,1)S(1)}, bf16[128,512]{1,0:T(8,128)(2,1)S(1)}, u32[]{:S(2)}, u32[]{:S(2)}) collective-permute-start(bf16[128,512]{1,0:T(8,128)(2,1)S(1)} %get-tuple-element.14), channel_id=1, source_target_pairs={{0,6},{2,0},{4,2},{6,4},{1,7},{3,1},{5,3},{7,5},{8,14},{10,8},{12,... | collective-permute-start | bytes 393224 | tf_op jit(solution)/shard_map/ppermute | solution.py:71
  188.2 5.3 %collective-permute-start.6 = (bf16[128,512]{1,0:T(8,128)(2,1)}, bf16[128,512]{1,0:T(8,128)(2,1)}, u32[]{:S(2)}, u32[]{:S(2)}) collective-permute-start(bf16[128,512]{1,0:T(8,128)(2,1)} %fusion.23), channel_id=1, source_target_pairs={{0,6},{2,0},{4,2},{6,4},{1,7},{3,1},{5,3},{7,5},{8,14},{10,8},{12,... | collective-permute-start | bytes 393224 | tf_op jit(solution)/shard_map/ppermute | solution.py:71
Sparse Core Ops, SparseCore 0:
  72.9 44.0 reduce-scatter.8
  127.7 51.2 reduce-scatter.10
  181.6 21.9 reduce-scatter.12
  206.0 23.9 reduce-scatter.14

commit v3 on v2

--- a/solution.py
+++ b/solution.py
@@ -82,7 +82,10 @@
 
 def reduce_ctx(part):
     part = lax.psum_scatter(part, "z", scatter_dimension=0, tiled=True)
-    return lax.psum_scatter(part, "x", scatter_dimension=0, tiled=True)
+    n_x = lax.psum(1, "x")
+    pieces = part.reshape((n_x, part.shape[0] // n_x) + part.shape[1:])
+    gathered = lax.all_to_all(pieces, "x", 0, 0, tiled=True)
+    return jnp.sum(gathered.astype(jnp.float32), 0).astype(part.dtype)
 
 
 def per_device(activations, w_qkv, matching, dropout_bits, out_grad):
@@ -126,15 +129,7 @@
     grad_value = (grad_values[:, :, :BLK] + returned[1].astype(f32)).astype(jnp.bfloat16)
     stacked = jnp.stack([grad_query, grad_key, grad_value], 3)
     grad_qkv = stacked.transpose(1, 2, 0, 3, 4).reshape(local_tokens, head_count * 3 * HD)
-    query_cols = grad_query.transpose(1, 2, 0, 3).reshape(local_tokens, head_count * HD)
-    kv_cols = jnp.stack([grad_key, grad_value], 3).transpose(1, 2, 0, 3, 4)
-    kv_cols = kv_cols.reshape(local_tokens, head_count * 2 * HD)
-    weight_q = reduce_ctx(weight_term(activations, query_cols))
-    weight_kv = reduce_ctx(weight_term(activations, kv_cols))
-    rows = weight_q.shape[0]
-    weight_grad = jnp.concatenate(
-        [weight_q.reshape(rows, head_count, 1, HD), weight_kv.reshape(rows, head_count, 2, HD)], 2
-    ).reshape(rows, head_count * 3 * HD)
+    weight_grad = reduce_ctx(weight_term(activations, grad_qkv))
     n_y = lax.psum(1, "y")
     width = activations.shape[1] // (2 * n_y)
     w_split = w_qkv.reshape(n_y, 2, width, w_qkv.shape[1])

time: 239 us -> 219 us (0.916)
  blocking collectives: 18.2 us -> 0 us
  starting transfers between devices: 25.2 us -> 40.7 us
  waiting for transfers between devices: 106 us -> 93 us
  local copies, waits for them, and re-layouts: 28.5 us -> 24.7 us
    unnamed x6 -> x1, waiting for transfers between devices: 34 us -> 0.02 us
    all_to_all x1 -> x0, blocking collectives: 18.2 us -> none  [route(): return lax.all_to_all(chosen, CTX, 0, 0, tiled=True)]
    unnamed x30 -> x26, local copies, waits for them, and re-layouts: 14.6 us -> 6.6 us
    all_to_all x0 -> x1, waiting for transfers between devices: none -> 7.19 us  [reduce_ctx(): gathered = lax.all_to_all(pieces, 'x', 0, 0, tiled=True)]
    all_to_all x1 -> x2, waiting for transfers between devices: 8.28 us -> 14.4 us  [route(): return lax.all_to_all(chosen, CTX, 0, 0, tiled=True)]
    reduce_scatter x2 -> x1, waiting for transfers between devices: 23.9 us -> 30 us  [reduce_ctx(): part = lax.psum_scatter(part, 'z', scatter_dimension=0, tiled=True)]
    ppermute x3, waiting for transfers between devices: 6.46 us -> 11.7 us  [ring_rs(): got_a = lax.ppermute(acc_a, axis, cw)]
    all_to_all x1 -> x2, starting transfers between devices: 4.59 us -> 9.18 us  [route(): return lax.all_to_all(chosen, CTX, 0, 0, tiled=True)]
  transfers between devices with their start and end apart: 14 -> 13, of which waited for: 11 -> 11; matrix products, arithmetic and copies ran while one was open for 19% -> 13% of each run, Pallas kernels for 0% -> 0%
where the time goes in v3:
time: 219 us; the launch traced here: 218 us
  waiting for transfers between devices  93 us (42%)
  starting transfers between devices  40.7 us (19%)
  matrix products  29.9 us (14%)
  local copies, waits for them, and re-layouts  24.7 us (11%)
  other arithmetic  15.1 us (7%)
  between operations  14.4 us (7%)
    reduce_scatter x1, waiting for transfers between devices, reduce_ctx(): part = lax.psum_scatter(part, 'z', scatter_dimension=0, tiled=True)  30 us
    all_to_all x2, waiting for transfers between devices, route(): spread = lax.all_to_all(payload, CTX, 0, 0, tiled=True)  24.4 us
    all_to_all x2, starting transfers between devices, route(): spread = lax.all_to_all(payload, CTX, 0, 0, tiled=True)  15.9 us
    all_to_all x2, waiting for transfers between devices, route(): return lax.all_to_all(chosen, CTX, 0, 0, tiled=True)  14.4 us
    ppermute x3, waiting for transfers between devices, ring_rs(): got_a = lax.ppermute(acc_a, axis, cw)  11.7 us
    all_to_all x2, starting transfers between devices, route(): return lax.all_to_all(chosen, CTX, 0, 0, tiled=True)  9.18 us
    all_to_all x1, waiting for transfers between devices, reduce_ctx(): gathered = lax.all_to_all(pieces, 'x', 0, 0, tiled=True)  7.19 us
    unnamed x26, local copies, waits for them, and re-layouts  6.6 us
  transfers between devices with their start and end apart: 13, of which 11 were waited for; matrix products, arithmetic and copies ran while one was open for 13% of the time, Pallas kernels for 0%

profile of v3, /device:TPU:8, one launch (start us, length us, event | category | flops | bytes accessed | tf_op | source)
XLA Modules:
  0.0 217.9 jit_solution(8440347698304002527)
XLA Ops:
  7.2 1.6 copy-done
  8.8 4.6 %convolution_convert_fusion.2 = bf16[256,768]{1,0:T(8,128)(2,1)S(1)} fusion(bf16[256,4096]{1,0:T(8,128)(2,1)S(1)} %copy-done, bf16[4096,768]{1,0:T(8,128)(2,1)} %param.8), kind=kOutput, calls=%fused_computation.16 | convolution fusion | flops 1610809344 | bytes 8781824 | tf_op jit(solution)/shard_map/dot_general | solution.py:97
  13.9 0.7 copy.60
  14.6 11.3 %all-to-all-start = ((bf16[32,2,2,1,8,128]{5,4,2,1,3,0:T(8,128)(2,1)}), bf16[32,2,2,1,8,128]{5,4,2,1,3,0:T(8,128)(2,1)S(1)}, u32[]{:S(2)}, u32[]{:S(2)}) async-start(bf16[32,2,2,1,8,128]{5,4,2,1,3,0:T(8,128)(2,1)} %copy.60), calls=%async_computation | async-start | bytes 524288 | tf_op jit(solution)/shard_map/all_to_all | solution.py:35
  26.0 12.8 %all-to-all-done = bf16[32,2,2,1,8,128]{5,4,2,1,3,0:T(8,128)(2,1)S(1)} async-done(((bf16[32,2,2,1,8,128]{5,4,2,1,3,0:T(8,128)(2,1)}), bf16[32,2,2,1,8,128]{5,4,2,1,3,0:T(8,128)(2,1)S(1)}, u32[]{:S(2)}, u32[]{:S(2)}) %all-to-all-start) | async-done | bytes 262176 | tf_op jit(solution)/shard_map/all_to_all | solution.py:35
  39.3 0.8 fusion.29
  40.2 4.6 %all-to-all-start.1 = ((bf16[32,2,2,1,8,128]{5,4,2,1,3,0:T(8,128)(2,1)}), bf16[32,2,2,1,8,128]{5,4,2,1,3,0:T(8,128)(2,1)}, u32[]{:S(2)}, u32[]{:S(2)}) async-start(bf16[32,2,2,1,8,128]{5,4,2,1,3,0:T(8,128)(2,1)} %fusion.29), calls=%async_computation.1 | async-start | bytes 524288 | tf_op jit(solution)/shard_map/all_to_all | solution.py:37
  44.9 0.8 copy.97
  45.6 0.9 shift_right_arithmetic.25
  46.6 1.3 copy.63
  47.9 0.7 scatter_custom_fusion
  48.6 8.1 %all-to-all-done.1 = bf16[32,2,2,1,8,128]{5,4,2,1,3,0:T(8,128)(2,1)} async-done(((bf16[32,2,2,1,8,128]{5,4,2,1,3,0:T(8,128)(2,1)}), bf16[32,2,2,1,8,128]{5,4,2,1,3,0:T(8,128)(2,1)}, u32[]{:S(2)}, u32[]{:S(2)}) %all-to-all-start.1) | async-done | bytes 262176 | tf_op jit(solution)/shard_map/all_to_all | solution.py:37
  56.7 1.0 copy.114
  57.7 0.7 slice_bitcast_fusion.2
  58.3 0.8 copy.64
  59.1 1.4 fusion.52
  61.5 1.3 fusion.6
  62.7 1.1 convolution_bitcast_fusion.1
  63.8 5.3 %convolution_bitcast_fusion.2 = f32[2,1,512,128]{2,3,0,1:T(8,128)} fusion(f32[2,256,512]{2,1,0:T(8,128)} %fusion.6, f32[2,256,512]{2,1,0:T(8,128)S(1)} %get-tuple-element.25, f32[2,256]{1,0:T(2,128)S(1)} %log_add_fusion, bf16[256,2,1,128]{3,0,1,2:T(8,128)(2,1)} %copy.97), kind=kOutput, calls=%fused_computation.18 | convolution fusion | flops 68944896 | bytes 2754560 | tf_op jit(solution)/shard_map/hnqk,hnqd->hnkd/dot_general | solution.py:124
  69.1 1.0 slice.133
  70.1 0.8 copy.71
  70.8 1.0 slice.132
  71.8 0.8 copy.74
  72.6 1.0 maximum_bitcast_fusion.4
  73.6 0.7 copy.75
  74.3 4.6 %all-to-all-start.2 = ((bf16[32,2,2,1,8,128]{5,4,2,1,3,0:T(8,128)(2,1)}), bf16[32,2,2,1,8,128]{5,4,2,1,3,0:T(8,128)(2,1)}, u32[]{:S(2)}, u32[]{:S(2)}) async-start(bf16[32,2,2,1,8,128]{5,4,2,1,3,0:T(8,128)(2,1)} %copy.75), calls=%async_computation.2 | async-start | bytes 524288 | tf_op jit(solution)/shard_map/all_to_all | solution.py:35
  79.0 11.7 %all-to-all-done.2 = bf16[32,2,2,1,8,128]{5,4,2,1,3,0:T(8,128)(2,1)} async-done(((bf16[32,2,2,1,8,128]{5,4,2,1,3,0:T(8,128)(2,1)}), bf16[32,2,2,1,8,128]{5,4,2,1,3,0:T(8,128)(2,1)}, u32[]{:S(2)}, u32[]{:S(2)}) %all-to-all-start.2) | async-done | bytes 262176 | tf_op jit(solution)/shard_map/all_to_all | solution.py:35
  90.6 2.2 %gather_fusion.1 = bf16[32,2,2,8,128]{4,3,2,1,0:T(8,128)(2,1)} fusion(bf16[32,2,2,8,128]{4,3,2,1,0:T(8,128)(2,1)} %bitcast.43, s32[1024]{0:T(1024)S(1)} %pad_clamp_fusion), kind=kCustom, calls=%fused_computation.1.clone | custom fusion | bytes 524416 | tf_op jit(solution)/shard_map/jit(_take)/gather | solution.py:36
  92.9 1.8 fusion.28
  94.6 4.6 %all-to-all-start.3 = ((bf16[32,2,2,1,8,128]{5,4,2,1,3,0:T(8,128)(2,1)}), bf16[32,2,2,1,8,128]{5,4,2,1,3,0:T(8,128)(2,1)}, u32[]{:S(2)}, u32[]{:S(2)}) async-start(bf16[32,2,2,1,8,128]{5,4,2,1,3,0:T(8,128)(2,1)} %fusion.28), calls=%async_computation.3 | async-start | bytes 524288 | tf_op jit(solution)/shard_map/all_to_all | solution.py:37
  99.5 5.2 %fusion.8 = bf16[2,1,256,1,128]{2,4,0,3,1:T(8,128)(2,1)} fusion(f32[2,256,512]{2,1,0:T(8,128)} %fusion.6, f32[2,256,512]{2,1,0:T(8,128)S(1)} %get-tuple-element.25, f32[2,256]{1,0:T(2,128)S(1)} %log_add_fusion, bf16[2,1,256,128]{3,2,0,1:T(8,128)(2,1)S(1)} %copy-done.7, bf16[2,1,256,128]{3,2,0,1:T(8,128)(2,1)S(1)} %bitcast.188), kind=kOutput, calls=%fused_computation.21 | convolution fusion | flops 69534720 | bytes 2492416 | tf_op jit(solution)/shard_map/hnqk,hnkd->hnqd/dot_general | solution.py:121
  104.6 6.3 %all-to-all-done.3 = bf16[32,2,2,1,8,128]{5,4,2,1,3,0:T(8,128)(2,1)} async-done(((bf16[32,2,2,1,8,128]{5,4,2,1,3,0:T(8,128)(2,1)}), bf16[32,2,2,1,8,128]{5,4,2,1,3,0:T(8,128)(2,1)}, u32[]{:S(2)}, u32[]{:S(2)}) %all-to-all-start.3) | async-done | bytes 262176 | tf_op jit(solution)/shard_map/all_to_all | solution.py:37
  110.9 1.0 copy.113
  111.9 0.7 fusion.33
  112.8 1.1 copy.79
  113.9 1.0 fusion.30
  115.0 4.5 %fusion.1 = bf16[4096,768]{0,1:T(8,128)(2,1)} fusion(bf16[256,768]{0,1:T(8,128)(2,1)S(1)} %bitcast.183, bf16[256,4096]{1,0:T(8,128)(2,1)S(1)} %copy-done), kind=kOutput, calls=%fused_computation.5 | convolution fusion | flops 1613758464 | bytes 8781824 | tf_op jit(solution)/shard_map/dot_general | solution.py:78
  119.5 4.6 %convolution_convert_fusion.1 = bf16[256,4,2,512]{3,0,2,1:T(8,128)(2,1)S(1)} fusion(bf16[256,768,1,1]{0,1,3,2:T(8,128)(2,1)S(1)} %bitcast.184, bf16[4,2,512,768]{3,2,1,0:T(8,128)(2,1)} %bitcast.197), kind=kOutput, calls=%fused_computation.8 | convolution fusion | flops 1611661312 | bytes 8781824 | tf_op jit(solution)/shard_map/tk,ycwk->cytw/dot_general | solution.py:136
  124.2 1.4 copy-done.3
  125.7 2.7 %collective-permute-done = bf16[4,256,512]{2,1,0:T(8,128)(2,1)} collective-permute-done((bf16[4,256,512]{2,1,0:T(8,128)(2,1)S(1)}, bf16[4,256,512]{2,1,0:T(8,128)(2,1)}, u32[]{:S(2)}, u32[]{:S(2)}) %collective-permute-start) | collective-permute-done | bytes 1048608 | tf_op jit(solution)/shard_map/ppermute | solution.py:57
  128.5 1.8 fusion.2
  130.3 1.7 collective-permute-start.1
  132.0 4.1 %collective-permute-done.1 = bf16[128,512]{1,0:T(8,128)(2,1)} collective-permute-done((bf16[128,512]{1,0:T(8,128)(2,1)S(1)}, bf16[128,512]{1,0:T(8,128)(2,1)}, u32[]{:S(2)}, u32[]{:S(2)}) %collective-permute-start.1) | collective-permute-done | bytes 131104 | tf_op jit(solution)/shard_map/ppermute | solution.py:70
  136.0 0.9 fusion.27
  137.0 1.7 collective-permute-start.2
  139.1 3.0 %collective-permute-done.2 = bf16[128,512]{1,0:T(8,128)(2,1)} collective-permute-done((bf16[128,512]{1,0:T(8,128)(2,1)S(1)}, bf16[128,512]{1,0:T(8,128)(2,1)}, u32[]{:S(2)}, u32[]{:S(2)}) %collective-permute-start.2) | collective-permute-done | bytes 131104 | tf_op jit(solution)/shard_map/ppermute | solution.py:70
  142.1 1.6 fusion.26
  143.7 1.6 collective-permute-start.3
  145.3 4.6 %collective-permute-done.3 = bf16[128,512]{1,0:T(8,128)(2,1)} collective-permute-done((bf16[128,512]{1,0:T(8,128)(2,1)}, bf16[128,512]{1,0:T(8,128)(2,1)}, u32[]{:S(2)}, u32[]{:S(2)}) %collective-permute-start.3) | collective-permute-done | bytes 131104 | tf_op jit(solution)/shard_map/ppermute | solution.py:70
  149.9 1.0 fusion.25
  151.0 3.3 %collective-permute-start.5 = (bf16[128,512]{1,0:T(8,128)(2,1)S(1)}, bf16[128,512]{1,0:T(8,128)(2,1)S(1)}, u32[]{:S(2)}, u32[]{:S(2)}) collective-permute-start(bf16[128,512]{1,0:T(8,128)(2,1)S(1)} %get-tuple-element.14), channel_id=1, source_target_pairs={{0,6},{2,0},{4,2},{6,4},{1,7},{3,1},{5,3},{7,5},{8,14},{10,8},{12,... | collective-permute-start | bytes 393224 | tf_op jit(solution)/shard_map/ppermute | solution.py:71
  154.3 2.5 %collective-permute-done.5 = bf16[128,512]{1,0:T(8,128)(2,1)S(1)} collective-permute-done((bf16[128,512]{1,0:T(8,128)(2,1)S(1)}, bf16[128,512]{1,0:T(8,128)(2,1)S(1)}, u32[]{:S(2)}, u32[]{:S(2)}) %collective-permute-start.5) | collective-permute-done | bytes 131104 | tf_op jit(solution)/shard_map/ppermute | solution.py:71
  156.8 0.7 fusion.23
  157.5 2.4 %collective-permute-start.6 = (bf16[128,512]{1,0:T(8,128)(2,1)}, bf16[128,512]{1,0:T(8,128)(2,1)}, u32[]{:S(2)}, u32[]{:S(2)}) collective-permute-start(bf16[128,512]{1,0:T(8,128)(2,1)} %fusion.23), channel_id=1, source_target_pairs={{0,6},{2,0},{4,2},{6,4},{1,7},{3,1},{5,3},{7,5},{8,14},{10,8},{12,... | collective-permute-start | bytes 393224 | tf_op jit(solution)/shard_map/ppermute | solution.py:71
  159.9 30.0 %reduce-scatter.2.cloned.1.call-done = bf16[512,768]{0,1:T(8,128)(2,1)} async-done(((bf16[4096,768]{0,1:T(8,128)(2,1)}), bf16[512,768]{0,1:T(8,128)(2,1)}) %reduce-scatter.2.cloned.1.call-update) | async-done | bytes 786448 | tf_op jit(solution)/shard_map/reduce_scatter | solution.py:84
  190.0 2.2 copy_bitcast_fusion
  192.1 4.2 %all-to-all-start.4 = ((bf16[4,128,768]{1,2,0:T(8,128)(2,1)}), bf16[4,128,768]{1,2,0:T(8,128)(2,1)}, u32[]{:S(2)}, u32[]{:S(2)}) async-start(bf16[4,128,768]{1,2,0:T(8,128)(2,1)} %copy_bitcast_fusion), calls=%async_computation.5 | async-start | bytes 1572864 | tf_op jit(solution)/shard_map/all_to_all | solution.py:87
  196.4 2.0 convolution_convert_fusion.4
  198.4 1.7 copy.85
  200.1 0.9 fusion.22
  201.0 0.7 pad_maximum_fusion
  201.7 7.2 %all-to-all-done.4 = bf16[4,128,768]{1,2,0:T(8,128)(2,1)} async-done(((bf16[4,128,768]{1,2,0:T(8,128)(2,1)}), bf16[4,128,768]{1,2,0:T(8,128)(2,1)}, u32[]{:S(2)}, u32[]{:S(2)}) %all-to-all-start.4) | async-done | bytes 786464 | tf_op jit(solution)/shard_map/all_to_all | solution.py:87
  208.9 1.3 reduce_sum.32
  210.2 0.8 copy.86
  (51 shorter events, 3.2 us)
Async XLA Ops:
  7.2 1.6 copy-start
  13.3 12.6 %copy-start.10 = (s32[1,32]{1,0:T(1,128)S(1)}, s32[1,32]{1,0:T(1,128)}, u32[]{:S(2)}) copy-start(s32[1,32]{1,0:T(1,128)} %param.9) | copy-start | bytes 388
  13.5 31.3 %copy-start.8 = (bf16[256,256]{1,0:T(8,128)(2,1)S(1)}, bf16[256,256]{1,0:T(8,128)(2,1)}, u32[]{:S(2)}) copy-start(bf16[256,256]{1,0:T(8,128)(2,1)} %param.11) | copy-start | bytes 393220
  14.6 24.1 %all-to-all-start = ((bf16[32,2,2,1,8,128]{5,4,2,1,3,0:T(8,128)(2,1)}), bf16[32,2,2,1,8,128]{5,4,2,1,3,0:T(8,128)(2,1)S(1)}, u32[]{:S(2)}, u32[]{:S(2)}) async-start(bf16[32,2,2,1,8,128]{5,4,2,1,3,0:T(8,128)(2,1)} %copy.60), calls=%async_computation | async-start | bytes 524288 | tf_op jit(solution)/shard_map/all_to_all | solution.py:35
  40.2 16.5 %all-to-all-start.1 = ((bf16[32,2,2,1,8,128]{5,4,2,1,3,0:T(8,128)(2,1)}), bf16[32,2,2,1,8,128]{5,4,2,1,3,0:T(8,128)(2,1)}, u32[]{:S(2)}, u32[]{:S(2)}) async-start(bf16[32,2,2,1,8,128]{5,4,2,1,3,0:T(8,128)(2,1)} %fusion.29), calls=%async_computation.1 | async-start | bytes 524288 | tf_op jit(solution)/shard_map/all_to_all | solution.py:37
  59.1 1.8 copy-start.1
  60.6 0.9 copy-start.5
  61.5 1.3 copy-start.2
  72.6 26.9 %copy-start.7 = (bf16[2,1,256,128]{3,2,0,1:T(8,128)(2,1)S(1)}, bf16[2,1,256,128]{3,2,0,1:T(8,128)(2,1)}, u32[]{:S(2)}) copy-start(bf16[2,1,256,128]{3,2,0,1:T(8,128)(2,1)} %get-tuple-element.23) | copy-start | bytes 393220
  74.3 16.3 %all-to-all-start.2 = ((bf16[32,2,2,1,8,128]{5,4,2,1,3,0:T(8,128)(2,1)}), bf16[32,2,2,1,8,128]{5,4,2,1,3,0:T(8,128)(2,1)}, u32[]{:S(2)}, u32[]{:S(2)}) async-start(bf16[32,2,2,1,8,128]{5,4,2,1,3,0:T(8,128)(2,1)} %copy.75), calls=%async_computation.2 | async-start | bytes 524288 | tf_op jit(solution)/shard_map/all_to_all | solution.py:35
  94.6 16.3 %all-to-all-start.3 = ((bf16[32,2,2,1,8,128]{5,4,2,1,3,0:T(8,128)(2,1)}), bf16[32,2,2,1,8,128]{5,4,2,1,3,0:T(8,128)(2,1)}, u32[]{:S(2)}, u32[]{:S(2)}) async-start(bf16[32,2,2,1,8,128]{5,4,2,1,3,0:T(8,128)(2,1)} %fusion.28), calls=%async_computation.3 | async-start | bytes 524288 | tf_op jit(solution)/shard_map/all_to_all | solution.py:37
  99.2 90.8 %reduce-scatter.2.cloned.1.call-start = ((), (), s32[]{:S(2)}) async-start(), calls=%async_computation.6 | async-start | bytes 7077888 | tf_op jit(solution)/shard_map/reduce_scatter | solution.py:84
  104.6 9.3 %copy-start.4 = (f32[2,1,512,128]{2,3,0,1:T(8,128)S(1)}, f32[2,1,512,128]{2,3,0,1:T(8,128)}, u32[]{:S(2)}) copy-start(f32[2,1,512,128]{2,3,0,1:T(8,128)} %convolution_bitcast_fusion.1) | copy-start | bytes 1572868
  104.6 10.3 %copy-start.9 = (bf16[2,1,256,1,128]{2,4,0,3,1:T(8,128)(2,1)S(1)}, bf16[2,1,256,1,128]{2,4,0,3,1:T(8,128)(2,1)}, u32[]{:S(2)}) copy-start(bf16[2,1,256,1,128]{2,4,0,3,1:T(8,128)(2,1)} %fusion.8) | copy-start | bytes 393220
  124.1 1.4 copy-start.3
  125.6 2.9 %collective-permute-start = (bf16[4,256,512]{2,1,0:T(8,128)(2,1)S(1)}, bf16[4,256,512]{2,1,0:T(8,128)(2,1)}, u32[]{:S(2)}, u32[]{:S(2)}) collective-permute-start(bf16[4,256,512]{2,1,0:T(8,128)(2,1)S(1)} %dynamic-slice_bitcast_fusion), channel_id=1, source_target_pairs={{0,1},{1,0},{2,3},{3,2},{4,5},{5,4},{6,7},{7,6},{8,9},{9,8},{10,11... | collective-permute-start | bytes 3145736 | tf_op jit(solution)/shard_map/ppermute | solution.py:57
  130.3 5.7 %collective-permute-start.1 = (bf16[128,512]{1,0:T(8,128)(2,1)S(1)}, bf16[128,512]{1,0:T(8,128)(2,1)}, u32[]{:S(2)}, u32[]{:S(2)}) collective-permute-start(bf16[128,512]{1,0:T(8,128)(2,1)S(1)} %get-tuple-element.15), channel_id=1, source_target_pairs={{0,2},{2,4},{4,6},{6,0},{1,3},{3,5},{5,7},{7,1},{8,10},{10,12},{12... | collective-permute-start | bytes 393224 | tf_op jit(solution)/shard_map/ppermute | solution.py:70
  137.0 5.2 %collective-permute-start.2 = (bf16[128,512]{1,0:T(8,128)(2,1)S(1)}, bf16[128,512]{1,0:T(8,128)(2,1)}, u32[]{:S(2)}, u32[]{:S(2)}) collective-permute-start(bf16[128,512]{1,0:T(8,128)(2,1)S(1)} %fusion.27), channel_id=1, source_target_pairs={{0,2},{2,4},{4,6},{6,0},{1,3},{3,5},{5,7},{7,1},{8,10},{10,12},{12... | collective-permute-start | bytes 393224 | tf_op jit(solution)/shard_map/ppermute | solution.py:70
  138.7 6.7 %collective-permute-start.4 = (bf16[128,512]{1,0:T(8,128)(2,1)S(1)}, bf16[128,512]{1,0:T(8,128)(2,1)}, u32[]{:S(2)}, u32[]{:S(2)}) collective-permute-start(bf16[128,512]{1,0:T(8,128)(2,1)S(1)} %get-tuple-element.16), channel_id=1, source_target_pairs={{0,6},{2,0},{4,2},{6,4},{1,7},{3,1},{5,3},{7,5},{8,14},{10,8},{12,... | collective-permute-start | bytes 393224 | tf_op jit(solution)/shard_map/ppermute | solution.py:71
  143.7 6.2 %collective-permute-start.3 = (bf16[128,512]{1,0:T(8,128)(2,1)}, bf16[128,512]{1,0:T(8,128)(2,1)}, u32[]{:S(2)}, u32[]{:S(2)}) collective-permute-start(bf16[128,512]{1,0:T(8,128)(2,1)} %fusion.26), channel_id=1, source_target_pairs={{0,2},{2,4},{4,6},{6,0},{1,3},{3,5},{5,7},{7,1},{8,10},{10,12},{12... | collective-permute-start | bytes 393224 | tf_op jit(solution)/shard_map/ppermute | solution.py:70
  145.3 51.1 %copy-start.6 = (bf16[2,1,256,128]{2,3,0,1:T(8,128)(2,1)S(1)}, bf16[2,1,256,128]{2,3,0,1:T(8,128)(2,1)}, u32[]{:S(2)}) copy-start(bf16[2,1,256,128]{2,3,0,1:T(8,128)(2,1)} %copy.64) | copy-start | bytes 393220
  151.0 5.8 %collective-permute-start.5 = (bf16[128,512]{1,0:T(8,128)(2,1)S(1)}, bf16[128,512]{1,0:T(8,128)(2,1)S(1)}, u32[]{:S(2)}, u32[]{:S(2)}) collective-permute-start(bf16[128,512]{1,0:T(8,128)(2,1)S(1)} %get-tuple-element.14), channel_id=1, source_target_pairs={{0,6},{2,0},{4,2},{6,4},{1,7},{3,1},{5,3},{7,5},{8,14},{10,8},{12,... | collective-permute-start | bytes 393224 | tf_op jit(solution)/shard_map/ppermute | solution.py:71
  157.5 42.6 %collective-permute-start.6 = (bf16[128,512]{1,0:T(8,128)(2,1)}, bf16[128,512]{1,0:T(8,128)(2,1)}, u32[]{:S(2)}, u32[]{:S(2)}) collective-permute-start(bf16[128,512]{1,0:T(8,128)(2,1)} %fusion.23), channel_id=1, source_target_pairs={{0,6},{2,0},{4,2},{6,4},{1,7},{3,1},{5,3},{7,5},{8,14},{10,8},{12,... | collective-permute-start | bytes 393224 | tf_op jit(solution)/shard_map/ppermute | solution.py:71
  192.1 16.8 %all-to-all-start.4 = ((bf16[4,128,768]{1,2,0:T(8,128)(2,1)}), bf16[4,128,768]{1,2,0:T(8,128)(2,1)}, u32[]{:S(2)}, u32[]{:S(2)}) async-start(bf16[4,128,768]{1,2,0:T(8,128)(2,1)} %copy_bitcast_fusion), calls=%async_computation.5 | async-start | bytes 1572864 | tf_op jit(solution)/shard_map/all_to_all | solution.py:87
Sparse Core Ops, SparseCore 0:
  119.6 70.3 reduce-scatter.1

commit v4 on v3

--- a/solution.py
+++ b/solution.py
@@ -88,6 +88,16 @@
     return jnp.sum(gathered.astype(jnp.float32), 0).astype(part.dtype)
 
 
+def reduce_ctx_x_first(part):
+    n_x = lax.psum(1, "x")
+    n_z = lax.psum(1, "z")
+    rows = part.shape[0] // (n_x * n_z)
+    pieces = part.reshape(n_z, n_x, rows, part.shape[1]).transpose(1, 0, 2, 3)
+    gathered = lax.all_to_all(pieces, "x", 0, 0, tiled=True)
+    summed = jnp.sum(gathered.astype(jnp.float32), 0).astype(part.dtype)
+    return ring_rs(summed, "z", n_z)
+
+
 def per_device(activations, w_qkv, matching, dropout_bits, out_grad):
     f32 = jnp.float32
     local_tokens = activations.shape[0]
@@ -129,7 +139,11 @@
     grad_value = (grad_values[:, :, :BLK] + returned[1].astype(f32)).astype(jnp.bfloat16)
     stacked = jnp.stack([grad_query, grad_key, grad_value], 3)
     grad_qkv = stacked.transpose(1, 2, 0, 3, 4).reshape(local_tokens, head_count * 3 * HD)
-    weight_grad = reduce_ctx(weight_term(activations, grad_qkv))
+    weight_part = weight_term(activations, grad_qkv)
+    split = weight_part.shape[1] // 2
+    weight_grad = jnp.concatenate(
+        [reduce_ctx(weight_part[:, :split]), reduce_ctx_x_first(weight_part[:, split:])], 1
+    )
     n_y = lax.psum(1, "y")
     width = activations.shape[1] // (2 * n_y)
     w_split = w_qkv.reshape(n_y, 2, width, w_qkv.shape[1])

time: 219 us -> 252 us (1.15)
  starting transfers between devices: 40.7 us -> 66.9 us
  local copies, waits for them, and re-layouts: 24.7 us -> 45.8 us
  waiting for transfers between devices: 93 us -> 75.6 us
  other arithmetic: 15.1 us -> 20 us
    reduce_scatter x1, waiting for transfers between devices: 30 us -> 0.02 us  [reduce_ctx(): part = lax.psum_scatter(part, 'z', scatter_dimension=0, tiled=True)]
    ppermute x3 -> x10, starting transfers between devices: 6.19 us -> 23.3 us  [ring_rs(): got_b = lax.ppermute(acc_b, axis, ccw)]
    ppermute x3 -> x10, waiting for transfers between devices: 2.53 us -> 12.9 us  [ring_rs(): got_b = lax.ppermute(acc_b, axis, ccw)]
    reshape x0 -> x2, local copies, waits for them, and re-layouts: none -> 10.3 us  [reduce_ctx_x_first(): pieces = part.reshape(n_z, n_x, rows, part.shape[1]).transpose(1, 0, 2, 3)]
    ppermute x3 -> x10, waiting for transfers between devices: 11.7 us -> 17.2 us  [ring_rs(): got_a = lax.ppermute(acc_a, axis, cw)]
    slice x1 -> x2, local copies, waits for them, and re-layouts: 0.03 us -> 5.04 us  [take(): return block[:half] if part == 0 else block[half:]]
    all_to_all x0 -> x1, starting transfers between devices: none -> 4.67 us  [reduce_ctx_x_first(): gathered = lax.all_to_all(pieces, 'x', 0, 0, tiled=True)]
    ppermute x3 -> x10, starting transfers between devices: 4.91 us -> 8.81 us  [ring_rs(): got_a = lax.ppermute(acc_a, axis, cw)]
  transfers between devices with their start and end apart: 13 -> 28, of which waited for: 11 -> 21; matrix products, arithmetic and copies ran while one was open for 13% -> 19% of each run, Pallas kernels for 0% -> 0%
where the time goes in v4:
time: 252 us; the launch traced here: 250 us
  waiting for transfers between devices  75.6 us (30%)
  starting transfers between devices  66.9 us (27%)
  local copies, waits for them, and re-layouts  45.8 us (18%)
  matrix products  27.5 us (11%)
  other arithmetic  20 us (8%)
  between operations  14.6 us (6%)
    all_to_all x2, waiting for transfers between devices, route(): spread = lax.all_to_all(payload, CTX, 0, 0, tiled=True)  24.4 us
    ppermute x10, starting transfers between devices, ring_rs(): got_b = lax.ppermute(acc_b, axis, ccw)  23.3 us
    ppermute x10, waiting for transfers between devices, ring_rs(): got_a = lax.ppermute(acc_a, axis, cw)  17.2 us
    all_to_all x2, starting transfers between devices, route(): spread = lax.all_to_all(payload, CTX, 0, 0, tiled=True)  15.9 us
    all_to_all x2, waiting for transfers between devices, route(): return lax.all_to_all(chosen, CTX, 0, 0, tiled=True)  13.7 us
    ppermute x10, waiting for transfers between devices, ring_rs(): got_b = lax.ppermute(acc_b, axis, ccw)  12.9 us
    reshape x2, local copies, waits for them, and re-layouts, reduce_ctx_x_first(): pieces = part.reshape(n_z, n_x, rows, part.shape[1]).transpose(1, 0, 2, 3)  10.3 us
    all_to_all x2, starting transfers between devices, route(): return lax.all_to_all(chosen, CTX, 0, 0, tiled=True)  9.19 us
  transfers between devices with their start and end apart: 28, of which 21 were waited for; matrix products, arithmetic and copies ran while one was open for 19% of the time, Pallas kernels for 0%

profile of v4, /device:TPU:8, one launch (start us, length us, event | category | flops | bytes accessed | tf_op | source)
XLA Modules:
  0.0 250.4 jit_solution(14360037609368924064)
XLA Ops:
  7.2 1.6 copy-done
  8.8 4.6 %convolution_convert_fusion.2 = bf16[256,768]{1,0:T(8,128)(2,1)S(1)} fusion(bf16[256,4096]{1,0:T(8,128)(2,1)S(1)} %copy-done, bf16[4096,768]{1,0:T(8,128)(2,1)} %param.8), kind=kOutput, calls=%fused_computation.17 | convolution fusion | flops 1610809344 | bytes 8781824 | tf_op jit(solution)/shard_map/dot_general | solution.py:107
  14.6 11.3 %all-to-all-start = ((bf16[32,2,2,1,8,128]{5,4,2,1,3,0:T(8,128)(2,1)}), bf16[32,2,2,1,8,128]{5,4,2,1,3,0:T(8,128)(2,1)S(1)}, u32[]{:S(2)}, u32[]{:S(2)}) async-start(bf16[32,2,2,1,8,128]{5,4,2,1,3,0:T(8,128)(2,1)} %copy.60), calls=%async_computation | async-start | bytes 524288 | tf_op jit(solution)/shard_map/all_to_all | solution.py:35
  26.0 12.8 %all-to-all-done = bf16[32,2,2,1,8,128]{5,4,2,1,3,0:T(8,128)(2,1)S(1)} async-done(((bf16[32,2,2,1,8,128]{5,4,2,1,3,0:T(8,128)(2,1)}), bf16[32,2,2,1,8,128]{5,4,2,1,3,0:T(8,128)(2,1)S(1)}, u32[]{:S(2)}, u32[]{:S(2)}) %all-to-all-start) | async-done | bytes 262176 | tf_op jit(solution)/shard_map/all_to_all | solution.py:35
  40.1 4.6 %all-to-all-start.1 = ((bf16[32,2,2,1,8,128]{5,4,2,1,3,0:T(8,128)(2,1)}), bf16[32,2,2,1,8,128]{5,4,2,1,3,0:T(8,128)(2,1)}, u32[]{:S(2)}, u32[]{:S(2)}) async-start(bf16[32,2,2,1,8,128]{5,4,2,1,3,0:T(8,128)(2,1)} %fusion.29), calls=%async_computation.1 | async-start | bytes 524288 | tf_op jit(solution)/shard_map/all_to_all | solution.py:37
  45.7 1.3 copy.63
  49.5 7.2 %all-to-all-done.1 = bf16[32,2,2,1,8,128]{5,4,2,1,3,0:T(8,128)(2,1)} async-done(((bf16[32,2,2,1,8,128]{5,4,2,1,3,0:T(8,128)(2,1)}), bf16[32,2,2,1,8,128]{5,4,2,1,3,0:T(8,128)(2,1)}, u32[]{:S(2)}, u32[]{:S(2)}) %all-to-all-start.1) | async-done | bytes 262176 | tf_op jit(solution)/shard_map/all_to_all | solution.py:37
  56.7 1.0 copy.207
  59.0 1.3 fusion.67
  60.6 1.7 copy.64
  62.3 1.5 multiply_convert_fusion
  66.4 1.7 copy.74
  68.1 2.6 %fusion.6 = f32[2,256,512]{2,1,0:T(8,128)} fusion(s32[2,256,512]{2,1,0:T(8,128)} %copy.63, s32[512]{0:T(512)S(1)} %shift_right_arithmetic.28, bf16[2,1,256,128]{2,3,0,1:T(8,128)(2,1)} %copy.64, bf16[2,1,256,128]{2,3,0,1:T(8,128)(2,1)S(1)} %get-tuple-element.36, bf16[1,256,2,128]{3,2,1,0:T(2,128)(2,1)S(1)} %reshape.312), kind=kOutput, calls=%fused_computation.14 | convolution fusion | flops 68943872 | bytes 2492416 | tf_op jit(solution)/shard_map/hnqd,hnkd->hnqk/dot_general | solution.py:128
  70.6 5.2 %convolution_bitcast_fusion.2 = f32[2,1,512,128]{2,3,0,1:T(8,128)} fusion(f32[2,256,512]{2,1,0:T(8,128)} %fusion.6, f32[2,256,512]{2,1,0:T(8,128)S(1)} %get-tuple-element.43, f32[2,256]{1,0:T(2,128)S(1)} %log_add_fusion, bf16[256,2,1,128]{3,0,1,2:T(8,128)(2,1)} %copy.114), kind=kOutput, calls=%fused_computation.19 | convolution fusion | flops 68944896 | bytes 2754560 | tf_op jit(solution)/shard_map/hnqk,hnqd->hnkd/dot_general | solution.py:134
  77.6 1.0 maximum_bitcast_fusion.4
  79.4 4.6 %all-to-all-start.2 = ((bf16[32,2,2,1,8,128]{5,4,2,1,3,0:T(8,128)(2,1)}), bf16[32,2,2,1,8,128]{5,4,2,1,3,0:T(8,128)(2,1)}, u32[]{:S(2)}, u32[]{:S(2)}) async-start(bf16[32,2,2,1,8,128]{5,4,2,1,3,0:T(8,128)(2,1)} %copy.75), calls=%async_computation.2 | async-start | bytes 524288 | tf_op jit(solution)/shard_map/all_to_all | solution.py:35
  84.0 11.7 %all-to-all-done.2 = bf16[32,2,2,1,8,128]{5,4,2,1,3,0:T(8,128)(2,1)} async-done(((bf16[32,2,2,1,8,128]{5,4,2,1,3,0:T(8,128)(2,1)}), bf16[32,2,2,1,8,128]{5,4,2,1,3,0:T(8,128)(2,1)}, u32[]{:S(2)}, u32[]{:S(2)}) %all-to-all-start.2) | async-done | bytes 262176 | tf_op jit(solution)/shard_map/all_to_all | solution.py:35
  95.7 2.2 gather_fusion.1
  97.9 1.8 fusion.28
  99.7 4.6 %all-to-all-start.3 = ((bf16[32,2,2,1,8,128]{5,4,2,1,3,0:T(8,128)(2,1)}), bf16[32,2,2,1,8,128]{5,4,2,1,3,0:T(8,128)(2,1)}, u32[]{:S(2)}, u32[]{:S(2)}) async-start(bf16[32,2,2,1,8,128]{5,4,2,1,3,0:T(8,128)(2,1)} %fusion.28), calls=%async_computation.3 | async-start | bytes 524288 | tf_op jit(solution)/shard_map/all_to_all | solution.py:37
  104.3 5.1 %fusion.8 = bf16[2,1,256,1,128]{2,4,0,3,1:T(8,128)(2,1)} fusion(f32[2,256,512]{2,1,0:T(8,128)} %fusion.6, f32[2,256,512]{2,1,0:T(8,128)S(1)} %get-tuple-element.43, f32[2,256]{1,0:T(2,128)S(1)} %log_add_fusion, bf16[2,1,256,128]{3,2,0,1:T(8,128)(2,1)S(1)} %copy-done.6, bf16[2,1,256,128]{3,2,0,1:T(8,128)(2,1)S(1)} %bitcast.269), kind=kOutput, calls=%fused_computation.22 | convolution fusion | flops 69534720 | bytes 2492416 | tf_op jit(solution)/shard_map/hnqk,hnkd->hnqd/dot_general | solution.py:131
  109.5 6.5 %all-to-all-done.3 = bf16[32,2,2,1,8,128]{5,4,2,1,3,0:T(8,128)(2,1)} async-done(((bf16[32,2,2,1,8,128]{5,4,2,1,3,0:T(8,128)(2,1)}), bf16[32,2,2,1,8,128]{5,4,2,1,3,0:T(8,128)(2,1)}, u32[]{:S(2)}, u32[]{:S(2)}) %all-to-all-start.3) | async-done | bytes 262176 | tf_op jit(solution)/shard_map/all_to_all | solution.py:37
  116.0 1.0 copy.206
  117.3 1.1 fusion.44
  118.5 4.6 %convolution_convert_fusion.1 = bf16[256,4,2,512]{3,0,2,1:T(8,128)(2,1)S(1)} fusion(bf16[256,768,1,1]{0,1,3,2:T(8,128)(2,1)S(1)} %bitcast.264, bf16[4,2,512,768]{3,2,1,0:T(8,128)(2,1)} %bitcast.280), kind=kOutput, calls=%fused_computation.9 | convolution fusion | flops 1611661312 | bytes 8781824 | tf_op jit(solution)/shard_map/tk,ycwk->cytw/dot_general | solution.py:150
  124.4 1.8 fusion.1
  126.2 3.1 %fusion.65 = (bf16[4096,384]{0,1:T(8,128)(2,1)}, bf16[4096,384]{0,1:T(8,128)(2,1)}) fusion(bf16[4096,768]{0,1:T(8,128)(2,1)S(1)} %fusion.1), kind=kLoop, calls=%fused_computation.168 | loop fusion | bytes 12582912 | tf_op jit(solution)/shard_map/slice | solution.py:145
  129.3 6.1 %reshape.317 = bf16[8,4,128,384]{2,1,0,3:T(4,128)(2,1)} reshape(bf16[4096,384]{0,1:T(8,128)(2,1)} %get-tuple-element.14) | data formatting | bytes 6291456 | tf_op jit(solution)/shard_map/reshape | solution.py:95
  135.4 4.2 %copy.205 = bf16[8,4,128,384]{2,0,3,1:T(8,128)(2,1)} copy(bf16[8,4,128,384]{2,1,0,3:T(4,128)(2,1)} %reshape.317) | data formatting | bytes 6291456 | tf_op jit(solution)/shard_map/reshape | solution.py:95
  139.6 4.7 %all-to-all-start.5 = ((bf16[4,8,128,384]{2,1,3,0:T(8,128)(2,1)}), bf16[4,8,128,384]{2,1,3,0:T(8,128)(2,1)}, u32[]{:S(2)}, u32[]{:S(2)}) async-start(bf16[4,8,128,384]{2,1,3,0:T(8,128)(2,1)} %bitcast.262), calls=%async_computation.6 | async-start | bytes 6291456 | tf_op jit(solution)/shard_map/all_to_all | solution.py:96
  144.3 1.9 fusion.2
  146.9 1.5 collective-permute-start.1
  148.4 3.8 %collective-permute-done.1 = bf16[128,512]{1,0:T(8,128)(2,1)} collective-permute-done((bf16[128,512]{1,0:T(8,128)(2,1)}, bf16[128,512]{1,0:T(8,128)(2,1)}, u32[]{:S(2)}, u32[]{:S(2)}) %collective-permute-start.1) | collective-permute-done | bytes 131104 | tf_op jit(solution)/shard_map/ppermute | solution.py:70
  152.3 1.6 fusion.27
  153.9 1.6 collective-permute-start.2
  155.9 3.3 %collective-permute-done.2 = bf16[128,512]{1,0:T(8,128)(2,1)} collective-permute-done((bf16[128,512]{1,0:T(8,128)(2,1)}, bf16[128,512]{1,0:T(8,128)(2,1)}, u32[]{:S(2)}, u32[]{:S(2)}) %collective-permute-start.2) | collective-permute-done | bytes 131104 | tf_op jit(solution)/shard_map/ppermute | solution.py:70
  159.2 1.6 fusion.26
  160.7 1.6 collective-permute-start.3
  162.3 4.6 %collective-permute-done.3 = bf16[128,512]{1,0:T(8,128)(2,1)} collective-permute-done((bf16[128,512]{1,0:T(8,128)(2,1)}, bf16[128,512]{1,0:T(8,128)(2,1)}, u32[]{:S(2)}, u32[]{:S(2)}) %collective-permute-start.3) | collective-permute-done | bytes 131104 | tf_op jit(solution)/shard_map/ppermute | solution.py:70
  166.9 1.7 fusion.25
  168.6 3.2 %collective-permute-start.5 = (bf16[128,512]{1,0:T(8,128)(2,1)}, bf16[128,512]{1,0:T(8,128)(2,1)}, u32[]{:S(2)}, u32[]{:S(2)}) collective-permute-start(bf16[128,512]{1,0:T(8,128)(2,1)} %get-tuple-element.16), channel_id=1, source_target_pairs={{0,6},{2,0},{4,2},{6,4},{1,7},{3,1},{5,3},{7,5},{8,14},{10,8},{12,... | collective-permute-start | bytes 393224 | tf_op jit(solution)/shard_map/ppermute | solution.py:71
  171.9 2.8 %collective-permute-done.5 = bf16[128,512]{1,0:T(8,128)(2,1)} collective-permute-done((bf16[128,512]{1,0:T(8,128)(2,1)}, bf16[128,512]{1,0:T(8,128)(2,1)}, u32[]{:S(2)}, u32[]{:S(2)}) %collective-permute-start.5) | collective-permute-done | bytes 131104 | tf_op jit(solution)/shard_map/ppermute | solution.py:71
  174.7 1.6 fusion.23
  176.3 2.4 collective-permute-start.6
  178.7 2.0 convolution_convert_fusion.4
  180.8 1.7 copy.101
  183.4 2.8 %reduce_sum.45 = bf16[8,128,384]{1,0,2:T(8,128)(2,1)S(1)} reduce(bf16[4,8,128,384]{2,1,3,0:T(8,128)(2,1)} %all-to-all-done.5, bf16[]{:T(256)} %constant.258.clone.1), dimensions={0}, to_apply=%region_6.8 | reduce | flops 1179648 | bytes 3932162 | tf_op jit(solution)/shard_map/reduce_sum | solution.py:97
  186.2 4.4 %constant_dynamic-slice_fusion = (bf16[1,64,384]{1,0,2:T(2,128)(2,1)S(1)}, bf16[1,64,384]{1,0,2:T(2,128)(2,1)S(1)}, bf16[1,64,384]{1,0,2:T(2,128)(2,1)S(1)}, bf1...) fusion(bf16[8,128,384]{1,0,2:T(8,128)(2,1)S(1)} %reduce_sum.45,, ...), kind=kLoop, calls=%fused_computation.133 | loop fusion | bytes 1572924 | tf_op jit(solution)/shard_map/slice | solution.py:65
  191.7 2.1 collective-permute-start.7
  193.7 2.8 %collective-permute-done.14 = bf16[64,384]{0,1:T(8,128)(2,1)S(1)} collective-permute-done((bf16[64,384]{0,1:T(8,128)(2,1)S(1)}, bf16[64,384]{0,1:T(8,128)(2,1)S(1)}, u32[]{:S(2)}, u32[]{:S(2)}) %collective-permute-start.14) | collective-permute-done | bytes 49184 | tf_op jit(solution)/shard_map/ppermute | solution.py:71
  197.6 1.6 collective-permute-start.8
  199.2 2.2 collective-permute-done.15
  201.5 2.0 collective-permute-start.16
  204.6 1.6 collective-permute-done.16
  206.2 3.4 %collective-permute-start.17 = (bf16[64,384]{0,1:T(8,128)(2,1)S(1)}, bf16[64,384]{0,1:T(8,128)(2,1)S(1)}, u32[]{:S(2)}, u32[]{:S(2)}) collective-permute-start(bf16[64,384]{0,1:T(8,128)(2,1)S(1)} %fusion.34), channel_id=1, source_target_pairs={{0,224},{32,0},{64,32},{96,64},{128,96},{160,128},{192,160},{224,1... | collective-permute-start | bytes 147464 | tf_op jit(solution)/shard_map/ppermute | solution.py:71
  210.8 1.1 collective-permute-done.17
  211.9 3.7 %collective-permute-start.18 = (bf16[64,384]{0,1:T(8,128)(2,1)S(1)}, bf16[64,384]{0,1:T(8,128)(2,1)S(1)}, u32[]{:S(2)}, u32[]{:S(2)}) collective-permute-start(bf16[64,384]{0,1:T(8,128)(2,1)S(1)} %fusion.33), channel_id=1, source_target_pairs={{0,224},{32,0},{64,32},{96,64},{128,96},{160,128},{192,160},{224,1... | collective-permute-start | bytes 147464 | tf_op jit(solution)/shard_map/ppermute | solution.py:71
  216.7 1.1 collective-permute-done.18
  217.9 3.7 %collective-permute-start.19 = (bf16[64,384]{0,1:T(8,128)(2,1)S(1)}, bf16[64,384]{0,1:T(8,128)(2,1)S(1)}, u32[]{:S(2)}, u32[]{:S(2)}) collective-permute-start(bf16[64,384]{0,1:T(8,128)(2,1)S(1)} %fusion.32), channel_id=1, source_target_pairs={{0,224},{32,0},{64,32},{96,64},{128,96},{160,128},{192,160},{224,1... | collective-permute-start | bytes 147464 | tf_op jit(solution)/shard_map/ppermute | solution.py:71
  222.6 1.1 collective-permute-done.19
  223.8 3.7 %collective-permute-start.20 = (bf16[64,384]{0,1:T(8,128)(2,1)S(1)}, bf16[64,384]{0,1:T(8,128)(2,1)S(1)}, u32[]{:S(2)}, u32[]{:S(2)}) collective-permute-start(bf16[64,384]{0,1:T(8,128)(2,1)S(1)} %fusion.31), channel_id=1, source_target_pairs={{0,224},{32,0},{64,32},{96,64},{128,96},{160,128},{192,160},{224,1... | collective-permute-start | bytes 147464 | tf_op jit(solution)/shard_map/ppermute | solution.py:71
  228.6 1.8 copy_bitcast_fusion.1
  230.4 4.7 %all-to-all-start.4 = ((bf16[4,128,384]{1,2,0:T(8,128)(2,1)}), bf16[4,128,384]{1,2,0:T(8,128)(2,1)S(1)}, u32[]{:S(2)}, u32[]{:S(2)}) async-start(bf16[4,128,384]{1,2,0:T(8,128)(2,1)} %copy_bitcast_fusion.1), calls=%async_computation.5 | async-start | bytes 786432 | tf_op jit(solution)/shard_map/all_to_all | solution.py:87
  235.2 7.3 %all-to-all-done.4 = bf16[4,128,384]{1,2,0:T(8,128)(2,1)S(1)} async-done(((bf16[4,128,384]{1,2,0:T(8,128)(2,1)}), bf16[4,128,384]{1,2,0:T(8,128)(2,1)S(1)}, u32[]{:S(2)}, u32[]{:S(2)}) %all-to-all-start.4) | async-done | bytes 393248 | tf_op jit(solution)/shard_map/all_to_all | solution.py:87
  (99 shorter events, 25.3 us)
Async XLA Ops:
  7.2 1.6 copy-start
  13.3 12.6 %copy-start.8 = (s32[1,32]{1,0:T(1,128)S(1)}, s32[1,32]{1,0:T(1,128)}, u32[]{:S(2)}) copy-start(s32[1,32]{1,0:T(1,128)} %param.9) | copy-start | bytes 388
  14.6 24.1 %all-to-all-start = ((bf16[32,2,2,1,8,128]{5,4,2,1,3,0:T(8,128)(2,1)}), bf16[32,2,2,1,8,128]{5,4,2,1,3,0:T(8,128)(2,1)S(1)}, u32[]{:S(2)}, u32[]{:S(2)}) async-start(bf16[32,2,2,1,8,128]{5,4,2,1,3,0:T(8,128)(2,1)} %copy.60), calls=%async_computation | async-start | bytes 524288 | tf_op jit(solution)/shard_map/all_to_all | solution.py:35
  40.1 16.5 %all-to-all-start.1 = ((bf16[32,2,2,1,8,128]{5,4,2,1,3,0:T(8,128)(2,1)}), bf16[32,2,2,1,8,128]{5,4,2,1,3,0:T(8,128)(2,1)}, u32[]{:S(2)}, u32[]{:S(2)}) async-start(bf16[32,2,2,1,8,128]{5,4,2,1,3,0:T(8,128)(2,1)} %fusion.29), calls=%async_computation.1 | async-start | bytes 524288 | tf_op jit(solution)/shard_map/all_to_all | solution.py:37
  58.3 0.7 copy-start.5
  63.8 0.8 copy-start.1
  64.9 0.8 copy-start.3
  77.6 26.7 %copy-start.6 = (bf16[2,1,256,128]{3,2,0,1:T(8,128)(2,1)S(1)}, bf16[2,1,256,128]{3,2,0,1:T(8,128)(2,1)}, u32[]{:S(2)}) copy-start(bf16[2,1,256,128]{3,2,0,1:T(8,128)(2,1)} %copy-done.5) | copy-start | bytes 393220
  79.4 16.3 %all-to-all-start.2 = ((bf16[32,2,2,1,8,128]{5,4,2,1,3,0:T(8,128)(2,1)}), bf16[32,2,2,1,8,128]{5,4,2,1,3,0:T(8,128)(2,1)}, u32[]{:S(2)}, u32[]{:S(2)}) async-start(bf16[32,2,2,1,8,128]{5,4,2,1,3,0:T(8,128)(2,1)} %copy.75), calls=%async_computation.2 | async-start | bytes 524288 | tf_op jit(solution)/shard_map/all_to_all | solution.py:35
  99.7 16.3 %all-to-all-start.3 = ((bf16[32,2,2,1,8,128]{5,4,2,1,3,0:T(8,128)(2,1)}), bf16[32,2,2,1,8,128]{5,4,2,1,3,0:T(8,128)(2,1)}, u32[]{:S(2)}, u32[]{:S(2)}) async-start(bf16[32,2,2,1,8,128]{5,4,2,1,3,0:T(8,128)(2,1)} %fusion.28), calls=%async_computation.3 | async-start | bytes 524288 | tf_op jit(solution)/shard_map/all_to_all | solution.py:37
  104.3 124.3 %reduce-scatter.2.cloned.1.call-start = ((), (), s32[]{:S(2)}) async-start(), calls=%async_computation.7 | async-start | bytes 3538944 | tf_op jit(solution)/shard_map/reduce_scatter | solution.py:84
  109.5 8.9 %copy-start.7 = (bf16[2,1,256,1,128]{2,4,0,3,1:T(8,128)(2,1)S(1)}, bf16[2,1,256,1,128]{2,4,0,3,1:T(8,128)(2,1)}, u32[]{:S(2)}) copy-start(bf16[2,1,256,1,128]{2,4,0,3,1:T(8,128)(2,1)} %fusion.8) | copy-start | bytes 393220
  123.1 1.3 copy-start.2
  123.2 21.1 %collective-permute-start = (bf16[4,256,512]{2,1,0:T(8,128)(2,1)S(1)}, bf16[4,256,512]{2,1,0:T(8,128)(2,1)}, u32[]{:S(2)}, u32[]{:S(2)}) collective-permute-start(bf16[4,256,512]{2,1,0:T(8,128)(2,1)S(1)} %dynamic-slice_bitcast_fusion), channel_id=1, source_target_pairs={{0,1},{1,0},{2,3},{3,2},{4,5},{5,4},{6,7},{7,6},{8,9},{9,8},{10,11... | collective-permute-start | bytes 3145736 | tf_op jit(solution)/shard_map/ppermute | solution.py:57
  139.6 43.8 %all-to-all-start.5 = ((bf16[4,8,128,384]{2,1,3,0:T(8,128)(2,1)}), bf16[4,8,128,384]{2,1,3,0:T(8,128)(2,1)}, u32[]{:S(2)}, u32[]{:S(2)}) async-start(bf16[4,8,128,384]{2,1,3,0:T(8,128)(2,1)} %bitcast.262), calls=%async_computation.6 | async-start | bytes 6291456 | tf_op jit(solution)/shard_map/all_to_all | solution.py:96
  144.3 34.5 %copy-start.4 = (bf16[2,1,256,128]{2,3,0,1:T(8,128)(2,1)S(1)}, bf16[2,1,256,128]{2,3,0,1:T(8,128)(2,1)}, u32[]{:S(2)}) copy-start(bf16[2,1,256,128]{2,3,0,1:T(8,128)(2,1)} %copy.64) | copy-start | bytes 393220
  146.9 5.4 %collective-permute-start.1 = (bf16[128,512]{1,0:T(8,128)(2,1)}, bf16[128,512]{1,0:T(8,128)(2,1)}, u32[]{:S(2)}, u32[]{:S(2)}) collective-permute-start(bf16[128,512]{1,0:T(8,128)(2,1)} %get-tuple-element.17), channel_id=1, source_target_pairs={{0,2},{2,4},{4,6},{6,0},{1,3},{3,5},{5,7},{7,1},{8,10},{10,12},{12... | collective-permute-start | bytes 393224 | tf_op jit(solution)/shard_map/ppermute | solution.py:70
  153.9 5.3 %collective-permute-start.2 = (bf16[128,512]{1,0:T(8,128)(2,1)}, bf16[128,512]{1,0:T(8,128)(2,1)}, u32[]{:S(2)}, u32[]{:S(2)}) collective-permute-start(bf16[128,512]{1,0:T(8,128)(2,1)} %fusion.27), channel_id=1, source_target_pairs={{0,2},{2,4},{4,6},{6,0},{1,3},{3,5},{5,7},{7,1},{8,10},{10,12},{12... | collective-permute-start | bytes 393224 | tf_op jit(solution)/shard_map/ppermute | solution.py:70
  155.4 6.9 %collective-permute-start.4 = (bf16[128,512]{1,0:T(8,128)(2,1)S(1)}, bf16[128,512]{1,0:T(8,128)(2,1)}, u32[]{:S(2)}, u32[]{:S(2)}) collective-permute-start(bf16[128,512]{1,0:T(8,128)(2,1)S(1)} %get-tuple-element.18), channel_id=1, source_target_pairs={{0,6},{2,0},{4,2},{6,4},{1,7},{3,1},{5,3},{7,5},{8,14},{10,8},{12,... | collective-permute-start | bytes 393224 | tf_op jit(solution)/shard_map/ppermute | solution.py:71
  160.7 6.2 %collective-permute-start.3 = (bf16[128,512]{1,0:T(8,128)(2,1)}, bf16[128,512]{1,0:T(8,128)(2,1)}, u32[]{:S(2)}, u32[]{:S(2)}) collective-permute-start(bf16[128,512]{1,0:T(8,128)(2,1)} %fusion.26), channel_id=1, source_target_pairs={{0,2},{2,4},{4,6},{6,0},{1,3},{3,5},{5,7},{7,1},{8,10},{10,12},{12... | collective-permute-start | bytes 393224 | tf_op jit(solution)/shard_map/ppermute | solution.py:70
  168.6 6.1 %collective-permute-start.5 = (bf16[128,512]{1,0:T(8,128)(2,1)}, bf16[128,512]{1,0:T(8,128)(2,1)}, u32[]{:S(2)}, u32[]{:S(2)}) collective-permute-start(bf16[128,512]{1,0:T(8,128)(2,1)} %get-tuple-element.16), channel_id=1, source_target_pairs={{0,6},{2,0},{4,2},{6,4},{1,7},{3,1},{5,3},{7,5},{8,14},{10,8},{12,... | collective-permute-start | bytes 393224 | tf_op jit(solution)/shard_map/ppermute | solution.py:71
  176.3 6.1 %collective-permute-start.6 = (bf16[128,512]{1,0:T(8,128)(2,1)}, bf16[128,512]{1,0:T(8,128)(2,1)}, u32[]{:S(2)}, u32[]{:S(2)}) collective-permute-start(bf16[128,512]{1,0:T(8,128)(2,1)} %fusion.23), channel_id=1, source_target_pairs={{0,6},{2,0},{4,2},{6,4},{1,7},{3,1},{5,3},{7,5},{8,14},{10,8},{12,... | collective-permute-start | bytes 393224 | tf_op jit(solution)/shard_map/ppermute | solution.py:71
  190.6 6.0 %collective-permute-start.14 = (bf16[64,384]{0,1:T(8,128)(2,1)S(1)}, bf16[64,384]{0,1:T(8,128)(2,1)S(1)}, u32[]{:S(2)}, u32[]{:S(2)}) collective-permute-start(bf16[64,384]{0,1:T(8,128)(2,1)S(1)} %bitcast.278), channel_id=1, source_target_pairs={{0,224},{32,0},{64,32},{96,64},{128,96},{160,128},{192,160},{224,1... | collective-permute-start | bytes 147464 | tf_op jit(solution)/shard_map/ppermute | solution.py:71
  191.7 5.9 %collective-permute-start.7 = (bf16[64,384]{0,1:T(8,128)(2,1)S(1)}, bf16[64,384]{0,1:T(8,128)(2,1)S(1)}, u32[]{:S(2)}, u32[]{:S(2)}) collective-permute-start(bf16[64,384]{0,1:T(8,128)(2,1)S(1)} %bitcast.277), channel_id=1, source_target_pairs={{0,32},{32,64},{64,96},{96,128},{128,160},{160,192},{192,224},{224... | collective-permute-start | bytes 147464 | tf_op jit(solution)/shard_map/ppermute | solution.py:70
  196.6 4.9 %collective-permute-start.15 = (bf16[64,384]{0,1:T(8,128)(2,1)S(1)}, bf16[64,384]{0,1:T(8,128)(2,1)S(1)}, u32[]{:S(2)}, u32[]{:S(2)}) collective-permute-start(bf16[64,384]{0,1:T(8,128)(2,1)S(1)} %fusion.36), channel_id=1, source_target_pairs={{0,224},{32,0},{64,32},{96,64},{128,96},{160,128},{192,160},{224,1... | collective-permute-start | bytes 147464 | tf_op jit(solution)/shard_map/ppermute | solution.py:71
  197.6 6.9 %collective-permute-start.8 = (bf16[64,384]{0,1:T(8,128)(2,1)S(1)}, bf16[64,384]{0,1:T(8,128)(2,1)S(1)}, u32[]{:S(2)}, u32[]{:S(2)}) collective-permute-start(bf16[64,384]{0,1:T(8,128)(2,1)S(1)} %fusion.43), channel_id=1, source_target_pairs={{0,32},{32,64},{64,96},{96,128},{128,160},{160,192},{192,224},{224... | collective-permute-start | bytes 147464 | tf_op jit(solution)/shard_map/ppermute | solution.py:70
  201.5 4.7 %collective-permute-start.16 = (bf16[64,384]{0,1:T(8,128)(2,1)S(1)}, bf16[64,384]{0,1:T(8,128)(2,1)S(1)}, u32[]{:S(2)}, u32[]{:S(2)}) collective-permute-start(bf16[64,384]{0,1:T(8,128)(2,1)S(1)} %fusion.35), channel_id=1, source_target_pairs={{0,224},{32,0},{64,32},{96,64},{128,96},{160,128},{192,160},{224,1... | collective-permute-start | bytes 147464 | tf_op jit(solution)/shard_map/ppermute | solution.py:71
  204.5 6.1 %collective-permute-start.9 = (bf16[64,384]{0,1:T(8,128)(2,1)S(1)}, bf16[64,384]{0,1:T(8,128)(2,1)S(1)}, u32[]{:S(2)}, u32[]{:S(2)}) collective-permute-start(bf16[64,384]{0,1:T(8,128)(2,1)S(1)} %fusion.42), channel_id=1, source_target_pairs={{0,32},{32,64},{64,96},{96,128},{128,160},{160,192},{192,224},{224... | collective-permute-start | bytes 147464 | tf_op jit(solution)/shard_map/ppermute | solution.py:70
  206.2 5.7 %collective-permute-start.17 = (bf16[64,384]{0,1:T(8,128)(2,1)S(1)}, bf16[64,384]{0,1:T(8,128)(2,1)S(1)}, u32[]{:S(2)}, u32[]{:S(2)}) collective-permute-start(bf16[64,384]{0,1:T(8,128)(2,1)S(1)} %fusion.34), channel_id=1, source_target_pairs={{0,224},{32,0},{64,32},{96,64},{128,96},{160,128},{192,160},{224,1... | collective-permute-start | bytes 147464 | tf_op jit(solution)/shard_map/ppermute | solution.py:71
  210.7 5.9 %collective-permute-start.10 = (bf16[64,384]{0,1:T(8,128)(2,1)S(1)}, bf16[64,384]{0,1:T(8,128)(2,1)S(1)}, u32[]{:S(2)}, u32[]{:S(2)}) collective-permute-start(bf16[64,384]{0,1:T(8,128)(2,1)S(1)} %fusion.41), channel_id=1, source_target_pairs={{0,32},{32,64},{64,96},{96,128},{128,160},{160,192},{192,224},{224... | collective-permute-start | bytes 147464 | tf_op jit(solution)/shard_map/ppermute | solution.py:70
  211.9 5.9 %collective-permute-start.18 = (bf16[64,384]{0,1:T(8,128)(2,1)S(1)}, bf16[64,384]{0,1:T(8,128)(2,1)S(1)}, u32[]{:S(2)}, u32[]{:S(2)}) collective-permute-start(bf16[64,384]{0,1:T(8,128)(2,1)S(1)} %fusion.33), channel_id=1, source_target_pairs={{0,224},{32,0},{64,32},{96,64},{128,96},{160,128},{192,160},{224,1... | collective-permute-start | bytes 147464 | tf_op jit(solution)/shard_map/ppermute | solution.py:71
  216.6 5.9 %collective-permute-start.11 = (bf16[64,384]{0,1:T(8,128)(2,1)S(1)}, bf16[64,384]{0,1:T(8,128)(2,1)S(1)}, u32[]{:S(2)}, u32[]{:S(2)}) collective-permute-start(bf16[64,384]{0,1:T(8,128)(2,1)S(1)} %fusion.40), channel_id=1, source_target_pairs={{0,32},{32,64},{64,96},{96,128},{128,160},{160,192},{192,224},{224... | collective-permute-start | bytes 147464 | tf_op jit(solution)/shard_map/ppermute | solution.py:70
  217.9 5.9 %collective-permute-start.19 = (bf16[64,384]{0,1:T(8,128)(2,1)S(1)}, bf16[64,384]{0,1:T(8,128)(2,1)S(1)}, u32[]{:S(2)}, u32[]{:S(2)}) collective-permute-start(bf16[64,384]{0,1:T(8,128)(2,1)S(1)} %fusion.32), channel_id=1, source_target_pairs={{0,224},{32,0},{64,32},{96,64},{128,96},{160,128},{192,160},{224,1... | collective-permute-start | bytes 147464 | tf_op jit(solution)/shard_map/ppermute | solution.py:71
  222.5 5.9 %collective-permute-start.12 = (bf16[64,384]{0,1:T(8,128)(2,1)S(1)}, bf16[64,384]{0,1:T(8,128)(2,1)S(1)}, u32[]{:S(2)}, u32[]{:S(2)}) collective-permute-start(bf16[64,384]{0,1:T(8,128)(2,1)S(1)} %fusion.39), channel_id=1, source_target_pairs={{0,32},{32,64},{64,96},{96,128},{128,160},{160,192},{192,224},{224... | collective-permute-start | bytes 147464 | tf_op jit(solution)/shard_map/ppermute | solution.py:70
  223.8 11.4 %collective-permute-start.20 = (bf16[64,384]{0,1:T(8,128)(2,1)S(1)}, bf16[64,384]{0,1:T(8,128)(2,1)S(1)}, u32[]{:S(2)}, u32[]{:S(2)}) collective-permute-start(bf16[64,384]{0,1:T(8,128)(2,1)S(1)} %fusion.31), channel_id=1, source_target_pairs={{0,224},{32,0},{64,32},{96,64},{128,96},{160,128},{192,160},{224,1... | collective-permute-start | bytes 147464 | tf_op jit(solution)/shard_map/ppermute | solution.py:71
  228.5 6.7 %collective-permute-start.13 = (bf16[64,384]{0,1:T(8,128)(2,1)S(1)}, bf16[64,384]{0,1:T(8,128)(2,1)S(1)}, u32[]{:S(2)}, u32[]{:S(2)}) collective-permute-start(bf16[64,384]{0,1:T(8,128)(2,1)S(1)} %fusion.38), channel_id=1, source_target_pairs={{0,32},{32,64},{64,96},{96,128},{128,160},{160,192},{192,224},{224... | collective-permute-start | bytes 147464 | tf_op jit(solution)/shard_map/ppermute | solution.py:70
  230.4 12.1 %all-to-all-start.4 = ((bf16[4,128,384]{1,2,0:T(8,128)(2,1)}), bf16[4,128,384]{1,2,0:T(8,128)(2,1)S(1)}, u32[]{:S(2)}, u32[]{:S(2)}) async-start(bf16[4,128,384]{1,2,0:T(8,128)(2,1)} %copy_bitcast_fusion.1), calls=%async_computation.5 | async-start | bytes 786432 | tf_op jit(solution)/shard_map/all_to_all | solution.py:87
Sparse Core Ops, SparseCore 0:
  129.4 42.0 reduce-scatter.1

commit v5 on v3

--- a/solution.py
+++ b/solution.py
@@ -33,8 +33,11 @@
 
 def route(payload, order):
     spread = lax.all_to_all(payload, CTX, 0, 0, tiled=True)
-    chosen = jnp.take(spread, order, axis=0)
-    return lax.all_to_all(chosen, CTX, 0, 0, tiled=True)
+    pieces = spread.shape[0]
+    pick = (order[:, None] == jnp.arange(pieces, dtype=order.dtype)[None, :]).astype(spread.dtype)
+    flat = spread.reshape(pieces, -1)
+    chosen = jnp.dot(pick, flat, preferred_element_type=jnp.float32).astype(spread.dtype)
+    return lax.all_to_all(chosen.reshape(spread.shape), CTX, 0, 0, tiled=True)
 
 
 def to_pieces(blocked, pieces):
@@ -103,30 +106,48 @@
     inverse = jnp.zeros_like(order).at[order].set(jnp.arange(n_ctx, dtype=order.dtype))
     own_kv = jnp.stack([key_own, value_own], 0)
     far_kv = from_pieces(route(to_pieces(own_kv, n_ctx), order))
-    keys = jnp.concatenate([key_own, far_kv[0]], 2)
-    values = jnp.concatenate([value_own, far_kv[1]], 2)
-    scores = jnp.einsum("hnqd,hnkd->hnqk", query, keys, preferred_element_type=f32) * score_scale
-    row_max = jnp.max(scores, -1, keepdims=True)
-    log_total = row_max + jnp.log(jnp.sum(jnp.exp(scores - row_max), -1, keepdims=True))
-    probability = jnp.exp(scores - log_total)
-    kept = unpack_bits(to_blocks(dropout_bits, WORDS))
-    dropped = (probability * kept).astype(jnp.bfloat16)
-    attended = jnp.einsum("hnqk,hnkd->hnqd", dropped, values, preferred_element_type=f32).astype(
-        jnp.bfloat16
+    key_far, value_far = far_kv[0], far_kv[1]
+
+    def mm(form, left, right):
+        return jnp.einsum(form, left, right, preferred_element_type=f32)
+
+    score_own = mm("hnqd,hnkd->hnqk", query, key_own) * score_scale
+    score_far = mm("hnqd,hnkd->hnqk", query, key_far) * score_scale
+    row_max = jnp.maximum(jnp.max(score_own, -1, keepdims=True), jnp.max(score_far, -1, keepdims=True))
+    total = jnp.sum(jnp.exp(score_own - row_max), -1, keepdims=True) + jnp.sum(
+        jnp.exp(score_far - row_max), -1, keepdims=True
     )
+    log_total = row_max + jnp.log(total)
+    prob_own = jnp.exp(score_own - log_total)
+    prob_far = jnp.exp(score_far - log_total)
+    words = to_blocks(dropout_bits, WORDS)
+    half_words = WORDS // 2
+    kept_own = unpack_bits(words[..., :half_words])
+    kept_far = unpack_bits(words[..., half_words:])
+    dropped_own = (prob_own * kept_own).astype(jnp.bfloat16)
+    dropped_far = (prob_far * kept_far).astype(jnp.bfloat16)
+    attended = (
+        mm("hnqk,hnkd->hnqd", dropped_own, value_own) + mm("hnqk,hnkd->hnqd", dropped_far, value_far)
+    ).astype(jnp.bfloat16)
     grad_out = to_blocks(out_grad, HD)
-    grad_prob = jnp.einsum("hnqd,hnkd->hnqk", grad_out, values, preferred_element_type=f32) * kept
-    row_delta = jnp.sum(probability * grad_prob, -1, keepdims=True)
-    grad_score = (probability * (grad_prob - row_delta) * score_scale).astype(jnp.bfloat16)
-    grad_query = jnp.einsum("hnqk,hnkd->hnqd", grad_score, keys, preferred_element_type=f32).astype(
-        jnp.bfloat16
+    grad_prob_own = mm("hnqd,hnkd->hnqk", grad_out, value_own) * kept_own
+    grad_prob_far = mm("hnqd,hnkd->hnqk", grad_out, value_far) * kept_far
+    row_delta = jnp.sum(prob_own * grad_prob_own, -1, keepdims=True) + jnp.sum(
+        prob_far * grad_prob_far, -1, keepdims=True
     )
-    grad_keys = jnp.einsum("hnqk,hnqd->hnkd", grad_score, query, preferred_element_type=f32)
-    grad_values = jnp.einsum("hnqk,hnqd->hnkd", dropped, grad_out, preferred_element_type=f32)
-    far_part = jnp.stack([grad_keys[:, :, BLK:], grad_values[:, :, BLK:]], 0).astype(jnp.bfloat16)
+    score_grad_own = (prob_own * (grad_prob_own - row_delta) * score_scale).astype(jnp.bfloat16)
+    score_grad_far = (prob_far * (grad_prob_far - row_delta) * score_scale).astype(jnp.bfloat16)
+    grad_query = (
+        mm("hnqk,hnkd->hnqd", score_grad_own, key_own) + mm("hnqk,hnkd->hnqd", score_grad_far, key_far)
+    ).astype(jnp.bfloat16)
+    grad_key_own = mm("hnqk,hnqd->hnkd", score_grad_own, query)
+    grad_value_own = mm("hnqk,hnqd->hnkd", dropped_own, grad_out)
+    far_part = jnp.stack(
+        [mm("hnqk,hnqd->hnkd", score_grad_far, query), mm("hnqk,hnqd->hnkd", dropped_far, grad_out)], 0
+    ).astype(jnp.bfloat16)
     returned = from_pieces(route(to_pieces(far_part, n_ctx), inverse))
-    grad_key = (grad_keys[:, :, :BLK] + returned[0].astype(f32)).astype(jnp.bfloat16)
-    grad_value = (grad_values[:, :, :BLK] + returned[1].astype(f32)).astype(jnp.bfloat16)
+    grad_key = (grad_key_own + returned[0].astype(f32)).astype(jnp.bfloat16)
+    grad_value = (grad_value_own + returned[1].astype(f32)).astype(jnp.bfloat16)
     stacked = jnp.stack([grad_query, grad_key, grad_value], 3)
     grad_qkv = stacked.transpose(1, 2, 0, 3, 4).reshape(local_tokens, head_count * 3 * HD)
     weight_grad = reduce_ctx(weight_term(activations, grad_qkv))

time: 219 us -> 203 us (0.927)
  blocking collectives: 0 us -> 23.9 us
  starting transfers between devices: 40.7 us -> 28.5 us
  waiting for transfers between devices: 93 us -> 80.9 us
  matrix products: 29.9 us -> 21.3 us
  local copies, waits for them, and re-layouts: 24.7 us -> 16.3 us
    all_to_all x0 -> x1, blocking collectives: none -> 23.9 us  [route(): spread = lax.all_to_all(payload, CTX, 0, 0, tiled=True)]
    all_to_all x2 -> x1, waiting for transfers between devices: 24.4 us -> 11.1 us  [route(): spread = lax.all_to_all(payload, CTX, 0, 0, tiled=True)]
    all_to_all x2 -> x1, starting transfers between devices: 15.9 us -> 3.87 us  [route(): spread = lax.all_to_all(payload, CTX, 0, 0, tiled=True)]
    dot_general x6 -> x14, matrix products: 16.2 us -> 7.65 us  [the longest x12 7.11 us: mm(): return jnp.einsum(form, left, right, preferred_element_type=f32)]
    all_to_all x2, waiting for transfers between devices: 14.4 us -> 18.6 us  [route(): return lax.all_to_all(chosen.reshape(spread.shape), CTX, 0, 0, tiled=True)]
    slice x5 -> x1, local copies, waits for them, and re-layouts: 3.48 us -> 0.03 us  [per_device(): projected[:, :, 1].reshape(local_tokens, head_count * HD)]
    gather x2 -> x0, local copies, waits for them, and re-layouts: 2.84 us -> none  [route(): chosen = jnp.take(spread, order, axis=0)]
    select_n x4 -> x0, other arithmetic: 2.57 us -> none  [route(): chosen = jnp.take(spread, order, axis=0)]
  transfers between devices with their start and end apart: 13 -> 12, of which waited for: 11 -> 10; matrix products, arithmetic and copies ran while one was open for 13% -> 13% of each run, Pallas kernels for 0% -> 0%
where the time goes in v5:
time: 203 us; the launch traced here: 202 us
  waiting for transfers between devices  80.9 us (40%)
  starting transfers between devices  28.5 us (14%)
  blocking collectives  23.9 us (12%)
  matrix products  21.3 us (10%)
  local copies, waits for them, and re-layouts  16.3 us (8%)
  other arithmetic  16.1 us (8%)
  between operations  14.5 us (7%)
    reduce_scatter x1, waiting for transfers between devices, reduce_ctx(): part = lax.psum_scatter(part, 'z', scatter_dimension=0, tiled=True)  27.7 us
    all_to_all x1, blocking collectives, route(): spread = lax.all_to_all(payload, CTX, 0, 0, tiled=True)  23.9 us
    all_to_all x2, waiting for transfers between devices, route(): return lax.all_to_all(chosen.reshape(spread.shape), CTX, 0, 0, tiled=True)  18.6 us
    ppermute x3, waiting for transfers between devices, ring_rs(): got_a = lax.ppermute(acc_a, axis, cw)  12.1 us
    all_to_all x1, waiting for transfers between devices, route(): spread = lax.all_to_all(payload, CTX, 0, 0, tiled=True)  11.1 us
    all_to_all x2, starting transfers between devices, route(): return lax.all_to_all(chosen.reshape(spread.shape), CTX, 0, 0, tiled=True)  9.18 us
    all_to_all x1, waiting for transfers between devices, reduce_ctx(): gathered = lax.all_to_all(pieces, 'x', 0, 0, tiled=True)  7.99 us
    unnamed x38, local copies, waits for them, and re-layouts  7.22 us
  transfers between devices with their start and end apart: 12, of which 10 were waited for; matrix products, arithmetic and copies ran while one was open for 13% of the time, Pallas kernels for 0%

profile of v5, /device:TPU:8, one launch (start us, length us, event | category | flops | bytes accessed | tf_op | source)
XLA Modules:
  0.0 201.6 jit_solution(9579217780362562435)
XLA Ops:
  7.2 1.6 copy-done
  8.8 4.6 %convolution_convert_fusion.4 = bf16[256,768]{1,0:T(8,128)(2,1)S(1)} fusion(bf16[256,4096]{1,0:T(8,128)(2,1)S(1)} %copy-done, bf16[4096,768]{1,0:T(8,128)(2,1)} %param.6), kind=kOutput, calls=%fused_computation.8 | convolution fusion | flops 1610809344 | bytes 8781824 | tf_op jit(solution)/shard_map/dot_general | solution.py:100
  13.9 23.9 %all_to_all.25 = bf16[32,2,2,1,8,128]{5,4,2,3,1,0:T(8,128)(2,1)S(1)} all-to-all(bf16[32,2,2,1,8,128]{5,4,2,3,1,0:T(8,128)(2,1)S(1)} %copy.68), channel_id=1, replica_groups=mesh['z'=8,'x'=4,'y'=4,'c'=2] {'z','x'}, dimensions={0} | all-to-all | bytes 524288 | tf_op jit(solution)/shard_map/all_to_all | solution.py:35
  37.8 0.3 fusion.4
  38.1 0.7 copy.124
  38.9 4.6 %all-to-all-start.1 = ((bf16[32,2,2,1,8,128]{5,4,2,3,1,0:T(8,128)(2,1)}), bf16[32,2,2,1,8,128]{5,4,2,3,1,0:T(8,128)(2,1)}, u32[]{:S(2)}, u32[]{:S(2)}) async-start(bf16[32,2,2,1,8,128]{5,4,2,3,1,0:T(8,128)(2,1)} %bitcast.16), calls=%async_computation.1 | async-start | bytes 524288 | tf_op jit(solution)/shard_map/all_to_all | solution.py:40
  43.5 0.8 slice_bitcast_fusion.10
  44.3 1.0 copy.114
  45.5 1.0 fusion.20
  46.5 0.2 fusion.51
  46.8 1.2 fusion.3
  47.9 7.4 %all-to-all-done.1 = bf16[32,2,2,1,8,128]{5,4,2,3,1,0:T(8,128)(2,1)} async-done(((bf16[32,2,2,1,8,128]{5,4,2,3,1,0:T(8,128)(2,1)}), bf16[32,2,2,1,8,128]{5,4,2,3,1,0:T(8,128)(2,1)}, u32[]{:S(2)}, u32[]{:S(2)}) %all-to-all-start.1) | async-done | bytes 262176 | tf_op jit(solution)/shard_map/all_to_all | solution.py:40
  55.4 1.1 copy.140
  56.4 0.2 fusion.52
  56.9 0.3 multiply_reduce_fusion
  57.5 1.2 multiply_convert_fusion
  58.7 0.7 copy-done.4
  59.6 0.2 fusion.11
  59.9 0.7 copy_bitcast_fusion.1
  60.6 3.9 %all-to-all-start.2 = ((bf16[32,2,2,1,8,128]{5,4,2,1,3,0:T(8,128)(2,1)}), bf16[32,2,2,1,8,128]{5,4,2,1,3,0:T(8,128)(2,1)S(1)}, u32[]{:S(2)}, u32[]{:S(2)}) async-start(bf16[32,2,2,1,8,128]{5,4,2,1,3,0:T(8,128)(2,1)} %copy_bitcast_fusion.1), calls=%async_computation.2 | async-start | bytes 524288 | tf_op jit(solution)/shard_map/all_to_all | solution.py:35
  64.5 0.7 scatter_custom_fusion
  65.2 11.1 %all-to-all-done.2 = bf16[32,2,2,1,8,128]{5,4,2,1,3,0:T(8,128)(2,1)S(1)} async-done(((bf16[32,2,2,1,8,128]{5,4,2,1,3,0:T(8,128)(2,1)}), bf16[32,2,2,1,8,128]{5,4,2,1,3,0:T(8,128)(2,1)S(1)}, u32[]{:S(2)}, u32[]{:S(2)}) %all-to-all-start.2) | async-done | bytes 262176 | tf_op jit(solution)/shard_map/all_to_all | solution.py:35
  76.3 0.3 fusion.5
  76.6 0.7 copy.126
  77.3 4.6 %all-to-all-start.3 = ((bf16[32,2,2,1,8,128]{5,4,2,3,1,0:T(8,128)(2,1)}), bf16[32,2,2,1,8,128]{5,4,2,3,1,0:T(8,128)(2,1)}, u32[]{:S(2)}, u32[]{:S(2)}) async-start(bf16[32,2,2,1,8,128]{5,4,2,3,1,0:T(8,128)(2,1)} %bitcast.47), calls=%async_computation.3 | async-start | bytes 524288 | tf_op jit(solution)/shard_map/all_to_all | solution.py:40
  82.2 0.2 fusion.14
  82.5 11.1 %all-to-all-done.3 = bf16[32,2,2,1,8,128]{5,4,2,3,1,0:T(8,128)(2,1)} async-done(((bf16[32,2,2,1,8,128]{5,4,2,3,1,0:T(8,128)(2,1)}), bf16[32,2,2,1,8,128]{5,4,2,3,1,0:T(8,128)(2,1)}, u32[]{:S(2)}, u32[]{:S(2)}) %all-to-all-start.3) | async-done | bytes 262176 | tf_op jit(solution)/shard_map/all_to_all | solution.py:40
  93.6 1.0 copy.139
  94.6 0.7 fusion.32
  95.3 1.1 copy.89
  96.4 0.9 fusion.13
  97.7 1.0 maximum_bitcast_fusion
  98.7 4.5 %fusion = bf16[4096,768]{0,1:T(8,128)(2,1)} fusion(bf16[256,768]{0,1:T(8,128)(2,1)S(1)} %bitcast.253, bf16[256,4096]{1,0:T(8,128)(2,1)S(1)} %copy-done), kind=kOutput, calls=%fused_computation.2 | convolution fusion | flops 1613758464 | bytes 8781824 | tf_op jit(solution)/shard_map/dot_general | solution.py:81
  103.2 4.6 %convolution_convert_fusion.3 = bf16[256,4,2,512]{3,0,2,1:T(8,128)(2,1)S(1)} fusion(bf16[256,768,1,1]{0,1,3,2:T(8,128)(2,1)S(1)} %bitcast.254, bf16[4,2,512,768]{3,2,1,0:T(8,128)(2,1)} %bitcast.262), kind=kOutput, calls=%fused_computation.7 | convolution fusion | flops 1611661312 | bytes 8781824 | tf_op jit(solution)/shard_map/tk,ycwk->cytw/dot_general | solution.py:157
  107.8 1.3 copy-done.10
  109.2 0.3 collective-permute-start
  109.6 2.7 %collective-permute-done = bf16[4,256,512]{2,1,0:T(8,128)(2,1)} collective-permute-done((bf16[4,256,512]{2,1,0:T(8,128)(2,1)S(1)}, bf16[4,256,512]{2,1,0:T(8,128)(2,1)}, u32[]{:S(2)}, u32[]{:S(2)}) %collective-permute-start) | collective-permute-done | bytes 1048608 | tf_op jit(solution)/shard_map/ppermute | solution.py:60
  112.3 1.8 fusion.1
  114.1 0.7 dynamic-slice_bitcast_fusion.8
  114.8 1.6 collective-permute-start.1
  116.4 4.3 %collective-permute-done.1 = bf16[128,512]{1,0:T(8,128)(2,1)} collective-permute-done((bf16[128,512]{1,0:T(8,128)(2,1)}, bf16[128,512]{1,0:T(8,128)(2,1)}, u32[]{:S(2)}, u32[]{:S(2)}) %collective-permute-start.1) | collective-permute-done | bytes 131104 | tf_op jit(solution)/shard_map/ppermute | solution.py:73
  120.7 1.6 fusion.30
  122.3 1.6 collective-permute-start.2
  123.9 0.4 collective-permute-start.4
  124.3 3.3 %collective-permute-done.2 = bf16[128,512]{1,0:T(8,128)(2,1)} collective-permute-done((bf16[128,512]{1,0:T(8,128)(2,1)}, bf16[128,512]{1,0:T(8,128)(2,1)}, u32[]{:S(2)}, u32[]{:S(2)}) %collective-permute-start.2) | collective-permute-done | bytes 131104 | tf_op jit(solution)/shard_map/ppermute | solution.py:73
  127.6 1.6 fusion.29
  129.2 1.6 collective-permute-start.3
  130.7 4.6 %collective-permute-done.3 = bf16[128,512]{1,0:T(8,128)(2,1)} collective-permute-done((bf16[128,512]{1,0:T(8,128)(2,1)}, bf16[128,512]{1,0:T(8,128)(2,1)}, u32[]{:S(2)}, u32[]{:S(2)}) %collective-permute-start.3) | collective-permute-done | bytes 131104 | tf_op jit(solution)/shard_map/ppermute | solution.py:73
  135.3 1.7 fusion.28
  137.0 3.2 %collective-permute-start.5 = (bf16[128,512]{1,0:T(8,128)(2,1)S(1)}, bf16[128,512]{1,0:T(8,128)(2,1)S(1)}, u32[]{:S(2)}, u32[]{:S(2)}) collective-permute-start(bf16[128,512]{1,0:T(8,128)(2,1)S(1)} %get-tuple-element.17), channel_id=1, source_target_pairs={{0,6},{2,0},{4,2},{6,4},{1,7},{3,1},{5,3},{7,5},{8,14},{10,8},{12,... | collective-permute-start | bytes 393224 | tf_op jit(solution)/shard_map/ppermute | solution.py:74
  140.3 1.9 fusion.42
  142.2 0.6 collective-permute-done.5
  142.8 0.7 fusion.26
  143.5 2.4 %collective-permute-start.6 = (bf16[128,512]{1,0:T(8,128)(2,1)}, bf16[128,512]{1,0:T(8,128)(2,1)}, u32[]{:S(2)}, u32[]{:S(2)}) collective-permute-start(bf16[128,512]{1,0:T(8,128)(2,1)} %fusion.26), channel_id=1, source_target_pairs={{0,6},{2,0},{4,2},{6,4},{1,7},{3,1},{5,3},{7,5},{8,14},{10,8},{12,... | collective-permute-start | bytes 393224 | tf_op jit(solution)/shard_map/ppermute | solution.py:74
  145.9 27.7 %reduce-scatter.2.cloned.1.call-done = bf16[512,768]{0,1:T(8,128)(2,1)} async-done(((bf16[4096,768]{0,1:T(8,128)(2,1)}), bf16[512,768]{0,1:T(8,128)(2,1)}) %reduce-scatter.2.cloned.1.call-update) | async-done | bytes 786448 | tf_op jit(solution)/shard_map/reduce_scatter | solution.py:87
  173.7 2.2 %copy_bitcast_fusion = bf16[4,128,768]{1,2,0:T(8,128)(2,1)} fusion(bf16[512,768]{0,1:T(8,128)(2,1)} %reduce-scatter.2.cloned.1.call-done), kind=kLoop, calls=%fused_computation.33 | loop fusion | bytes 1572864 | tf_op jit(solution)/shard_map/reshape | solution.py:89
  175.8 4.2 %all-to-all-start.4 = ((bf16[4,128,768]{1,2,0:T(8,128)(2,1)}), bf16[4,128,768]{1,2,0:T(8,128)(2,1)}, u32[]{:S(2)}, u32[]{:S(2)}) async-start(bf16[4,128,768]{1,2,0:T(8,128)(2,1)} %copy_bitcast_fusion), calls=%async_computation.5 | async-start | bytes 1572864 | tf_op jit(solution)/shard_map/all_to_all | solution.py:90
  180.0 1.2 fusion.9
  181.3 0.8 copy.97
  182.0 0.9 fusion.25
  183.0 1.6 pad_maximum_fusion.1
  184.6 8.0 %all-to-all-done.4 = bf16[4,128,768]{1,2,0:T(8,128)(2,1)} async-done(((bf16[4,128,768]{1,2,0:T(8,128)(2,1)}), bf16[4,128,768]{1,2,0:T(8,128)(2,1)}, u32[]{:S(2)}, u32[]{:S(2)}) %all-to-all-start.4) | async-done | bytes 786464 | tf_op jit(solution)/shard_map/all_to_all | solution.py:90
  192.6 1.3 reduce_sum.52
  193.9 0.8 copy.98
  (54 shorter events, 2.1 us)
Async XLA Ops:
  7.2 1.6 copy-start
  13.3 24.5 %copy-start.15 = (s32[1,32]{1,0:T(1,128)S(1)}, s32[1,32]{1,0:T(1,128)}, u32[]{:S(2)}) copy-start(s32[1,32]{1,0:T(1,128)} %param.7) | copy-start | bytes 388
  13.5 25.3 %copy-start.1 = (bf16[256,768]{0,1:T(8,128)(2,1)}, bf16[256,768]{0,1:T(8,128)(2,1)S(1)}, u32[]{:S(2)}) copy-start(bf16[256,768]{0,1:T(8,128)(2,1)S(1)} %copy.63) | copy-start | bytes 1179652
  38.9 16.5 %all-to-all-start.1 = ((bf16[32,2,2,1,8,128]{5,4,2,3,1,0:T(8,128)(2,1)}), bf16[32,2,2,1,8,128]{5,4,2,3,1,0:T(8,128)(2,1)}, u32[]{:S(2)}, u32[]{:S(2)}) async-start(bf16[32,2,2,1,8,128]{5,4,2,3,1,0:T(8,128)(2,1)} %bitcast.16), calls=%async_computation.1 | async-start | bytes 524288 | tf_op jit(solution)/shard_map/all_to_all | solution.py:40
  44.2 2.5 %copy-start.11 = (s32[2,256,16]{1,2,0:T(8,128)}, s32[2,256,16]{1,2,0:T(8,128)S(1)}, u32[]{:S(2)}) copy-start(s32[2,256,16]{1,2,0:T(8,128)S(1)} %get-tuple-element.29) | copy-start | bytes 98308
  44.2 2.5 %copy-start.13 = (s32[2,256,16]{1,2,0:T(8,128)}, s32[2,256,16]{1,2,0:T(8,128)S(1)}, u32[]{:S(2)}) copy-start(s32[2,256,16]{1,2,0:T(8,128)S(1)} %get-tuple-element.30) | copy-start | bytes 98308
  55.4 1.5 copy-start.9
  56.4 0.8 copy-start.7
  56.7 0.8 copy-start.12
  56.7 0.8 copy-start.14
  58.7 0.7 copy-start.4
  58.7 0.9 copy-start.6
  58.7 23.3 %copy-start.3 = (bf16[2,256,256]{1,2,0:T(8,128)(2,1)S(1)}, bf16[2,256,256]{1,2,0:T(8,128)(2,1)}, u32[]{:S(2)}) copy-start(bf16[2,256,256]{1,2,0:T(8,128)(2,1)} %get-tuple-element.32) | copy-start | bytes 786436
  59.4 22.8 %copy-start.8 = (bf16[32,2,2,1,8,128]{5,4,0,2,3,1:T(8,128)(2,1)S(1)}, bf16[32,2,2,1,8,128]{5,4,0,2,3,1:T(8,128)(2,1)}, u32[]{:S(2)}) copy-start(bf16[32,2,2,1,8,128]{5,4,0,2,3,1:T(8,128)(2,1)} %copy-done.7) | copy-start | bytes 786436
  59.6 22.6 %copy-start.5 = (bf16[2,256,256]{1,2,0:T(8,128)(2,1)S(1)}, bf16[2,256,256]{1,2,0:T(8,128)(2,1)}, u32[]{:S(2)}) copy-start(bf16[2,256,256]{1,2,0:T(8,128)(2,1)} %copy-done.4) | copy-start | bytes 786436
  60.6 15.7 %all-to-all-start.2 = ((bf16[32,2,2,1,8,128]{5,4,2,1,3,0:T(8,128)(2,1)}), bf16[32,2,2,1,8,128]{5,4,2,1,3,0:T(8,128)(2,1)S(1)}, u32[]{:S(2)}, u32[]{:S(2)}) async-start(bf16[32,2,2,1,8,128]{5,4,2,1,3,0:T(8,128)(2,1)} %copy_bitcast_fusion.1), calls=%async_computation.2 | async-start | bytes 524288 | tf_op jit(solution)/shard_map/all_to_all | solution.py:35
  77.3 16.3 %all-to-all-start.3 = ((bf16[32,2,2,1,8,128]{5,4,2,3,1,0:T(8,128)(2,1)}), bf16[32,2,2,1,8,128]{5,4,2,3,1,0:T(8,128)(2,1)}, u32[]{:S(2)}, u32[]{:S(2)}) async-start(bf16[32,2,2,1,8,128]{5,4,2,3,1,0:T(8,128)(2,1)} %bitcast.47), calls=%async_computation.3 | async-start | bytes 524288 | tf_op jit(solution)/shard_map/all_to_all | solution.py:40
  81.9 91.8 %reduce-scatter.2.cloned.1.call-start = ((), (), s32[]{:S(2)}) async-start(), calls=%async_computation.6 | async-start | bytes 7077888 | tf_op jit(solution)/shard_map/reduce_scatter | solution.py:87
  82.2 15.2 %copy-start.2 = (bf16[2,256,256]{1,2,0:T(8,128)(2,1)S(1)}, bf16[2,256,256]{1,2,0:T(8,128)(2,1)}, u32[]{:S(2)}) copy-start(bf16[2,256,256]{1,2,0:T(8,128)(2,1)} %get-tuple-element.31) | copy-start | bytes 786436
  107.8 1.4 copy-start.10
  109.2 3.1 %collective-permute-start = (bf16[4,256,512]{2,1,0:T(8,128)(2,1)S(1)}, bf16[4,256,512]{2,1,0:T(8,128)(2,1)}, u32[]{:S(2)}, u32[]{:S(2)}) collective-permute-start(bf16[4,256,512]{2,1,0:T(8,128)(2,1)S(1)} %dynamic-slice_bitcast_fusion), channel_id=1, source_target_pairs={{0,1},{1,0},{2,3},{3,2},{4,5},{5,4},{6,7},{7,6},{8,9},{9,8},{10,11... | collective-permute-start | bytes 3145736 | tf_op jit(solution)/shard_map/ppermute | solution.py:60
  114.8 5.9 %collective-permute-start.1 = (bf16[128,512]{1,0:T(8,128)(2,1)}, bf16[128,512]{1,0:T(8,128)(2,1)}, u32[]{:S(2)}, u32[]{:S(2)}) collective-permute-start(bf16[128,512]{1,0:T(8,128)(2,1)} %get-tuple-element.18), channel_id=1, source_target_pairs={{0,2},{2,4},{4,6},{6,0},{1,3},{3,5},{5,7},{7,1},{8,10},{10,12},{12... | collective-permute-start | bytes 393224 | tf_op jit(solution)/shard_map/ppermute | solution.py:73
  122.3 5.3 %collective-permute-start.2 = (bf16[128,512]{1,0:T(8,128)(2,1)}, bf16[128,512]{1,0:T(8,128)(2,1)}, u32[]{:S(2)}, u32[]{:S(2)}) collective-permute-start(bf16[128,512]{1,0:T(8,128)(2,1)} %fusion.30), channel_id=1, source_target_pairs={{0,2},{2,4},{4,6},{6,0},{1,3},{3,5},{5,7},{7,1},{8,10},{10,12},{12... | collective-permute-start | bytes 393224 | tf_op jit(solution)/shard_map/ppermute | solution.py:73
  123.9 6.9 %collective-permute-start.4 = (bf16[128,512]{1,0:T(8,128)(2,1)S(1)}, bf16[128,512]{1,0:T(8,128)(2,1)}, u32[]{:S(2)}, u32[]{:S(2)}) collective-permute-start(bf16[128,512]{1,0:T(8,128)(2,1)S(1)} %get-tuple-element.19), channel_id=1, source_target_pairs={{0,6},{2,0},{4,2},{6,4},{1,7},{3,1},{5,3},{7,5},{8,14},{10,8},{12,... | collective-permute-start | bytes 393224 | tf_op jit(solution)/shard_map/ppermute | solution.py:74
  129.2 6.2 %collective-permute-start.3 = (bf16[128,512]{1,0:T(8,128)(2,1)}, bf16[128,512]{1,0:T(8,128)(2,1)}, u32[]{:S(2)}, u32[]{:S(2)}) collective-permute-start(bf16[128,512]{1,0:T(8,128)(2,1)} %fusion.29), channel_id=1, source_target_pairs={{0,2},{2,4},{4,6},{6,0},{1,3},{3,5},{5,7},{7,1},{8,10},{10,12},{12... | collective-permute-start | bytes 393224 | tf_op jit(solution)/shard_map/ppermute | solution.py:73
  137.0 5.8 %collective-permute-start.5 = (bf16[128,512]{1,0:T(8,128)(2,1)S(1)}, bf16[128,512]{1,0:T(8,128)(2,1)S(1)}, u32[]{:S(2)}, u32[]{:S(2)}) collective-permute-start(bf16[128,512]{1,0:T(8,128)(2,1)S(1)} %get-tuple-element.17), channel_id=1, source_target_pairs={{0,6},{2,0},{4,2},{6,4},{1,7},{3,1},{5,3},{7,5},{8,14},{10,8},{12,... | collective-permute-start | bytes 393224 | tf_op jit(solution)/shard_map/ppermute | solution.py:74
  143.5 38.5 %collective-permute-start.6 = (bf16[128,512]{1,0:T(8,128)(2,1)}, bf16[128,512]{1,0:T(8,128)(2,1)}, u32[]{:S(2)}, u32[]{:S(2)}) collective-permute-start(bf16[128,512]{1,0:T(8,128)(2,1)} %fusion.26), channel_id=1, source_target_pairs={{0,6},{2,0},{4,2},{6,4},{1,7},{3,1},{5,3},{7,5},{8,14},{10,8},{12,... | collective-permute-start | bytes 393224 | tf_op jit(solution)/shard_map/ppermute | solution.py:74
  175.8 16.8 %all-to-all-start.4 = ((bf16[4,128,768]{1,2,0:T(8,128)(2,1)}), bf16[4,128,768]{1,2,0:T(8,128)(2,1)}, u32[]{:S(2)}, u32[]{:S(2)}) async-start(bf16[4,128,768]{1,2,0:T(8,128)(2,1)} %copy_bitcast_fusion), calls=%async_computation.5 | async-start | bytes 1572864 | tf_op jit(solution)/shard_map/all_to_all | solution.py:90
Sparse Core Ops, SparseCore 0:
  103.3 70.3 reduce-scatter.1

commit v6 on v5

--- a/solution.py
+++ b/solution.py
@@ -150,7 +150,15 @@
     grad_value = (grad_value_own + returned[1].astype(f32)).astype(jnp.bfloat16)
     stacked = jnp.stack([grad_query, grad_key, grad_value], 3)
     grad_qkv = stacked.transpose(1, 2, 0, 3, 4).reshape(local_tokens, head_count * 3 * HD)
-    weight_grad = reduce_ctx(weight_term(activations, grad_qkv))
+    query_cols = grad_query.transpose(1, 2, 0, 3).reshape(local_tokens, head_count * HD)
+    kv_cols = jnp.stack([grad_key, grad_value], 3).transpose(1, 2, 0, 3, 4)
+    kv_cols = kv_cols.reshape(local_tokens, head_count * 2 * HD)
+    weight_q = reduce_ctx(weight_term(activations, query_cols))
+    weight_kv = reduce_ctx(weight_term(activations, kv_cols))
+    rows = weight_q.shape[0]
+    weight_grad = jnp.concatenate(
+        [weight_q.reshape(rows, head_count, 1, HD), weight_kv.reshape(rows, head_count, 2, HD)], 2
+    ).reshape(rows, head_count * 3 * HD)
     n_y = lax.psum(1, "y")
     width = activations.shape[1] // (2 * n_y)
     w_split = w_qkv.reshape(n_y, 2, width, w_qkv.shape[1])

time: 203 us -> 189 us (0.931)
  waiting for transfers between devices: 80.9 us -> 45.3 us
  blocking collectives: 23.9 us -> 41.5 us
  matrix products: 21.3 us -> 23.8 us
  local copies, waits for them, and re-layouts: 16.3 us -> 18.6 us
    reduce_scatter x1 -> x2, waiting for transfers between devices: 27.7 us -> 4.31 us  [reduce_ctx(): part = lax.psum_scatter(part, 'z', scatter_dimension=0, tiled=True)]
    all_to_all x0 -> x1, blocking collectives: none -> 17.6 us  [route(): return lax.all_to_all(chosen.reshape(spread.shape), CTX, 0, 0, tiled=True)]
    all_to_all x2 -> x1, waiting for transfers between devices: 18.6 us -> 7.4 us  [route(): return lax.all_to_all(chosen.reshape(spread.shape), CTX, 0, 0, tiled=True)]
    all_to_all x2 -> x1, starting transfers between devices: 9.18 us -> 4.59 us  [route(): return lax.all_to_all(chosen.reshape(spread.shape), CTX, 0, 0, tiled=True)]
    all_to_all x1 -> x2, starting transfers between devices: 4.23 us -> 8.17 us  [reduce_ctx(): gathered = lax.all_to_all(pieces, 'x', 0, 0, tiled=True)]
    all_to_all x1 -> x2, waiting for transfers between devices: 7.99 us -> 4.22 us  [reduce_ctx(): gathered = lax.all_to_all(pieces, 'x', 0, 0, tiled=True)]
    all_to_all x1, waiting for transfers between devices: 11.1 us -> 13.2 us  [route(): spread = lax.all_to_all(payload, CTX, 0, 0, tiled=True)]
    unnamed x38 -> x36, local copies, waits for them, and re-layouts: 7.22 us -> 6.11 us
  transfers between devices with their start and end apart: 12 -> 13, of which waited for: 10 -> 10; matrix products, arithmetic and copies ran while one was open for 13% -> 22% of each run, Pallas kernels for 0% -> 0%
where the time goes in v6:
time: 189 us; the launch traced here: 187 us
  waiting for transfers between devices  45.3 us (24%)
  blocking collectives  41.5 us (22%)
  starting transfers between devices  27.5 us (15%)
  matrix products  23.8 us (13%)
  local copies, waits for them, and re-layouts  18.6 us (10%)
  other arithmetic  16.2 us (9%)
  between operations  14.5 us (8%)
    all_to_all x1, blocking collectives, route(): spread = lax.all_to_all(payload, CTX, 0, 0, tiled=True)  23.9 us
    all_to_all x1, blocking collectives, route(): return lax.all_to_all(chosen.reshape(spread.shape), CTX, 0, 0, tiled=True)  17.6 us
    all_to_all x1, waiting for transfers between devices, route(): spread = lax.all_to_all(payload, CTX, 0, 0, tiled=True)  13.2 us
    ppermute x3, waiting for transfers between devices, ring_rs(): got_a = lax.ppermute(acc_a, axis, cw)  12.7 us
    all_to_all x2, starting transfers between devices, reduce_ctx(): gathered = lax.all_to_all(pieces, 'x', 0, 0, tiled=True)  8.17 us
    dot_general x12, matrix products, mm(): return jnp.einsum(form, left, right, preferred_element_type=f32)  7.42 us
    all_to_all x1, waiting for transfers between devices, route(): return lax.all_to_all(chosen.reshape(spread.shape), CTX, 0, 0, tiled=True)  7.4 us
    ppermute x3, starting transfers between devices, ring_rs(): got_b = lax.ppermute(acc_b, axis, ccw)  6.32 us
  transfers between devices with their start and end apart: 13, of which 10 were waited for; matrix products, arithmetic and copies ran while one was open for 22% of the time, Pallas kernels for 0%

profile of v6, /device:TPU:8, one launch (start us, length us, event | category | flops | bytes accessed | tf_op | source)
XLA Modules:
  0.0 187.4 jit_solution(17853681484765922203)
XLA Ops:
  7.2 1.6 copy-done
  8.8 4.6 %convolution_convert_fusion.5 = bf16[256,768]{1,0:T(8,128)(2,1)S(1)} fusion(bf16[256,4096]{1,0:T(8,128)(2,1)S(1)} %copy-done, bf16[4096,768]{1,0:T(8,128)(2,1)} %param.6), kind=kOutput, calls=%fused_computation.10 | convolution fusion | flops 1610809344 | bytes 8781824 | tf_op jit(solution)/shard_map/dot_general | solution.py:100
  13.9 23.9 %all_to_all.30 = bf16[32,2,2,1,8,128]{5,4,2,3,1,0:T(8,128)(2,1)S(1)} all-to-all(bf16[32,2,2,1,8,128]{5,4,2,3,1,0:T(8,128)(2,1)S(1)} %copy.71), channel_id=1, replica_groups=mesh['z'=8,'x'=4,'y'=4,'c'=2] {'z','x'}, dimensions={0} | all-to-all | bytes 524288 | tf_op jit(solution)/shard_map/all_to_all | solution.py:35
  37.8 0.3 fusion.5
  38.1 0.7 copy.129
  38.9 4.6 %all-to-all-start.1 = ((bf16[32,2,2,1,8,128]{5,4,2,3,1,0:T(8,128)(2,1)}), bf16[32,2,2,1,8,128]{5,4,2,3,1,0:T(8,128)(2,1)}, u32[]{:S(2)}, u32[]{:S(2)}) async-start(bf16[32,2,2,1,8,128]{5,4,2,3,1,0:T(8,128)(2,1)} %bitcast.16), calls=%async_computation.1 | async-start | bytes 524288 | tf_op jit(solution)/shard_map/all_to_all | solution.py:40
  43.5 0.8 slice_bitcast_fusion.10
  44.4 1.0 copy.119
  45.5 1.0 fusion.20
  46.8 1.2 fusion.4
  48.0 7.4 %all-to-all-done.1 = bf16[32,2,2,1,8,128]{5,4,2,3,1,0:T(8,128)(2,1)} async-done(((bf16[32,2,2,1,8,128]{5,4,2,3,1,0:T(8,128)(2,1)}), bf16[32,2,2,1,8,128]{5,4,2,3,1,0:T(8,128)(2,1)}, u32[]{:S(2)}, u32[]{:S(2)}) %all-to-all-start.1) | async-done | bytes 262176 | tf_op jit(solution)/shard_map/all_to_all | solution.py:40
  55.4 1.1 copy.146
  56.4 0.2 fusion.52
  56.9 0.3 multiply_reduce_fusion
  57.5 1.2 multiply_convert_fusion
  58.7 0.7 copy-done.3
  59.9 2.1 %fusion.1 = bf16[4096,256]{0,1:T(8,128)(2,1)} fusion(bf16[256,256]{0,1:T(8,128)(2,1)S(1)} %bitcast.274, bf16[256,4096]{1,0:T(8,128)(2,1)S(1)} %copy-done), kind=kOutput, calls=%fused_computation.4 | convolution fusion | flops 537919488 | bytes 4325376 | tf_op jit(solution)/shard_map/dot_general | solution.py:81
  62.0 0.9 copy-done.6
  63.4 0.8 copy_bitcast_fusion.2
  64.1 3.9 %all-to-all-start.2 = ((bf16[32,2,2,1,8,128]{5,4,2,1,3,0:T(8,128)(2,1)}), bf16[32,2,2,1,8,128]{5,4,2,1,3,0:T(8,128)(2,1)S(1)}, u32[]{:S(2)}, u32[]{:S(2)}) async-start(bf16[32,2,2,1,8,128]{5,4,2,1,3,0:T(8,128)(2,1)} %copy_bitcast_fusion.2), calls=%async_computation.2 | async-start | bytes 524288 | tf_op jit(solution)/shard_map/all_to_all | solution.py:35
  68.1 0.7 scatter_custom_fusion
  68.8 13.2 %all-to-all-done.2 = bf16[32,2,2,1,8,128]{5,4,2,1,3,0:T(8,128)(2,1)S(1)} async-done(((bf16[32,2,2,1,8,128]{5,4,2,1,3,0:T(8,128)(2,1)}), bf16[32,2,2,1,8,128]{5,4,2,1,3,0:T(8,128)(2,1)S(1)}, u32[]{:S(2)}, u32[]{:S(2)}) %all-to-all-start.2) | async-done | bytes 262176 | tf_op jit(solution)/shard_map/all_to_all | solution.py:35
  82.0 0.3 fusion.6
  82.3 17.6 %all_to_all.31 = bf16[32,2,2,1,8,128]{5,4,2,3,1,0:T(8,128)(2,1)S(1)} all-to-all(bf16[32,2,2,1,8,128]{5,4,2,3,1,0:T(8,128)(2,1)S(1)} %bitcast.280), channel_id=1, replica_groups=mesh['z'=8,'x'=4,'y'=4,'c'=2] {'z','x'}, dimensions={0} | all-to-all | bytes 524288 | tf_op jit(solution)/shard_map/all_to_all | solution.py:40
  100.0 0.8 fusion.32
  100.8 1.8 copy.92
  102.6 1.1 copy.94
  103.7 1.2 fusion.14
  105.2 3.2 %fusion = bf16[4096,512]{0,1:T(8,128)(2,1)} fusion(bf16[256,512]{0,1:T(8,128)(2,1)S(1)} %bitcast.277, bf16[256,4096]{1,0:T(8,128)(2,1)S(1)} %copy-done), kind=kOutput, calls=%fused_computation.2 | convolution fusion | flops 1075838976 | bytes 6553600 | tf_op jit(solution)/shard_map/dot_general | solution.py:81
  108.5 6.0 %convolution_convert_fusion.4 = bf16[256,4,2,512]{3,0,2,1:T(8,128)(2,1)} fusion(bf16[256,768,1,1]{0,1,3,2:T(8,128)(2,1)S(1)} %bitcast.285, bf16[4,2,512,768]{3,2,1,0:T(8,128)(2,1)} %bitcast.289), kind=kOutput, calls=%fused_computation.9 | convolution fusion | flops 1611661312 | bytes 8781824 | tf_op jit(solution)/shard_map/tk,ycwk->cytw/dot_general | solution.py:165
  114.5 1.3 dynamic-slice_bitcast_fusion
  115.8 0.3 collective-permute-start
  116.1 2.7 %collective-permute-done = bf16[4,256,512]{2,1,0:T(8,128)(2,1)} collective-permute-done((bf16[4,256,512]{2,1,0:T(8,128)(2,1)S(1)}, bf16[4,256,512]{2,1,0:T(8,128)(2,1)}, u32[]{:S(2)}, u32[]{:S(2)}) %collective-permute-start) | collective-permute-done | bytes 1048608 | tf_op jit(solution)/shard_map/ppermute | solution.py:60
  118.8 1.9 %fusion.2 = bf16[4,256,512]{2,1,0:T(8,128)(2,1)S(1)} fusion(bf16[4,256,512]{2,1,0:T(8,128)(2,1)} %collective-permute-done, bf16[256,4,2,512]{3,0,2,1:T(8,128)(2,1)} %convolution_convert_fusion.4, s32[]{:T(128)S(6)} %select_n.71), kind=kLoop, calls=%fused_computation.8 | loop fusion | flops 2097152 | bytes 3145732 | tf_op jit(solution)/shard_map/convert_element_type | solution.py:61
  120.7 0.7 dynamic-slice_bitcast_fusion.8
  121.4 1.4 collective-permute-start.1
  122.8 4.5 %collective-permute-done.1 = bf16[128,512]{1,0:T(8,128)(2,1)} collective-permute-done((bf16[128,512]{1,0:T(8,128)(2,1)}, bf16[128,512]{1,0:T(8,128)(2,1)}, u32[]{:S(2)}, u32[]{:S(2)}) %collective-permute-start.1) | collective-permute-done | bytes 131104 | tf_op jit(solution)/shard_map/ppermute | solution.py:73
  127.3 1.6 fusion.30
  128.9 1.4 collective-permute-start.2
  130.2 0.6 collective-permute-start.4
  130.9 3.3 %collective-permute-done.2 = bf16[128,512]{1,0:T(8,128)(2,1)} collective-permute-done((bf16[128,512]{1,0:T(8,128)(2,1)}, bf16[128,512]{1,0:T(8,128)(2,1)}, u32[]{:S(2)}, u32[]{:S(2)}) %collective-permute-start.2) | collective-permute-done | bytes 131104 | tf_op jit(solution)/shard_map/ppermute | solution.py:73
  134.1 1.6 fusion.29
  135.7 1.4 collective-permute-start.3
  137.1 5.0 %collective-permute-done.3 = bf16[128,512]{1,0:T(8,128)(2,1)} collective-permute-done((bf16[128,512]{1,0:T(8,128)(2,1)}, bf16[128,512]{1,0:T(8,128)(2,1)}, u32[]{:S(2)}, u32[]{:S(2)}) %collective-permute-start.3) | collective-permute-done | bytes 131104 | tf_op jit(solution)/shard_map/ppermute | solution.py:73
  142.1 1.7 fusion.28
  143.8 3.2 %collective-permute-start.5 = (bf16[128,512]{1,0:T(8,128)(2,1)S(1)}, bf16[128,512]{1,0:T(8,128)(2,1)S(1)}, u32[]{:S(2)}, u32[]{:S(2)}) collective-permute-start(bf16[128,512]{1,0:T(8,128)(2,1)S(1)} %get-tuple-element.17), channel_id=1, source_target_pairs={{0,6},{2,0},{4,2},{6,4},{1,7},{3,1},{5,3},{7,5},{8,14},{10,8},{12,... | collective-permute-start | bytes 393224 | tf_op jit(solution)/shard_map/ppermute | solution.py:74
  147.0 1.9 %fusion.42 = f32[2,256,128]{1,2,0:T(8,128)} fusion(bf16[2,256,256]{1,2,0:T(8,128)(2,1)} %get-tuple-element.23, bf16[2,2,1,32,8,128]{5,4,3,1,2,0:T(8,128)(2,1)} %bitcast.272), kind=kOutput, calls=%fused_computation.102 | convolution fusion | flops 33554432 | bytes 655360 | tf_op jit(solution)/shard_map/hnqk,hnkd->hnqd/dot_general | solution.py:112
  149.0 0.6 collective-permute-done.5
  149.6 0.7 fusion.26
  150.3 2.4 %collective-permute-start.6 = (bf16[128,512]{1,0:T(8,128)(2,1)}, bf16[128,512]{1,0:T(8,128)(2,1)}, u32[]{:S(2)}, u32[]{:S(2)}) collective-permute-start(bf16[128,512]{1,0:T(8,128)(2,1)} %fusion.26), channel_id=1, source_target_pairs={{0,6},{2,0},{4,2},{6,4},{1,7},{3,1},{5,3},{7,5},{8,14},{10,8},{12,... | collective-permute-start | bytes 393224 | tf_op jit(solution)/shard_map/ppermute | solution.py:74
  152.7 1.7 copy_bitcast_fusion.1
  154.4 4.0 %all-to-all-start.4 = ((bf16[4,128,256]{1,2,0:T(8,128)(2,1)}), bf16[4,128,256]{1,2,0:T(8,128)(2,1)}, u32[]{:S(2)}, u32[]{:S(2)}) async-start(bf16[4,128,256]{1,2,0:T(8,128)(2,1)} %copy_bitcast_fusion.1), calls=%async_computation.5 | async-start | bytes 524288 | tf_op jit(solution)/shard_map/all_to_all | solution.py:90
  158.4 4.3 %reduce-scatter.5.cloned.1.call-done = bf16[512,512]{0,1:T(8,128)(2,1)} async-done(((bf16[4096,512]{0,1:T(8,128)(2,1)}), bf16[512,512]{0,1:T(8,128)(2,1)}) %reduce-scatter.5.cloned.1.call-update) | async-done | bytes 524304 | tf_op jit(solution)/shard_map/reduce_scatter | solution.py:87
  162.8 1.9 %copy_bitcast_fusion = bf16[4,128,512]{1,2,0:T(8,128)(2,1)} fusion(bf16[512,512]{0,1:T(8,128)(2,1)} %reduce-scatter.5.cloned.1.call-done), kind=kLoop, calls=%fused_computation.34 | loop fusion | bytes 1048576 | tf_op jit(solution)/shard_map/reshape | solution.py:89
  164.7 0.5 all-to-all-done.4
  165.2 4.1 %all-to-all-start.5 = ((bf16[4,128,512]{1,2,0:T(8,128)(2,1)}), bf16[4,128,512]{1,2,0:T(8,128)(2,1)}, u32[]{:S(2)}, u32[]{:S(2)}) async-start(bf16[4,128,512]{1,2,0:T(8,128)(2,1)} %copy_bitcast_fusion), calls=%async_computation.7 | async-start | bytes 1048576 | tf_op jit(solution)/shard_map/all_to_all | solution.py:90
  169.3 1.2 fusion.10
  170.6 0.8 copy.102
  171.3 0.9 fusion.25
  172.3 1.6 pad_maximum_fusion.1
  173.9 1.0 reduce_sum.64
  174.9 3.7 %all-to-all-done.5 = bf16[4,128,512]{1,2,0:T(8,128)(2,1)} async-done(((bf16[4,128,512]{1,2,0:T(8,128)(2,1)}), bf16[4,128,512]{1,2,0:T(8,128)(2,1)}, u32[]{:S(2)}, u32[]{:S(2)}) %all-to-all-start.5) | async-done | bytes 524320 | tf_op jit(solution)/shard_map/all_to_all | solution.py:90
  178.6 1.1 reduce_sum.65
  179.7 0.8 copy.103
  (62 shorter events, 2.9 us)
Async XLA Ops:
  7.2 1.6 copy-start
  13.3 24.5 %copy-start.14 = (s32[1,32]{1,0:T(1,128)S(1)}, s32[1,32]{1,0:T(1,128)}, u32[]{:S(2)}) copy-start(s32[1,32]{1,0:T(1,128)} %param.7) | copy-start | bytes 388
  13.5 25.3 %copy-start.1 = (bf16[256,768]{0,1:T(8,128)(2,1)}, bf16[256,768]{0,1:T(8,128)(2,1)S(1)}, u32[]{:S(2)}) copy-start(bf16[256,768]{0,1:T(8,128)(2,1)S(1)} %copy.66) | copy-start | bytes 1179652
  38.9 16.5 %all-to-all-start.1 = ((bf16[32,2,2,1,8,128]{5,4,2,3,1,0:T(8,128)(2,1)}), bf16[32,2,2,1,8,128]{5,4,2,3,1,0:T(8,128)(2,1)}, u32[]{:S(2)}, u32[]{:S(2)}) async-start(bf16[32,2,2,1,8,128]{5,4,2,3,1,0:T(8,128)(2,1)} %bitcast.16), calls=%async_computation.1 | async-start | bytes 524288 | tf_op jit(solution)/shard_map/all_to_all | solution.py:40
  43.5 109.2 %reduce-scatter.3.cloned.1.call-start = ((), (), s32[]{:S(2)}) async-start(), calls=%async_computation.8 | async-start | bytes 2359296 | tf_op jit(solution)/shard_map/reduce_scatter | solution.py:87
  44.3 2.5 %copy-start.10 = (s32[2,256,16]{1,2,0:T(8,128)}, s32[2,256,16]{1,2,0:T(8,128)S(1)}, u32[]{:S(2)}) copy-start(s32[2,256,16]{1,2,0:T(8,128)S(1)} %get-tuple-element.29) | copy-start | bytes 98308
  44.3 2.5 %copy-start.12 = (s32[2,256,16]{1,2,0:T(8,128)}, s32[2,256,16]{1,2,0:T(8,128)S(1)}, u32[]{:S(2)}) copy-start(s32[2,256,16]{1,2,0:T(8,128)S(1)} %get-tuple-element.30) | copy-start | bytes 98308
  55.4 1.5 copy-start.9
  56.4 3.5 %copy-start.8 = (bf16[32,2,2,1,8,128]{5,4,0,2,3,1:T(8,128)(2,1)}, bf16[32,2,2,1,8,128]{5,4,0,2,3,1:T(8,128)(2,1)S(1)}, u32[]{:S(2)}) copy-start(bf16[32,2,2,1,8,128]{5,4,0,2,3,1:T(8,128)(2,1)S(1)} %copy.146) | copy-start | bytes 786436
  56.7 0.8 copy-start.11
  56.7 0.8 copy-start.13
  58.7 0.7 copy-start.3
  58.7 0.9 copy-start.5
  62.0 0.9 copy-start.6
  62.0 1.2 copy-start.7
  64.1 17.9 %all-to-all-start.2 = ((bf16[32,2,2,1,8,128]{5,4,2,1,3,0:T(8,128)(2,1)}), bf16[32,2,2,1,8,128]{5,4,2,1,3,0:T(8,128)(2,1)S(1)}, u32[]{:S(2)}, u32[]{:S(2)}) async-start(bf16[32,2,2,1,8,128]{5,4,2,1,3,0:T(8,128)(2,1)} %copy_bitcast_fusion.2), calls=%async_computation.2 | async-start | bytes 524288 | tf_op jit(solution)/shard_map/all_to_all | solution.py:35
  68.0 35.7 %copy-start.4 = (bf16[2,256,256]{1,2,0:T(8,128)(2,1)S(1)}, bf16[2,256,256]{1,2,0:T(8,128)(2,1)}, u32[]{:S(2)}) copy-start(bf16[2,256,256]{1,2,0:T(8,128)(2,1)} %copy-done.3) | copy-start | bytes 786436
  68.0 94.7 %reduce-scatter.5.cloned.1.call-start = ((), (), s32[]{:S(2)}) async-start(), calls=%async_computation.9 | async-start | bytes 4718592 | tf_op jit(solution)/shard_map/reduce_scatter | solution.py:87
  82.3 22.6 %copy-start.2 = (bf16[2,256,256]{1,2,0:T(8,128)(2,1)S(1)}, bf16[2,256,256]{1,2,0:T(8,128)(2,1)}, u32[]{:S(2)}) copy-start(bf16[2,256,256]{1,2,0:T(8,128)(2,1)} %get-tuple-element.31) | copy-start | bytes 786436
  115.8 3.1 %collective-permute-start = (bf16[4,256,512]{2,1,0:T(8,128)(2,1)S(1)}, bf16[4,256,512]{2,1,0:T(8,128)(2,1)}, u32[]{:S(2)}, u32[]{:S(2)}) collective-permute-start(bf16[4,256,512]{2,1,0:T(8,128)(2,1)S(1)} %dynamic-slice_bitcast_fusion), channel_id=1, source_target_pairs={{0,1},{1,0},{2,3},{3,2},{4,5},{5,4},{6,7},{7,6},{8,9},{9,8},{10,11... | collective-permute-start | bytes 3145736 | tf_op jit(solution)/shard_map/ppermute | solution.py:60
  121.4 5.9 %collective-permute-start.1 = (bf16[128,512]{1,0:T(8,128)(2,1)}, bf16[128,512]{1,0:T(8,128)(2,1)}, u32[]{:S(2)}, u32[]{:S(2)}) collective-permute-start(bf16[128,512]{1,0:T(8,128)(2,1)} %get-tuple-element.18), channel_id=1, source_target_pairs={{0,2},{2,4},{4,6},{6,0},{1,3},{3,5},{5,7},{7,1},{8,10},{10,12},{12... | collective-permute-start | bytes 393224 | tf_op jit(solution)/shard_map/ppermute | solution.py:73
  128.9 5.3 %collective-permute-start.2 = (bf16[128,512]{1,0:T(8,128)(2,1)}, bf16[128,512]{1,0:T(8,128)(2,1)}, u32[]{:S(2)}, u32[]{:S(2)}) collective-permute-start(bf16[128,512]{1,0:T(8,128)(2,1)} %fusion.30), channel_id=1, source_target_pairs={{0,2},{2,4},{4,6},{6,0},{1,3},{3,5},{5,7},{7,1},{8,10},{10,12},{12... | collective-permute-start | bytes 393224 | tf_op jit(solution)/shard_map/ppermute | solution.py:73
  130.2 6.9 %collective-permute-start.4 = (bf16[128,512]{1,0:T(8,128)(2,1)S(1)}, bf16[128,512]{1,0:T(8,128)(2,1)}, u32[]{:S(2)}, u32[]{:S(2)}) collective-permute-start(bf16[128,512]{1,0:T(8,128)(2,1)S(1)} %get-tuple-element.19), channel_id=1, source_target_pairs={{0,6},{2,0},{4,2},{6,4},{1,7},{3,1},{5,3},{7,5},{8,14},{10,8},{12,... | collective-permute-start | bytes 393224 | tf_op jit(solution)/shard_map/ppermute | solution.py:74
  135.7 6.4 %collective-permute-start.3 = (bf16[128,512]{1,0:T(8,128)(2,1)}, bf16[128,512]{1,0:T(8,128)(2,1)}, u32[]{:S(2)}, u32[]{:S(2)}) collective-permute-start(bf16[128,512]{1,0:T(8,128)(2,1)} %fusion.29), channel_id=1, source_target_pairs={{0,2},{2,4},{4,6},{6,0},{1,3},{3,5},{5,7},{7,1},{8,10},{10,12},{12... | collective-permute-start | bytes 393224 | tf_op jit(solution)/shard_map/ppermute | solution.py:73
  143.8 5.8 %collective-permute-start.5 = (bf16[128,512]{1,0:T(8,128)(2,1)S(1)}, bf16[128,512]{1,0:T(8,128)(2,1)S(1)}, u32[]{:S(2)}, u32[]{:S(2)}) collective-permute-start(bf16[128,512]{1,0:T(8,128)(2,1)S(1)} %get-tuple-element.17), channel_id=1, source_target_pairs={{0,6},{2,0},{4,2},{6,4},{1,7},{3,1},{5,3},{7,5},{8,14},{10,8},{12,... | collective-permute-start | bytes 393224 | tf_op jit(solution)/shard_map/ppermute | solution.py:74
  150.3 21.1 %collective-permute-start.6 = (bf16[128,512]{1,0:T(8,128)(2,1)}, bf16[128,512]{1,0:T(8,128)(2,1)}, u32[]{:S(2)}, u32[]{:S(2)}) collective-permute-start(bf16[128,512]{1,0:T(8,128)(2,1)} %fusion.26), channel_id=1, source_target_pairs={{0,6},{2,0},{4,2},{6,4},{1,7},{3,1},{5,3},{7,5},{8,14},{10,8},{12,... | collective-permute-start | bytes 393224 | tf_op jit(solution)/shard_map/ppermute | solution.py:74
  154.4 10.8 %all-to-all-start.4 = ((bf16[4,128,256]{1,2,0:T(8,128)(2,1)}), bf16[4,128,256]{1,2,0:T(8,128)(2,1)}, u32[]{:S(2)}, u32[]{:S(2)}) async-start(bf16[4,128,256]{1,2,0:T(8,128)(2,1)} %copy_bitcast_fusion.1), calls=%async_computation.5 | async-start | bytes 524288 | tf_op jit(solution)/shard_map/all_to_all | solution.py:90
  165.2 13.4 %all-to-all-start.5 = ((bf16[4,128,512]{1,2,0:T(8,128)(2,1)}), bf16[4,128,512]{1,2,0:T(8,128)(2,1)}, u32[]{:S(2)}, u32[]{:S(2)}) async-start(bf16[4,128,512]{1,2,0:T(8,128)(2,1)} %copy_bitcast_fusion), calls=%async_computation.7 | async-start | bytes 1048576 | tf_op jit(solution)/shard_map/all_to_all | solution.py:90
Sparse Core Ops, SparseCore 0:
  62.1 43.2 reduce-scatter.2
  108.5 54.1 reduce-scatter.4

commit v7 on v5

--- a/solution.py
+++ b/solution.py
@@ -104,8 +104,10 @@
     value_own = to_blocks(projected[:, :, 2].reshape(local_tokens, head_count * HD), HD)
     order = matching[0]
     inverse = jnp.zeros_like(order).at[order].set(jnp.arange(n_ctx, dtype=order.dtype))
+    far_rows = from_pieces(route(to_pieces(activations, n_ctx), order))
     own_kv = jnp.stack([key_own, value_own], 0)
     far_kv = from_pieces(route(to_pieces(own_kv, n_ctx), order))
+    far_rows, far_kv = lax.optimization_barrier((far_rows, far_kv))
     key_far, value_far = far_kv[0], far_kv[1]
 
     def mm(form, left, right):
@@ -145,12 +147,22 @@
     far_part = jnp.stack(
         [mm("hnqk,hnqd->hnkd", score_grad_far, query), mm("hnqk,hnqd->hnkd", dropped_far, grad_out)], 0
     ).astype(jnp.bfloat16)
+    near_cols = jnp.stack(
+        [grad_query.astype(f32), grad_key_own, grad_value_own], 3
+    ).transpose(1, 2, 0, 3, 4).reshape(local_tokens, head_count * 3 * HD)
+    far_cols = jnp.concatenate(
+        [jnp.zeros((1,) + far_part.shape[1:], far_part.dtype), far_part], 0
+    ).transpose(2, 3, 1, 0, 4).reshape(local_tokens, head_count * 3 * HD)
+    both_rows = jnp.concatenate([activations, far_rows], 0)
+    both_cols = jnp.concatenate([near_cols.astype(jnp.bfloat16), far_cols], 0)
+    weight_part = weight_term(both_rows, both_cols)
+    far_part, weight_part = lax.optimization_barrier((far_part, weight_part))
     returned = from_pieces(route(to_pieces(far_part, n_ctx), inverse))
     grad_key = (grad_key_own + returned[0].astype(f32)).astype(jnp.bfloat16)
     grad_value = (grad_value_own + returned[1].astype(f32)).astype(jnp.bfloat16)
     stacked = jnp.stack([grad_query, grad_key, grad_value], 3)
     grad_qkv = stacked.transpose(1, 2, 0, 3, 4).reshape(local_tokens, head_count * 3 * HD)
-    weight_grad = reduce_ctx(weight_term(activations, grad_qkv))
+    weight_grad = reduce_ctx(weight_part)
     n_y = lax.psum(1, "y")
     width = activations.shape[1] // (2 * n_y)
     w_split = w_qkv.reshape(n_y, 2, width, w_qkv.shape[1])

time: 203 us -> 278 us (1.37)
  waiting for transfers between devices: 80.9 us -> 159 us
  starting transfers between devices: 28.5 us -> 39.9 us
  other arithmetic: 16.1 us -> 4.76 us
  local copies, waits for them, and re-layouts: 16.3 us -> 11.5 us
    all_to_all x1 -> x2, waiting for transfers between devices: 11.1 us -> 60.9 us  [route(): spread = lax.all_to_all(payload, CTX, 0, 0, tiled=True)]
    all_to_all x2 -> x3, waiting for transfers between devices: 18.6 us -> 68.3 us  [route(): return lax.all_to_all(chosen.reshape(spread.shape), CTX, 0, 0, tiled=True)]
    reduce_scatter x1, waiting for transfers between devices: 27.7 us -> 2.75 us  [reduce_ctx(): part = lax.psum_scatter(part, 'z', scatter_dimension=0, tiled=True)]
    all_to_all x2 -> x3, starting transfers between devices: 9.18 us -> 14.7 us  [route(): return lax.all_to_all(chosen.reshape(spread.shape), CTX, 0, 0, tiled=True)]
    all_to_all x1 -> x2, starting transfers between devices: 3.87 us -> 9.38 us  [route(): spread = lax.all_to_all(payload, CTX, 0, 0, tiled=True)]
    convert_element_type x3, other arithmetic: 4.89 us -> 0.15 us  [ring_rs(): (got_a.astype(jnp.float32) + take(i - s - 2 + 2 * n, 0).astype(jnp.float3...]
    dot_general x12, matrix products: 7.11 us -> 2.83 us  [mm(): return jnp.einsum(form, left, right, preferred_element_type=f32)]
    dot_general x1, matrix products: 4.48 us -> 7.75 us  [weight_term(): lax.dot_general(activations, cols, (((0,), (0,)), ((), ())), preferred_el...]
  transfers between devices with their start and end apart: 12 -> 14, of which waited for: 10 -> 12; matrix products, arithmetic and copies ran while one was open for 13% -> 8% of each run, Pallas kernels for 0% -> 0%
where the time goes in v7:
time: 278 us; the launch traced here: 277 us
  waiting for transfers between devices  159 us (57%)
  starting transfers between devices  39.9 us (14%)
  blocking collectives  23.9 us (9%)
  matrix products  23.1 us (8%)
  between operations  14.5 us (5%)
  local copies, waits for them, and re-layouts  11.5 us (4%)
  other arithmetic  4.76 us (2%)
    all_to_all x3, waiting for transfers between devices, route(): return lax.all_to_all(chosen.reshape(spread.shape), CTX, 0, 0, tiled=True)  68.3 us
    all_to_all x2, waiting for transfers between devices, route(): spread = lax.all_to_all(payload, CTX, 0, 0, tiled=True)  60.9 us
    all_to_all x1, blocking collectives, route(): spread = lax.all_to_all(payload, CTX, 0, 0, tiled=True)  23.9 us
    all_to_all x3, starting transfers between devices, route(): return lax.all_to_all(chosen.reshape(spread.shape), CTX, 0, 0, tiled=True)  14.7 us
    ppermute x3, waiting for transfers between devices, ring_rs(): got_a = lax.ppermute(acc_a, axis, cw)  11.6 us
    all_to_all x1, waiting for transfers between devices, reduce_ctx(): gathered = lax.all_to_all(pieces, 'x', 0, 0, tiled=True)  10.8 us
    all_to_all x2, starting transfers between devices, route(): spread = lax.all_to_all(payload, CTX, 0, 0, tiled=True)  9.38 us
    dot_general x1, matrix products, weight_term(): lax.dot_general(activations, cols, (((0,), (0,)), ((), ())), preferred_el...  7.75 us
  transfers between devices with their start and end apart: 14, of which 12 were waited for; matrix products, arithmetic and copies ran while one was open for 8% of the time, Pallas kernels for 0%

profile of v7, /device:TPU:8, one launch (start us, length us, event | category | flops | bytes accessed | tf_op | source)
XLA Modules:
  0.0 277.1 jit_solution(2530476852641998978)
XLA Ops:
  7.2 5.2 %convolution_convert_fusion.5 = bf16[256,768]{1,0:T(8,128)(2,1)S(1)} fusion(bf16[256,4096]{1,0:T(8,128)(2,1)} %param.5, bf16[4096,768]{1,0:T(8,128)(2,1)} %param.6), kind=kOutput, calls=%fused_computation.11 | convolution fusion | flops 1610809344 | bytes 8781824 | tf_op jit(solution)/shard_map/dot_general | solution.py:100
  12.4 0.2 copy.68
  12.7 0.1 copy.72
  12.9 23.9 %all_to_all.35 = bf16[32,2,2,1,8,128]{5,4,2,3,1,0:T(8,128)(2,1)S(1)} all-to-all(bf16[32,2,2,1,8,128]{5,4,2,3,1,0:T(8,128)(2,1)S(1)} %copy.73), channel_id=1, replica_groups=mesh['z'=8,'x'=4,'y'=4,'c'=2] {'z','x'}, dimensions={0} | all-to-all | bytes 524288 | tf_op jit(solution)/shard_map/all_to_all | solution.py:35
  36.9 4.1 %all-to-all-start = ((bf16[32,8,4096]{2,1,0:T(8,128)(2,1)}), bf16[32,8,4096]{2,1,0:T(8,128)(2,1)S(1)}, u32[]{:S(2)}, u32[]{:S(2)}) async-start(bf16[32,8,4096]{2,1,0:T(8,128)(2,1)} %bitcast.265), calls=%async_computation | async-start | bytes 4194304 | tf_op jit(solution)/shard_map/all_to_all | solution.py:35
  41.0 0.3 fusion.6
  41.3 0.7 copy.131
  42.0 48.3 %all-to-all-done = bf16[32,8,4096]{2,1,0:T(8,128)(2,1)S(1)} async-done(((bf16[32,8,4096]{2,1,0:T(8,128)(2,1)}), bf16[32,8,4096]{2,1,0:T(8,128)(2,1)S(1)}, u32[]{:S(2)}, u32[]{:S(2)}) %all-to-all-start) | async-done | bytes 2097184 | tf_op jit(solution)/shard_map/all_to_all | solution.py:35
  90.4 5.9 %all-to-all-start.3 = ((bf16[32,2,2,1,8,128]{5,4,2,1,3,0:T(8,128)(2,1)}), bf16[32,2,2,1,8,128]{5,4,2,1,3,0:T(8,128)(2,1)S(1)}, u32[]{:S(2)}, u32[]{:S(2)}) async-start(bf16[32,2,2,1,8,128]{5,4,2,1,3,0:T(8,128)(2,1)} %bitcast.18), calls=%async_computation.3 | async-start | bytes 524288 | tf_op jit(solution)/shard_map/all_to_all | solution.py:40
  96.3 1.2 copy.128
  97.5 0.8 convolution_convert_fusion
  98.2 2.5 copy.129
  100.7 7.3 %all-to-all-done.3 = bf16[32,2,2,1,8,128]{5,4,2,1,3,0:T(8,128)(2,1)S(1)} async-done(((bf16[32,2,2,1,8,128]{5,4,2,1,3,0:T(8,128)(2,1)}), bf16[32,2,2,1,8,128]{5,4,2,1,3,0:T(8,128)(2,1)S(1)}, u32[]{:S(2)}, u32[]{:S(2)}) %all-to-all-start.3) | async-done | bytes 262176 | tf_op jit(solution)/shard_map/all_to_all | solution.py:40
  108.0 4.9 %all-to-all-start.1 = ((bf16[32,8,4096]{2,1,0:T(8,128)(2,1)}), bf16[32,8,4096]{2,1,0:T(8,128)(2,1)}, u32[]{:S(2)}, u32[]{:S(2)}) async-start(bf16[32,8,4096]{2,1,0:T(8,128)(2,1)} %bitcast.103), calls=%async_computation.1 | async-start | bytes 4194304 | tf_op jit(solution)/shard_map/all_to_all | solution.py:40
  113.0 0.2 reduce-scatter.2.cloned.1.call-start
  113.5 0.2 fusion.18
  113.7 0.2 fusion.69
  114.0 0.3 fusion.5
  114.3 46.7 %all-to-all-done.1 = bf16[32,8,4096]{2,1,0:T(8,128)(2,1)} async-done(((bf16[32,8,4096]{2,1,0:T(8,128)(2,1)}), bf16[32,8,4096]{2,1,0:T(8,128)(2,1)}, u32[]{:S(2)}, u32[]{:S(2)}) %all-to-all-start.1) | async-done | bytes 2097184 | tf_op jit(solution)/shard_map/all_to_all | solution.py:40
  161.0 0.2 fusion.70
  161.3 0.2 exponential_reduce_fusion
  161.5 0.3 multiply_reduce_fusion
  161.8 0.4 multiply_convert_fusion.1
  162.2 0.2 fusion.42
  162.5 0.2 fusion.51
  162.7 0.2 fusion.10
  162.9 0.2 fusion.12
  163.2 0.2 fusion.11
  163.4 0.2 fusion.71
  163.9 1.4 copy-done
  165.2 7.8 %convolution_convert_fusion.1 = bf16[4096,768]{1,0:T(8,128)(2,1)} fusion(bf16[256,4096]{1,0:T(8,128)(2,1)} %bitcast.11, bf16[256,4096]{1,0:T(8,128)(2,1)S(1)} %copy-done, bf16[256,768]{0,1:T(8,128)(2,1)S(1)} %bitcast.275, bf16[256,768]{0,1:T(8,128)(2,1)S(1)} %bitcast.274), kind=kOutput, calls=%fused_computation.2 | convolution fusion | flops 3234332672 | bytes 11272192 | tf_op jit(solution)/shard_map/dot_general | solution.py:81
  173.0 0.2 copy.95
  173.2 0.8 copy.96
  173.9 5.2 %all-to-all-start.4 = ((bf16[32,2,2,1,8,128]{5,4,2,1,3,0:T(8,128)(2,1)}), bf16[32,2,2,1,8,128]{5,4,2,1,3,0:T(8,128)(2,1)S(1)}, u32[]{:S(2)}, u32[]{:S(2)}) async-start(bf16[32,2,2,1,8,128]{5,4,2,1,3,0:T(8,128)(2,1)} %copy.96), calls=%async_computation.4 | async-start | bytes 524288 | tf_op jit(solution)/shard_map/all_to_all | solution.py:35
  179.2 0.7 scatter_custom_fusion
  179.9 12.6 %all-to-all-done.4 = bf16[32,2,2,1,8,128]{5,4,2,1,3,0:T(8,128)(2,1)S(1)} async-done(((bf16[32,2,2,1,8,128]{5,4,2,1,3,0:T(8,128)(2,1)}), bf16[32,2,2,1,8,128]{5,4,2,1,3,0:T(8,128)(2,1)S(1)}, u32[]{:S(2)}, u32[]{:S(2)}) %all-to-all-start.4) | async-done | bytes 262176 | tf_op jit(solution)/shard_map/all_to_all | solution.py:35
  192.4 0.3 fusion.7
  192.7 0.7 copy.133
  193.4 3.9 %all-to-all-start.5 = ((bf16[32,2,2,1,8,128]{5,4,2,3,1,0:T(8,128)(2,1)}), bf16[32,2,2,1,8,128]{5,4,2,3,1,0:T(8,128)(2,1)S(1)}, u32[]{:S(2)}, u32[]{:S(2)}) async-start(bf16[32,2,2,1,8,128]{5,4,2,3,1,0:T(8,128)(2,1)} %bitcast.57), calls=%async_computation.5 | async-start | bytes 524288 | tf_op jit(solution)/shard_map/all_to_all | solution.py:40
  197.3 14.3 %all-to-all-done.5 = bf16[32,2,2,1,8,128]{5,4,2,3,1,0:T(8,128)(2,1)S(1)} async-done(((bf16[32,2,2,1,8,128]{5,4,2,3,1,0:T(8,128)(2,1)}), bf16[32,2,2,1,8,128]{5,4,2,3,1,0:T(8,128)(2,1)S(1)}, u32[]{:S(2)}, u32[]{:S(2)}) %all-to-all-start.5) | async-done | bytes 262176 | tf_op jit(solution)/shard_map/all_to_all | solution.py:40
  211.7 0.1 copy.99
  211.9 0.1 copy.100
  212.2 6.0 %convolution_convert_fusion.4 = bf16[256,4,2,512]{3,0,2,1:T(8,128)(2,1)} fusion(bf16[256,768,1,1]{0,1,3,2:T(8,128)(2,1)S(1)} %bitcast.276, bf16[4,2,512,768]{3,2,1,0:T(8,128)(2,1)} %bitcast.280), kind=kOutput, calls=%fused_computation.10 | convolution fusion | flops 1611661312 | bytes 8781824 | tf_op jit(solution)/shard_map/tk,ycwk->cytw/dot_general | solution.py:169
  218.2 1.3 dynamic-slice_bitcast_fusion
  219.7 2.7 collective-permute-done
  222.4 1.9 fusion.3
  224.3 1.7 collective-permute-start.1
  226.0 3.9 %collective-permute-done.1 = bf16[128,512]{1,0:T(8,128)(2,1)S(1)} collective-permute-done((bf16[128,512]{1,0:T(8,128)(2,1)S(1)}, bf16[128,512]{1,0:T(8,128)(2,1)S(1)}, u32[]{:S(2)}, u32[]{:S(2)}) %collective-permute-start.1) | collective-permute-done | bytes 131104 | tf_op jit(solution)/shard_map/ppermute | solution.py:73
  230.0 1.9 collective-permute-start.2
  231.9 0.4 collective-permute-start.4
  232.3 3.2 %collective-permute-done.2 = bf16[128,512]{1,0:T(8,128)(2,1)S(1)} collective-permute-done((bf16[128,512]{1,0:T(8,128)(2,1)S(1)}, bf16[128,512]{1,0:T(8,128)(2,1)S(1)}, u32[]{:S(2)}, u32[]{:S(2)}) %collective-permute-start.2) | collective-permute-done | bytes 131104 | tf_op jit(solution)/shard_map/ppermute | solution.py:73
  235.5 1.5 collective-permute-start.3
  237.0 4.5 %collective-permute-done.3 = bf16[128,512]{1,0:T(8,128)(2,1)S(1)} collective-permute-done((bf16[128,512]{1,0:T(8,128)(2,1)S(1)}, bf16[128,512]{1,0:T(8,128)(2,1)S(1)}, u32[]{:S(2)}, u32[]{:S(2)}) %collective-permute-start.3) | collective-permute-done | bytes 131104 | tf_op jit(solution)/shard_map/ppermute | solution.py:73
  241.6 3.3 %collective-permute-start.5 = (bf16[128,512]{1,0:T(8,128)(2,1)S(1)}, bf16[128,512]{1,0:T(8,128)(2,1)S(1)}, u32[]{:S(2)}, u32[]{:S(2)}) collective-permute-start(bf16[128,512]{1,0:T(8,128)(2,1)S(1)} %get-tuple-element.25), channel_id=1, source_target_pairs={{0,6},{2,0},{4,2},{6,4},{1,7},{3,1},{5,3},{7,5},{8,14},{10,8},{12,... | collective-permute-start | bytes 393224 | tf_op jit(solution)/shard_map/ppermute | solution.py:74
  244.9 0.2 fusion.46
  245.1 2.3 collective-permute-done.5
  247.5 2.5 collective-permute-start.6
  250.0 2.8 reduce-scatter.2.cloned.1.call-done
  252.7 4.2 %all-to-all-start.6 = ((bf16[4,128,768]{2,1,0:T(8,128)(2,1)}), bf16[4,128,768]{2,1,0:T(8,128)(2,1)S(1)}, u32[]{:S(2)}, u32[]{:S(2)}) async-start(bf16[4,128,768]{2,1,0:T(8,128)(2,1)} %bitcast.271), calls=%async_computation.7 | async-start | bytes 1572864 | tf_op jit(solution)/shard_map/all_to_all | solution.py:90
  256.9 0.2 fusion.9
  257.1 0.8 copy.104
  257.9 0.7 pad_maximum_fusion.3
  258.6 10.8 %all-to-all-done.6 = bf16[4,128,768]{2,1,0:T(8,128)(2,1)S(1)} async-done(((bf16[4,128,768]{2,1,0:T(8,128)(2,1)}), bf16[4,128,768]{2,1,0:T(8,128)(2,1)S(1)}, u32[]{:S(2)}, u32[]{:S(2)}) %all-to-all-start.6) | async-done | bytes 786464 | tf_op jit(solution)/shard_map/all_to_all | solution.py:90
  269.5 0.8 reduce_sum.52
  (44 shorter events, 1.4 us)
Async XLA Ops:
  36.9 4.2 %copy-start.3 = (s32[1,32]{1,0:T(1,128)S(1)}, s32[1,32]{1,0:T(1,128)}, u32[]{:S(2)}) copy-start(s32[1,32]{1,0:T(1,128)} %param.7) | copy-start | bytes 388
  36.9 53.5 %all-to-all-start = ((bf16[32,8,4096]{2,1,0:T(8,128)(2,1)}), bf16[32,8,4096]{2,1,0:T(8,128)(2,1)S(1)}, u32[]{:S(2)}, u32[]{:S(2)}) async-start(bf16[32,8,4096]{2,1,0:T(8,128)(2,1)} %bitcast.265), calls=%async_computation | async-start | bytes 4194304 | tf_op jit(solution)/shard_map/all_to_all | solution.py:35
  90.4 17.7 %all-to-all-start.3 = ((bf16[32,2,2,1,8,128]{5,4,2,1,3,0:T(8,128)(2,1)}), bf16[32,2,2,1,8,128]{5,4,2,1,3,0:T(8,128)(2,1)S(1)}, u32[]{:S(2)}, u32[]{:S(2)}) async-start(bf16[32,2,2,1,8,128]{5,4,2,1,3,0:T(8,128)(2,1)} %bitcast.18), calls=%async_computation.3 | async-start | bytes 524288 | tf_op jit(solution)/shard_map/all_to_all | solution.py:40
  108.0 5.2 %copy-start.1 = (bf16[256,256]{1,0:T(8,128)(2,1)S(1)}, bf16[256,256]{1,0:T(8,128)(2,1)}, u32[]{:S(2)}) copy-start(bf16[256,256]{1,0:T(8,128)(2,1)} %param.9) | copy-start | bytes 393220
  108.0 5.5 %copy-start.2 = (s32[256,64]{0,1:T(8,128)S(1)}, s32[256,64]{0,1:T(8,128)}, u32[]{:S(2)}) copy-start(s32[256,64]{0,1:T(8,128)} %param.8) | copy-start | bytes 196612
  108.0 53.0 %all-to-all-start.1 = ((bf16[32,8,4096]{2,1,0:T(8,128)(2,1)}), bf16[32,8,4096]{2,1,0:T(8,128)(2,1)}, u32[]{:S(2)}, u32[]{:S(2)}) async-start(bf16[32,8,4096]{2,1,0:T(8,128)(2,1)} %bitcast.103), calls=%async_computation.1 | async-start | bytes 4194304 | tf_op jit(solution)/shard_map/all_to_all | solution.py:40
  113.0 139.8 %reduce-scatter.2.cloned.1.call-start = ((), (), s32[]{:S(2)}) async-start(), calls=%async_computation.8 | async-start | bytes 7077888 | tf_op jit(solution)/shard_map/reduce_scatter | solution.py:87
  163.6 1.6 copy-start
  173.9 18.5 %all-to-all-start.4 = ((bf16[32,2,2,1,8,128]{5,4,2,1,3,0:T(8,128)(2,1)}), bf16[32,2,2,1,8,128]{5,4,2,1,3,0:T(8,128)(2,1)S(1)}, u32[]{:S(2)}, u32[]{:S(2)}) async-start(bf16[32,2,2,1,8,128]{5,4,2,1,3,0:T(8,128)(2,1)} %copy.96), calls=%async_computation.4 | async-start | bytes 524288 | tf_op jit(solution)/shard_map/all_to_all | solution.py:35
  193.4 18.2 %all-to-all-start.5 = ((bf16[32,2,2,1,8,128]{5,4,2,3,1,0:T(8,128)(2,1)}), bf16[32,2,2,1,8,128]{5,4,2,3,1,0:T(8,128)(2,1)S(1)}, u32[]{:S(2)}, u32[]{:S(2)}) async-start(bf16[32,2,2,1,8,128]{5,4,2,3,1,0:T(8,128)(2,1)} %bitcast.57), calls=%async_computation.5 | async-start | bytes 524288 | tf_op jit(solution)/shard_map/all_to_all | solution.py:40
  219.5 2.9 %collective-permute-start = (bf16[4,256,512]{2,1,0:T(8,128)(2,1)S(1)}, bf16[4,256,512]{2,1,0:T(8,128)(2,1)}, u32[]{:S(2)}, u32[]{:S(2)}) collective-permute-start(bf16[4,256,512]{2,1,0:T(8,128)(2,1)S(1)} %dynamic-slice_bitcast_fusion), channel_id=1, source_target_pairs={{0,1},{1,0},{2,3},{3,2},{4,5},{5,4},{6,7},{7,6},{8,9},{9,8},{10,11... | collective-permute-start | bytes 3145736 | tf_op jit(solution)/shard_map/ppermute | solution.py:60
  224.3 5.6 %collective-permute-start.1 = (bf16[128,512]{1,0:T(8,128)(2,1)S(1)}, bf16[128,512]{1,0:T(8,128)(2,1)S(1)}, u32[]{:S(2)}, u32[]{:S(2)}) collective-permute-start(bf16[128,512]{1,0:T(8,128)(2,1)S(1)} %get-tuple-element.26), channel_id=1, source_target_pairs={{0,2},{2,4},{4,6},{6,0},{1,3},{3,5},{5,7},{7,1},{8,10},{10,12},{12... | collective-permute-start | bytes 393224 | tf_op jit(solution)/shard_map/ppermute | solution.py:73
  230.0 5.5 %collective-permute-start.2 = (bf16[128,512]{1,0:T(8,128)(2,1)S(1)}, bf16[128,512]{1,0:T(8,128)(2,1)S(1)}, u32[]{:S(2)}, u32[]{:S(2)}) collective-permute-start(bf16[128,512]{1,0:T(8,128)(2,1)S(1)} %fusion.35), channel_id=1, source_target_pairs={{0,2},{2,4},{4,6},{6,0},{1,3},{3,5},{5,7},{7,1},{8,10},{10,12},{12... | collective-permute-start | bytes 393224 | tf_op jit(solution)/shard_map/ppermute | solution.py:73
  231.9 5.1 %collective-permute-start.4 = (bf16[128,512]{1,0:T(8,128)(2,1)S(1)}, bf16[128,512]{1,0:T(8,128)(2,1)S(1)}, u32[]{:S(2)}, u32[]{:S(2)}) collective-permute-start(bf16[128,512]{1,0:T(8,128)(2,1)S(1)} %get-tuple-element.27), channel_id=1, source_target_pairs={{0,6},{2,0},{4,2},{6,4},{1,7},{3,1},{5,3},{7,5},{8,14},{10,8},{12,... | collective-permute-start | bytes 393224 | tf_op jit(solution)/shard_map/ppermute | solution.py:74
  235.5 6.0 %collective-permute-start.3 = (bf16[128,512]{1,0:T(8,128)(2,1)S(1)}, bf16[128,512]{1,0:T(8,128)(2,1)S(1)}, u32[]{:S(2)}, u32[]{:S(2)}) collective-permute-start(bf16[128,512]{1,0:T(8,128)(2,1)S(1)} %fusion.34), channel_id=1, source_target_pairs={{0,2},{2,4},{4,6},{6,0},{1,3},{3,5},{5,7},{7,1},{8,10},{10,12},{12... | collective-permute-start | bytes 393224 | tf_op jit(solution)/shard_map/ppermute | solution.py:73
  241.6 5.8 %collective-permute-start.5 = (bf16[128,512]{1,0:T(8,128)(2,1)S(1)}, bf16[128,512]{1,0:T(8,128)(2,1)S(1)}, u32[]{:S(2)}, u32[]{:S(2)}) collective-permute-start(bf16[128,512]{1,0:T(8,128)(2,1)S(1)} %get-tuple-element.25), channel_id=1, source_target_pairs={{0,6},{2,0},{4,2},{6,4},{1,7},{3,1},{5,3},{7,5},{8,14},{10,8},{12,... | collective-permute-start | bytes 393224 | tf_op jit(solution)/shard_map/ppermute | solution.py:74
  247.5 10.4 %collective-permute-start.6 = (bf16[128,512]{1,0:T(8,128)(2,1)S(1)}, bf16[128,512]{1,0:T(8,128)(2,1)S(1)}, u32[]{:S(2)}, u32[]{:S(2)}) collective-permute-start(bf16[128,512]{1,0:T(8,128)(2,1)S(1)} %fusion.31), channel_id=1, source_target_pairs={{0,6},{2,0},{4,2},{6,4},{1,7},{3,1},{5,3},{7,5},{8,14},{10,8},{12,... | collective-permute-start | bytes 393224 | tf_op jit(solution)/shard_map/ppermute | solution.py:74
  252.7 16.7 %all-to-all-start.6 = ((bf16[4,128,768]{2,1,0:T(8,128)(2,1)}), bf16[4,128,768]{2,1,0:T(8,128)(2,1)S(1)}, u32[]{:S(2)}, u32[]{:S(2)}) async-start(bf16[4,128,768]{2,1,0:T(8,128)(2,1)} %bitcast.271), calls=%async_computation.7 | async-start | bytes 1572864 | tf_op jit(solution)/shard_map/all_to_all | solution.py:90
Sparse Core Ops, SparseCore 0:
  173.1 79.5 reduce-scatter.1

commit v8 on v6

--- a/solution.py
+++ b/solution.py
@@ -84,7 +84,10 @@
 
 
 def reduce_ctx(part):
-    part = lax.psum_scatter(part, "z", scatter_dimension=0, tiled=True)
+    return reduce_x(lax.psum_scatter(part, "z", scatter_dimension=0, tiled=True))
+
+
+def reduce_x(part):
     n_x = lax.psum(1, "x")
     pieces = part.reshape((n_x, part.shape[0] // n_x) + part.shape[1:])
     gathered = lax.all_to_all(pieces, "x", 0, 0, tiled=True)
@@ -154,17 +157,19 @@
     kv_cols = jnp.stack([grad_key, grad_value], 3).transpose(1, 2, 0, 3, 4)
     kv_cols = kv_cols.reshape(local_tokens, head_count * 2 * HD)
     weight_q = reduce_ctx(weight_term(activations, query_cols))
-    weight_kv = reduce_ctx(weight_term(activations, kv_cols))
-    rows = weight_q.shape[0]
-    weight_grad = jnp.concatenate(
-        [weight_q.reshape(rows, head_count, 1, HD), weight_kv.reshape(rows, head_count, 2, HD)], 2
-    ).reshape(rows, head_count * 3 * HD)
+    weight_kv = lax.psum_scatter(weight_term(activations, kv_cols), "z", scatter_dimension=0, tiled=True)
     n_y = lax.psum(1, "y")
     width = activations.shape[1] // (2 * n_y)
     w_split = w_qkv.reshape(n_y, 2, width, w_qkv.shape[1])
     by_core = jnp.einsum("tk,ycwk->cytw", grad_qkv, w_split, preferred_element_type=f32)
     core_sum = ring_rs(by_core.astype(jnp.bfloat16), "c", 2)
     input_grad = ring_rs(core_sum, "y", n_y)
+    input_grad, weight_q, weight_kv = lax.optimization_barrier((input_grad, weight_q, weight_kv))
+    weight_kv = reduce_x(weight_kv)
+    rows = weight_q.shape[0]
+    weight_grad = jnp.concatenate(
+        [weight_q.reshape(rows, head_count, 1, HD), weight_kv.reshape(rows, head_count, 2, HD)], 2
+    ).reshape(rows, head_count * 3 * HD)
     return (from_blocks(attended), input_grad, weight_grad)
 
 

time: 189 us -> 188 us (level)
  waiting for transfers between devices: 45.3 us -> 49.6 us
  other arithmetic: 16.2 us -> 13.7 us
    all_to_all x2, waiting for transfers between devices: 4.22 us -> 11 us  [reduce_x(): gathered = lax.all_to_all(pieces, 'x', 0, 0, tiled=True)]
    reduce_scatter x2, waiting for transfers between devices: 4.31 us -> 0.02 us  [the longest x1 0.02 us: per_device(): lax.psum_scatter(weight_term(activations, kv_cols), 'z', scatter_dimensio...]
    ppermute x3, waiting for transfers between devices: 0.6 us -> 2.53 us  [ring_rs(): got_b = lax.ppermute(acc_b, axis, ccw)]
    unnamed x36 -> x40, local copies, waits for them, and re-layouts: 6.11 us -> 6.1 us
  transfers between devices with their start and end apart: 13 -> 13, of which waited for: 10 -> 9; matrix products, arithmetic and copies ran while one was open for 22% -> 19% of each run, Pallas kernels for 0% -> 0%
where the time goes in v8:
time: 188 us; the launch traced here: 187 us
  waiting for transfers between devices  49.6 us (26%)
  blocking collectives  41.4 us (22%)
  starting transfers between devices  26.9 us (14%)
  matrix products  22 us (12%)
  local copies, waits for them, and re-layouts  18.7 us (10%)
  between operations  14.6 us (8%)
  other arithmetic  13.7 us (7%)
    all_to_all x1, blocking collectives, route(): spread = lax.all_to_all(payload, CTX, 0, 0, tiled=True)  23.9 us
    all_to_all x1, blocking collectives, route(): return lax.all_to_all(chosen.reshape(spread.shape), CTX, 0, 0, tiled=True)  17.5 us
    all_to_all x1, waiting for transfers between devices, route(): spread = lax.all_to_all(payload, CTX, 0, 0, tiled=True)  13.2 us
    ppermute x3, waiting for transfers between devices, ring_rs(): got_a = lax.ppermute(acc_a, axis, cw)  12.7 us
    all_to_all x2, waiting for transfers between devices, reduce_x(): gathered = lax.all_to_all(pieces, 'x', 0, 0, tiled=True)  11 us
    all_to_all x2, starting transfers between devices, reduce_x(): gathered = lax.all_to_all(pieces, 'x', 0, 0, tiled=True)  7.51 us
    all_to_all x1, waiting for transfers between devices, route(): return lax.all_to_all(chosen.reshape(spread.shape), CTX, 0, 0, tiled=True)  7.39 us
    ppermute x3, starting transfers between devices, ring_rs(): got_b = lax.ppermute(acc_b, axis, ccw)  6.39 us
  transfers between devices with their start and end apart: 13, of which 9 were waited for; matrix products, arithmetic and copies ran while one was open for 19% of the time, Pallas kernels for 0%

profile of v8, /device:TPU:8, one launch (start us, length us, event | category | flops | bytes accessed | tf_op | source)
XLA Modules:
  0.0 186.9 jit_solution(14060579156049557886)
XLA Ops:
  7.2 1.6 copy-done
  8.8 4.6 %convolution_convert_fusion.5 = bf16[256,768]{1,0:T(8,128)(2,1)S(1)} fusion(bf16[256,4096]{1,0:T(8,128)(2,1)S(1)} %copy-done, bf16[4096,768]{1,0:T(8,128)(2,1)} %param.6), kind=kOutput, calls=%fused_computation.10 | convolution fusion | flops 1610809344 | bytes 8781824 | tf_op jit(solution)/shard_map/dot_general | solution.py:103
  13.9 23.9 %all_to_all.30 = bf16[32,2,2,1,8,128]{5,4,2,3,1,0:T(8,128)(2,1)S(1)} all-to-all(bf16[32,2,2,1,8,128]{5,4,2,3,1,0:T(8,128)(2,1)S(1)} %copy.71), channel_id=1, replica_groups=mesh['z'=8,'x'=4,'y'=4,'c'=2] {'z','x'}, dimensions={0} | all-to-all | bytes 524288 | tf_op jit(solution)/shard_map/all_to_all | solution.py:35
  37.8 0.3 fusion.5
  38.1 0.7 copy.129
  38.9 4.6 %all-to-all-start.1 = ((bf16[32,2,2,1,8,128]{5,4,2,3,1,0:T(8,128)(2,1)}), bf16[32,2,2,1,8,128]{5,4,2,3,1,0:T(8,128)(2,1)}, u32[]{:S(2)}, u32[]{:S(2)}) async-start(bf16[32,2,2,1,8,128]{5,4,2,3,1,0:T(8,128)(2,1)} %bitcast.16), calls=%async_computation.1 | async-start | bytes 524288 | tf_op jit(solution)/shard_map/all_to_all | solution.py:40
  43.5 0.8 slice_bitcast_fusion.10
  44.4 1.0 copy.119
  45.5 1.0 fusion.20
  46.5 0.2 fusion.51
  46.8 1.2 fusion.4
  48.0 7.4 %all-to-all-done.1 = bf16[32,2,2,1,8,128]{5,4,2,3,1,0:T(8,128)(2,1)} async-done(((bf16[32,2,2,1,8,128]{5,4,2,3,1,0:T(8,128)(2,1)}), bf16[32,2,2,1,8,128]{5,4,2,3,1,0:T(8,128)(2,1)}, u32[]{:S(2)}, u32[]{:S(2)}) %all-to-all-start.1) | async-done | bytes 262176 | tf_op jit(solution)/shard_map/all_to_all | solution.py:40
  55.4 1.1 copy.146
  56.4 0.2 fusion.52
  56.9 0.3 multiply_reduce_fusion
  57.5 1.2 multiply_convert_fusion
  58.7 0.7 copy-done.3
  59.4 0.2 fusion.35
  59.7 0.2 fusion.7
  59.9 2.1 %fusion.1 = bf16[4096,256]{0,1:T(8,128)(2,1)} fusion(bf16[256,256]{0,1:T(8,128)(2,1)S(1)} %bitcast.274, bf16[256,4096]{1,0:T(8,128)(2,1)S(1)} %copy-done), kind=kOutput, calls=%fused_computation.4 | convolution fusion | flops 537919488 | bytes 4325376 | tf_op jit(solution)/shard_map/dot_general | solution.py:81
  62.0 0.9 copy-done.6
  63.4 0.8 copy_bitcast_fusion.2
  64.1 3.9 %all-to-all-start.2 = ((bf16[32,2,2,1,8,128]{5,4,2,1,3,0:T(8,128)(2,1)}), bf16[32,2,2,1,8,128]{5,4,2,1,3,0:T(8,128)(2,1)S(1)}, u32[]{:S(2)}, u32[]{:S(2)}) async-start(bf16[32,2,2,1,8,128]{5,4,2,1,3,0:T(8,128)(2,1)} %copy_bitcast_fusion.2), calls=%async_computation.2 | async-start | bytes 524288 | tf_op jit(solution)/shard_map/all_to_all | solution.py:35
  68.1 0.7 scatter_custom_fusion
  68.8 13.2 %all-to-all-done.2 = bf16[32,2,2,1,8,128]{5,4,2,1,3,0:T(8,128)(2,1)S(1)} async-done(((bf16[32,2,2,1,8,128]{5,4,2,1,3,0:T(8,128)(2,1)}), bf16[32,2,2,1,8,128]{5,4,2,1,3,0:T(8,128)(2,1)S(1)}, u32[]{:S(2)}, u32[]{:S(2)}) %all-to-all-start.2) | async-done | bytes 262176 | tf_op jit(solution)/shard_map/all_to_all | solution.py:35
  82.0 0.3 fusion.6
  82.4 17.5 %all_to_all.31 = bf16[32,2,2,1,8,128]{5,4,2,3,1,0:T(8,128)(2,1)S(1)} all-to-all(bf16[32,2,2,1,8,128]{5,4,2,3,1,0:T(8,128)(2,1)S(1)} %bitcast.280), channel_id=1, replica_groups=mesh['z'=8,'x'=4,'y'=4,'c'=2] {'z','x'}, dimensions={0} | all-to-all | bytes 524288 | tf_op jit(solution)/shard_map/all_to_all | solution.py:40
  99.9 0.8 fusion.32
  100.7 1.8 copy.92
  102.5 1.1 copy.94
  103.6 1.2 fusion.14
  105.1 3.2 %fusion = bf16[4096,512]{0,1:T(8,128)(2,1)} fusion(bf16[256,512]{0,1:T(8,128)(2,1)S(1)} %bitcast.277, bf16[256,4096]{1,0:T(8,128)(2,1)S(1)} %copy-done), kind=kOutput, calls=%fused_computation.2 | convolution fusion | flops 1075838976 | bytes 6553600 | tf_op jit(solution)/shard_map/dot_general | solution.py:81
  108.5 6.0 %convolution_convert_fusion.4 = bf16[256,4,2,512]{3,0,2,1:T(8,128)(2,1)} fusion(bf16[256,768,1,1]{0,1,3,2:T(8,128)(2,1)S(1)} %bitcast.285, bf16[4,2,512,768]{3,2,1,0:T(8,128)(2,1)} %bitcast.289), kind=kOutput, calls=%fused_computation.9 | convolution fusion | flops 1611661312 | bytes 8781824 | tf_op jit(solution)/shard_map/tk,ycwk->cytw/dot_general | solution.py:164
  114.5 1.3 dynamic-slice_bitcast_fusion
  115.8 0.3 collective-permute-start
  116.1 2.7 %collective-permute-done = bf16[4,256,512]{2,1,0:T(8,128)(2,1)} collective-permute-done((bf16[4,256,512]{2,1,0:T(8,128)(2,1)S(1)}, bf16[4,256,512]{2,1,0:T(8,128)(2,1)}, u32[]{:S(2)}, u32[]{:S(2)}) %collective-permute-start) | collective-permute-done | bytes 1048608 | tf_op jit(solution)/shard_map/ppermute | solution.py:60
  118.8 1.9 %fusion.2 = bf16[4,256,512]{2,1,0:T(8,128)(2,1)S(1)} fusion(bf16[4,256,512]{2,1,0:T(8,128)(2,1)} %collective-permute-done, bf16[256,4,2,512]{3,0,2,1:T(8,128)(2,1)} %convolution_convert_fusion.4, s32[]{:T(128)S(6)} %select_n.71), kind=kLoop, calls=%fused_computation.8 | loop fusion | flops 2097152 | bytes 3145732 | tf_op jit(solution)/shard_map/convert_element_type | solution.py:61
  120.7 0.7 dynamic-slice_bitcast_fusion.8
  121.4 1.4 collective-permute-start.1
  122.8 4.5 %collective-permute-done.1 = bf16[128,512]{1,0:T(8,128)(2,1)} collective-permute-done((bf16[128,512]{1,0:T(8,128)(2,1)}, bf16[128,512]{1,0:T(8,128)(2,1)}, u32[]{:S(2)}, u32[]{:S(2)}) %collective-permute-start.1) | collective-permute-done | bytes 131104 | tf_op jit(solution)/shard_map/ppermute | solution.py:73
  127.3 1.6 fusion.30
  128.9 1.4 collective-permute-start.2
  130.3 0.6 collective-permute-start.4
  130.9 3.3 %collective-permute-done.2 = bf16[128,512]{1,0:T(8,128)(2,1)} collective-permute-done((bf16[128,512]{1,0:T(8,128)(2,1)}, bf16[128,512]{1,0:T(8,128)(2,1)}, u32[]{:S(2)}, u32[]{:S(2)}) %collective-permute-start.2) | collective-permute-done | bytes 131104 | tf_op jit(solution)/shard_map/ppermute | solution.py:73
  134.2 1.6 fusion.29
  135.8 1.4 collective-permute-start.3
  137.2 5.0 %collective-permute-done.3 = bf16[128,512]{1,0:T(8,128)(2,1)} collective-permute-done((bf16[128,512]{1,0:T(8,128)(2,1)}, bf16[128,512]{1,0:T(8,128)(2,1)}, u32[]{:S(2)}, u32[]{:S(2)}) %collective-permute-start.3) | collective-permute-done | bytes 131104 | tf_op jit(solution)/shard_map/ppermute | solution.py:73
  142.2 1.0 fusion.28
  143.2 3.3 %collective-permute-start.5 = (bf16[128,512]{1,0:T(8,128)(2,1)S(1)}, bf16[128,512]{1,0:T(8,128)(2,1)S(1)}, u32[]{:S(2)}, u32[]{:S(2)}) collective-permute-start(bf16[128,512]{1,0:T(8,128)(2,1)S(1)} %get-tuple-element.23), channel_id=1, source_target_pairs={{0,6},{2,0},{4,2},{6,4},{1,7},{3,1},{5,3},{7,5},{8,14},{10,8},{12,... | collective-permute-start | bytes 393224 | tf_op jit(solution)/shard_map/ppermute | solution.py:74
  146.5 2.5 %collective-permute-done.5 = bf16[128,512]{1,0:T(8,128)(2,1)S(1)} collective-permute-done((bf16[128,512]{1,0:T(8,128)(2,1)S(1)}, bf16[128,512]{1,0:T(8,128)(2,1)S(1)}, u32[]{:S(2)}, u32[]{:S(2)}) %collective-permute-start.5) | collective-permute-done | bytes 131104 | tf_op jit(solution)/shard_map/ppermute | solution.py:74
  149.0 0.7 fusion.26
  149.7 2.4 %collective-permute-start.6 = (bf16[128,512]{1,0:T(8,128)(2,1)}, bf16[128,512]{1,0:T(8,128)(2,1)}, u32[]{:S(2)}, u32[]{:S(2)}) collective-permute-start(bf16[128,512]{1,0:T(8,128)(2,1)} %fusion.26), channel_id=1, source_target_pairs={{0,6},{2,0},{4,2},{6,4},{1,7},{3,1},{5,3},{7,5},{8,14},{10,8},{12,... | collective-permute-start | bytes 393224 | tf_op jit(solution)/shard_map/ppermute | solution.py:74
  152.2 1.7 copy_bitcast_fusion.1
  153.9 4.0 %all-to-all-start.4 = ((bf16[4,128,256]{1,2,0:T(8,128)(2,1)}), bf16[4,128,256]{1,2,0:T(8,128)(2,1)}, u32[]{:S(2)}, u32[]{:S(2)}) async-start(bf16[4,128,256]{1,2,0:T(8,128)(2,1)} %copy_bitcast_fusion.1), calls=%async_computation.5 | async-start | bytes 524288 | tf_op jit(solution)/shard_map/all_to_all | solution.py:93
  157.9 0.9 fusion.25
  158.9 0.7 pad_maximum_fusion.1
  159.6 5.0 %all-to-all-done.4 = bf16[4,128,256]{1,2,0:T(8,128)(2,1)} async-done(((bf16[4,128,256]{1,2,0:T(8,128)(2,1)}), bf16[4,128,256]{1,2,0:T(8,128)(2,1)}, u32[]{:S(2)}, u32[]{:S(2)}) %all-to-all-start.4) | async-done | bytes 262176 | tf_op jit(solution)/shard_map/all_to_all | solution.py:93
  164.7 1.0 reduce_sum.64
  165.7 1.9 %copy_bitcast_fusion = bf16[4,128,512]{1,2,0:T(8,128)(2,1)} fusion(bf16[512,512]{0,1:T(8,128)(2,1)} %reduce-scatter.5.cloned.1.call-done), kind=kLoop, calls=%fused_computation.34 | loop fusion | bytes 1048576 | tf_op jit(solution)/shard_map/reshape | solution.py:92
  167.6 3.5 %all-to-all-start.5 = ((bf16[4,128,512]{1,2,0:T(8,128)(2,1)}), bf16[4,128,512]{1,2,0:T(8,128)(2,1)S(1)}, u32[]{:S(2)}, u32[]{:S(2)}) async-start(bf16[4,128,512]{1,2,0:T(8,128)(2,1)} %copy_bitcast_fusion), calls=%async_computation.7 | async-start | bytes 1048576 | tf_op jit(solution)/shard_map/all_to_all | solution.py:93
  171.3 1.1 fusion.10
  172.4 0.8 copy.102
  173.2 5.9 %all-to-all-done.5 = bf16[4,128,512]{1,2,0:T(8,128)(2,1)S(1)} async-done(((bf16[4,128,512]{1,2,0:T(8,128)(2,1)}), bf16[4,128,512]{1,2,0:T(8,128)(2,1)S(1)}, u32[]{:S(2)}, u32[]{:S(2)}) %all-to-all-start.5) | async-done | bytes 524320 | tf_op jit(solution)/shard_map/all_to_all | solution.py:93
  179.2 0.8 copy.103
  (66 shorter events, 2.5 us)
Async XLA Ops:
  7.2 1.6 copy-start
  13.3 24.5 %copy-start.16 = (s32[1,32]{1,0:T(1,128)S(1)}, s32[1,32]{1,0:T(1,128)}, u32[]{:S(2)}) copy-start(s32[1,32]{1,0:T(1,128)} %param.7) | copy-start | bytes 388
  13.5 25.3 %copy-start.1 = (bf16[256,768]{0,1:T(8,128)(2,1)}, bf16[256,768]{0,1:T(8,128)(2,1)S(1)}, u32[]{:S(2)}) copy-start(bf16[256,768]{0,1:T(8,128)(2,1)S(1)} %copy.66) | copy-start | bytes 1179652
  38.9 16.5 %all-to-all-start.1 = ((bf16[32,2,2,1,8,128]{5,4,2,3,1,0:T(8,128)(2,1)}), bf16[32,2,2,1,8,128]{5,4,2,3,1,0:T(8,128)(2,1)}, u32[]{:S(2)}, u32[]{:S(2)}) async-start(bf16[32,2,2,1,8,128]{5,4,2,3,1,0:T(8,128)(2,1)} %bitcast.16), calls=%async_computation.1 | async-start | bytes 524288 | tf_op jit(solution)/shard_map/all_to_all | solution.py:40
  43.5 108.7 %reduce-scatter.3.cloned.1.call-start = ((), (), s32[]{:S(2)}) async-start(), calls=%async_computation.8 | async-start | bytes 2359296 | tf_op jit(solution)/shard_map/reduce_scatter | solution.py:87
  44.3 2.5 %copy-start.12 = (s32[2,256,16]{1,2,0:T(8,128)}, s32[2,256,16]{1,2,0:T(8,128)S(1)}, u32[]{:S(2)}) copy-start(s32[2,256,16]{1,2,0:T(8,128)S(1)} %get-tuple-element.35) | copy-start | bytes 98308
  44.3 2.5 %copy-start.14 = (s32[2,256,16]{1,2,0:T(8,128)}, s32[2,256,16]{1,2,0:T(8,128)S(1)}, u32[]{:S(2)}) copy-start(s32[2,256,16]{1,2,0:T(8,128)S(1)} %get-tuple-element.36) | copy-start | bytes 98308
  55.4 1.5 copy-start.11
  56.4 3.2 %copy-start.9 = (bf16[32,2,2,1,8,128]{5,4,0,2,3,1:T(8,128)(2,1)}, bf16[32,2,2,1,8,128]{5,4,0,2,3,1:T(8,128)(2,1)S(1)}, u32[]{:S(2)}) copy-start(bf16[32,2,2,1,8,128]{5,4,0,2,3,1:T(8,128)(2,1)S(1)} %copy.146) | copy-start | bytes 786436
  56.7 0.8 copy-start.13
  56.7 0.8 copy-start.15
  58.7 0.7 copy-start.3
  58.7 0.9 copy-start.5
  62.0 0.9 copy-start.6
  62.0 1.2 copy-start.7
  64.1 17.9 %all-to-all-start.2 = ((bf16[32,2,2,1,8,128]{5,4,2,1,3,0:T(8,128)(2,1)}), bf16[32,2,2,1,8,128]{5,4,2,1,3,0:T(8,128)(2,1)S(1)}, u32[]{:S(2)}, u32[]{:S(2)}) async-start(bf16[32,2,2,1,8,128]{5,4,2,1,3,0:T(8,128)(2,1)} %copy_bitcast_fusion.2), calls=%async_computation.2 | async-start | bytes 524288 | tf_op jit(solution)/shard_map/all_to_all | solution.py:35
  68.0 35.6 %copy-start.4 = (bf16[2,256,256]{1,2,0:T(8,128)(2,1)S(1)}, bf16[2,256,256]{1,2,0:T(8,128)(2,1)}, u32[]{:S(2)}) copy-start(bf16[2,256,256]{1,2,0:T(8,128)(2,1)} %copy-done.3) | copy-start | bytes 786436
  68.0 97.7 %reduce-scatter.5.cloned.1.call-start = ((), (), s32[]{:S(2)}) async-start(), calls=%async_computation.9 | async-start | bytes 4718592 | tf_op jit(solution)/shard_map/reduce_scatter | solution.py:160
  82.3 22.5 %copy-start.2 = (bf16[2,256,256]{1,2,0:T(8,128)(2,1)S(1)}, bf16[2,256,256]{1,2,0:T(8,128)(2,1)}, u32[]{:S(2)}) copy-start(bf16[2,256,256]{1,2,0:T(8,128)(2,1)} %get-tuple-element.37) | copy-start | bytes 786436
  115.8 3.1 %collective-permute-start = (bf16[4,256,512]{2,1,0:T(8,128)(2,1)S(1)}, bf16[4,256,512]{2,1,0:T(8,128)(2,1)}, u32[]{:S(2)}, u32[]{:S(2)}) collective-permute-start(bf16[4,256,512]{2,1,0:T(8,128)(2,1)S(1)} %dynamic-slice_bitcast_fusion), channel_id=1, source_target_pairs={{0,1},{1,0},{2,3},{3,2},{4,5},{5,4},{6,7},{7,6},{8,9},{9,8},{10,11... | collective-permute-start | bytes 3145736 | tf_op jit(solution)/shard_map/ppermute | solution.py:60
  121.4 5.9 %collective-permute-start.1 = (bf16[128,512]{1,0:T(8,128)(2,1)}, bf16[128,512]{1,0:T(8,128)(2,1)}, u32[]{:S(2)}, u32[]{:S(2)}) collective-permute-start(bf16[128,512]{1,0:T(8,128)(2,1)} %get-tuple-element.24), channel_id=1, source_target_pairs={{0,2},{2,4},{4,6},{6,0},{1,3},{3,5},{5,7},{7,1},{8,10},{10,12},{12... | collective-permute-start | bytes 393224 | tf_op jit(solution)/shard_map/ppermute | solution.py:73
  128.9 5.3 %collective-permute-start.2 = (bf16[128,512]{1,0:T(8,128)(2,1)}, bf16[128,512]{1,0:T(8,128)(2,1)}, u32[]{:S(2)}, u32[]{:S(2)}) collective-permute-start(bf16[128,512]{1,0:T(8,128)(2,1)} %fusion.30), channel_id=1, source_target_pairs={{0,2},{2,4},{4,6},{6,0},{1,3},{3,5},{5,7},{7,1},{8,10},{10,12},{12... | collective-permute-start | bytes 393224 | tf_op jit(solution)/shard_map/ppermute | solution.py:73
  130.3 6.9 %collective-permute-start.4 = (bf16[128,512]{1,0:T(8,128)(2,1)S(1)}, bf16[128,512]{1,0:T(8,128)(2,1)}, u32[]{:S(2)}, u32[]{:S(2)}) collective-permute-start(bf16[128,512]{1,0:T(8,128)(2,1)S(1)} %get-tuple-element.25), channel_id=1, source_target_pairs={{0,6},{2,0},{4,2},{6,4},{1,7},{3,1},{5,3},{7,5},{8,14},{10,8},{12,... | collective-permute-start | bytes 393224 | tf_op jit(solution)/shard_map/ppermute | solution.py:74
  135.8 6.4 %collective-permute-start.3 = (bf16[128,512]{1,0:T(8,128)(2,1)}, bf16[128,512]{1,0:T(8,128)(2,1)}, u32[]{:S(2)}, u32[]{:S(2)}) collective-permute-start(bf16[128,512]{1,0:T(8,128)(2,1)} %fusion.29), channel_id=1, source_target_pairs={{0,2},{2,4},{4,6},{6,0},{1,3},{3,5},{5,7},{7,1},{8,10},{10,12},{12... | collective-permute-start | bytes 393224 | tf_op jit(solution)/shard_map/ppermute | solution.py:73
  143.2 5.8 %collective-permute-start.5 = (bf16[128,512]{1,0:T(8,128)(2,1)S(1)}, bf16[128,512]{1,0:T(8,128)(2,1)S(1)}, u32[]{:S(2)}, u32[]{:S(2)}) collective-permute-start(bf16[128,512]{1,0:T(8,128)(2,1)S(1)} %get-tuple-element.23), channel_id=1, source_target_pairs={{0,6},{2,0},{4,2},{6,4},{1,7},{3,1},{5,3},{7,5},{8,14},{10,8},{12,... | collective-permute-start | bytes 393224 | tf_op jit(solution)/shard_map/ppermute | solution.py:74
  149.7 8.2 %collective-permute-start.6 = (bf16[128,512]{1,0:T(8,128)(2,1)}, bf16[128,512]{1,0:T(8,128)(2,1)}, u32[]{:S(2)}, u32[]{:S(2)}) collective-permute-start(bf16[128,512]{1,0:T(8,128)(2,1)} %fusion.26), channel_id=1, source_target_pairs={{0,6},{2,0},{4,2},{6,4},{1,7},{3,1},{5,3},{7,5},{8,14},{10,8},{12,... | collective-permute-start | bytes 393224 | tf_op jit(solution)/shard_map/ppermute | solution.py:74
  153.9 10.8 %all-to-all-start.4 = ((bf16[4,128,256]{1,2,0:T(8,128)(2,1)}), bf16[4,128,256]{1,2,0:T(8,128)(2,1)}, u32[]{:S(2)}, u32[]{:S(2)}) async-start(bf16[4,128,256]{1,2,0:T(8,128)(2,1)} %copy_bitcast_fusion.1), calls=%async_computation.5 | async-start | bytes 524288 | tf_op jit(solution)/shard_map/all_to_all | solution.py:93
  158.9 12.2 %copy-start.8 = (bf16[2,256,256]{1,2,0:T(8,128)(2,1)S(1)}, bf16[2,256,256]{1,2,0:T(8,128)(2,1)}, u32[]{:S(2)}) copy-start(bf16[2,256,256]{1,2,0:T(8,128)(2,1)} %get-tuple-element.29) | copy-start | bytes 786436
  158.9 12.2 %copy-start.10 = (bf16[32,2,2,1,8,128]{5,4,0,2,3,1:T(8,128)(2,1)S(1)}, bf16[32,2,2,1,8,128]{5,4,0,2,3,1:T(8,128)(2,1)}, u32[]{:S(2)}) copy-start(bf16[32,2,2,1,8,128]{5,4,0,2,3,1:T(8,128)(2,1)} %copy-done.9) | copy-start | bytes 786436
  167.6 11.5 %all-to-all-start.5 = ((bf16[4,128,512]{1,2,0:T(8,128)(2,1)}), bf16[4,128,512]{1,2,0:T(8,128)(2,1)S(1)}, u32[]{:S(2)}, u32[]{:S(2)}) async-start(bf16[4,128,512]{1,2,0:T(8,128)(2,1)} %copy_bitcast_fusion), calls=%async_computation.7 | async-start | bytes 1048576 | tf_op jit(solution)/shard_map/all_to_all | solution.py:93
Sparse Core Ops, SparseCore 0:
  62.1 43.2 reduce-scatter.2
  108.5 54.4 reduce-scatter.4

commit v9 on v8

--- a/solution.py
+++ b/solution.py
@@ -92,6 +92,17 @@
     pieces = part.reshape((n_x, part.shape[0] // n_x) + part.shape[1:])
     gathered = lax.all_to_all(pieces, "x", 0, 0, tiled=True)
     return jnp.sum(gathered.astype(jnp.float32), 0).astype(part.dtype)
+
+
+def reduce_x_then_z(part):
+    n_x = lax.psum(1, "x")
+    n_z = lax.psum(1, "z")
+    rows = part.shape[0] // (n_x * n_z)
+    pieces = part.reshape(n_z, n_x, rows, part.shape[1]).transpose(1, 0, 2, 3)
+    got = lax.all_to_all(pieces, "x", 0, 0, tiled=True)
+    summed = jnp.sum(got.astype(jnp.float32), 0).astype(part.dtype)
+    got = lax.all_to_all(summed, "z", 0, 0, tiled=True)
+    return jnp.sum(got.astype(jnp.float32), 0).astype(part.dtype)
 
 
 def per_device(activations, w_qkv, matching, dropout_bits, out_grad):
@@ -157,15 +168,18 @@
     kv_cols = jnp.stack([grad_key, grad_value], 3).transpose(1, 2, 0, 3, 4)
     kv_cols = kv_cols.reshape(local_tokens, head_count * 2 * HD)
     weight_q = reduce_ctx(weight_term(activations, query_cols))
-    weight_kv = lax.psum_scatter(weight_term(activations, kv_cols), "z", scatter_dimension=0, tiled=True)
+    kv_part = weight_term(activations, kv_cols)
+    side = kv_part.shape[1] // 4
+    weight_side = reduce_x_then_z(kv_part[:, -side:])
+    weight_kv = lax.psum_scatter(kv_part[:, :-side], "z", scatter_dimension=0, tiled=True)
     n_y = lax.psum(1, "y")
     width = activations.shape[1] // (2 * n_y)
     w_split = w_qkv.reshape(n_y, 2, width, w_qkv.shape[1])
     by_core = jnp.einsum("tk,ycwk->cytw", grad_qkv, w_split, preferred_element_type=f32)
     core_sum = ring_rs(by_core.astype(jnp.bfloat16), "c", 2)
     input_grad = ring_rs(core_sum, "y", n_y)
-    input_grad, weight_q, weight_kv = lax.optimization_barrier((input_grad, weight_q, weight_kv))
-    weight_kv = reduce_x(weight_kv)
+    weight_side, weight_q, weight_kv = lax.optimization_barrier((weight_side, weight_q, weight_kv))
+    weight_kv = jnp.concatenate([reduce_x(weight_kv), weight_side], 1)
     rows = weight_q.shape[0]
     weight_grad = jnp.concatenate(
         [weight_q.reshape(rows, head_count, 1, HD), weight_kv.reshape(rows, head_count, 2, HD)], 2

time: 188 us -> 202 us (1.074)
  local copies, waits for them, and re-layouts: 18.7 us -> 29.8 us
  waiting for transfers between devices: 49.6 us -> 41.4 us
  other arithmetic: 13.7 us -> 19.7 us
  starting transfers between devices: 26.9 us -> 32.3 us
    ppermute x3, waiting for transfers between devices: 12.7 us -> 4.14 us  [ring_rs(): got_a = lax.ppermute(acc_a, axis, cw)]
    all_to_all x0 -> x2, waiting for transfers between devices: none -> 8.39 us  [the longest x1 5.21 us: reduce_x_then_z(): got = lax.all_to_all(summed, 'z', 0, 0, tiled=True)]
    all_to_all x0 -> x2, starting transfers between devices: none -> 8.3 us  [the longest x1 4.25 us: reduce_x_then_z(): got = lax.all_to_all(pieces, 'x', 0, 0, tiled=True)]
    reshape x0 -> x2, local copies, waits for them, and re-layouts: none -> 3.9 us  [reduce_x_then_z(): pieces = part.reshape(n_z, n_x, rows, part.shape[1]).transpose(1, 0, 2, 3)]
    reduce_sum x0 -> x2, other arithmetic: none -> 3.76 us  [the longest x1 2.16 us: reduce_x_then_z(): summed = jnp.sum(got.astype(jnp.float32), 0).astype(part.dtype)]
    unnamed x40 -> x42, local copies, waits for them, and re-layouts: 6.1 us -> 9.37 us
    ppermute x1, waiting for transfers between devices: 2.75 us -> 0.01 us  [ring_rs(): got = lax.ppermute(other, axis, [(0, 1), (1, 0)])]
    all_to_all x2, waiting for transfers between devices: 11 us -> 8.25 us  [reduce_x(): gathered = lax.all_to_all(pieces, 'x', 0, 0, tiled=True)]
  transfers between devices with their start and end apart: 13 -> 15, of which waited for: 9 -> 7; matrix products, arithmetic and copies ran while one was open for 19% -> 24% of each run, Pallas kernels for 0% -> 0%
where the time goes in v9:
time: 202 us; the launch traced here: 200 us
  blocking collectives  41.4 us (20%)
  waiting for transfers between devices  41.4 us (20%)
  starting transfers between devices  32.3 us (16%)
  local copies, waits for them, and re-layouts  29.8 us (15%)
  matrix products  20.5 us (10%)
  other arithmetic  19.7 us (10%)
  between operations  14.6 us (7%)
    all_to_all x1, blocking collectives, route(): spread = lax.all_to_all(payload, CTX, 0, 0, tiled=True)  23.9 us
    all_to_all x1, blocking collectives, route(): return lax.all_to_all(chosen.reshape(spread.shape), CTX, 0, 0, tiled=True)  17.4 us
    all_to_all x1, waiting for transfers between devices, route(): spread = lax.all_to_all(payload, CTX, 0, 0, tiled=True)  13.2 us
    unnamed x42, local copies, waits for them, and re-layouts  9.37 us
    all_to_all x2, waiting for transfers between devices, reduce_x(): gathered = lax.all_to_all(pieces, 'x', 0, 0, tiled=True)  8.25 us
    dot_general x12, matrix products, mm(): return jnp.einsum(form, left, right, preferred_element_type=f32)  7.41 us
    all_to_all x1, waiting for transfers between devices, route(): return lax.all_to_all(chosen.reshape(spread.shape), CTX, 0, 0, tiled=True)  7.38 us
    all_to_all x2, starting transfers between devices, reduce_x(): gathered = lax.all_to_all(pieces, 'x', 0, 0, tiled=True)  6.87 us
  transfers between devices with their start and end apart: 15, of which 7 were waited for; matrix products, arithmetic and copies ran while one was open for 24% of the time, Pallas kernels for 0%

profile of v9, /device:TPU:8, one launch (start us, length us, event | category | flops | bytes accessed | tf_op | source)
XLA Modules:
  0.0 199.6 jit_solution(4926908301060128904)
XLA Ops:
  7.2 1.6 copy-done
  8.8 4.6 %convolution_convert_fusion.5 = bf16[256,768]{1,0:T(8,128)(2,1)S(1)} fusion(bf16[256,4096]{1,0:T(8,128)(2,1)S(1)} %copy-done, bf16[4096,768]{1,0:T(8,128)(2,1)} %param.6), kind=kOutput, calls=%fused_computation.10 | convolution fusion | flops 1610809344 | bytes 8781824 | tf_op jit(solution)/shard_map/dot_general | solution.py:114
  13.9 23.9 %all_to_all.40 = bf16[32,2,2,1,8,128]{5,4,2,3,1,0:T(8,128)(2,1)S(1)} all-to-all(bf16[32,2,2,1,8,128]{5,4,2,3,1,0:T(8,128)(2,1)S(1)} %copy.111), channel_id=1, replica_groups=mesh['z'=8,'x'=4,'y'=4,'c'=2] {'z','x'}, dimensions={0} | all-to-all | bytes 524288 | tf_op jit(solution)/shard_map/all_to_all | solution.py:35
  38.1 0.7 copy.173
  38.9 4.6 %all-to-all-start.1 = ((bf16[32,2,2,1,8,128]{5,4,2,3,1,0:T(8,128)(2,1)}), bf16[32,2,2,1,8,128]{5,4,2,3,1,0:T(8,128)(2,1)}, u32[]{:S(2)}, u32[]{:S(2)}) async-start(bf16[32,2,2,1,8,128]{5,4,2,3,1,0:T(8,128)(2,1)} %bitcast.16), calls=%async_computation.1 | async-start | bytes 524288 | tf_op jit(solution)/shard_map/all_to_all | solution.py:40
  43.5 0.8 slice_bitcast_fusion.10
  44.5 1.0 copy.162
  45.6 1.0 fusion.20
  46.8 1.2 fusion.4
  48.0 7.4 %all-to-all-done.1 = bf16[32,2,2,1,8,128]{5,4,2,3,1,0:T(8,128)(2,1)} async-done(((bf16[32,2,2,1,8,128]{5,4,2,3,1,0:T(8,128)(2,1)}), bf16[32,2,2,1,8,128]{5,4,2,3,1,0:T(8,128)(2,1)}, u32[]{:S(2)}, u32[]{:S(2)}) %all-to-all-start.1) | async-done | bytes 262176 | tf_op jit(solution)/shard_map/all_to_all | solution.py:40
  55.4 1.1 copy.192
  57.5 1.2 multiply_convert_fusion
  58.7 0.7 copy-done.5
  59.9 2.1 %fusion.1 = bf16[4096,256]{0,1:T(8,128)(2,1)} fusion(bf16[256,256]{0,1:T(8,128)(2,1)S(1)} %bitcast.278, bf16[256,4096]{1,0:T(8,128)(2,1)S(1)} %copy-done), kind=kOutput, calls=%fused_computation.4 | convolution fusion | flops 537919488 | bytes 4325376 | tf_op jit(solution)/shard_map/dot_general | solution.py:81
  62.0 0.9 copy-done.8
  63.4 0.7 copy_bitcast_fusion.3
  64.2 3.9 %all-to-all-start.2 = ((bf16[32,2,2,1,8,128]{5,4,2,1,3,0:T(8,128)(2,1)}), bf16[32,2,2,1,8,128]{5,4,2,1,3,0:T(8,128)(2,1)S(1)}, u32[]{:S(2)}, u32[]{:S(2)}) async-start(bf16[32,2,2,1,8,128]{5,4,2,1,3,0:T(8,128)(2,1)} %copy_bitcast_fusion.3), calls=%async_computation.2 | async-start | bytes 524288 | tf_op jit(solution)/shard_map/all_to_all | solution.py:35
  68.8 13.2 %all-to-all-done.2 = bf16[32,2,2,1,8,128]{5,4,2,1,3,0:T(8,128)(2,1)S(1)} async-done(((bf16[32,2,2,1,8,128]{5,4,2,1,3,0:T(8,128)(2,1)}), bf16[32,2,2,1,8,128]{5,4,2,1,3,0:T(8,128)(2,1)S(1)}, u32[]{:S(2)}, u32[]{:S(2)}) %all-to-all-start.2) | async-done | bytes 262176 | tf_op jit(solution)/shard_map/all_to_all | solution.py:35
  82.4 17.4 %all_to_all.41 = bf16[32,2,2,1,8,128]{5,4,2,3,1,0:T(8,128)(2,1)S(1)} all-to-all(bf16[32,2,2,1,8,128]{5,4,2,3,1,0:T(8,128)(2,1)S(1)} %bitcast.284), channel_id=1, replica_groups=mesh['z'=8,'x'=4,'y'=4,'c'=2] {'z','x'}, dimensions={0} | all-to-all | bytes 524288 | tf_op jit(solution)/shard_map/all_to_all | solution.py:40
  99.9 0.8 fusion.32
  100.7 1.1 copy.134
  101.8 1.8 copy.132
  103.6 1.2 fusion.14
  105.1 1.3 fusion
  106.4 1.9 copy-done.1
  108.3 2.0 %slice.104 = bf16[4096,384]{0,1:T(8,128)(2,1)} slice(bf16[4096,512]{0,1:T(8,128)(2,1)S(1)} %fusion), slice={[0:4096], [0:384]} | slice | bytes 6291456 | tf_op jit(solution)/shard_map/slice | solution.py:174
  110.5 4.6 %convolution_convert_fusion.4 = bf16[256,4,2,512]{3,0,2,1:T(8,128)(2,1)S(1)} fusion(bf16[256,768,1,1]{0,1,3,2:T(8,128)(2,1)S(1)} %bitcast.289, bf16[4,2,512,768]{3,2,1,0:T(8,128)(2,1)} %bitcast.293), kind=kOutput, calls=%fused_computation.9 | convolution fusion | flops 1611661312 | bytes 8781824 | tf_op jit(solution)/shard_map/tk,ycwk->cytw/dot_general | solution.py:178
  115.1 1.3 copy-done.12
  116.4 1.1 dynamic-slice_bitcast_fusion
  118.0 1.6 reshape.370
  119.6 2.3 %copy.190 = bf16[8,4,128,128]{2,0,3,1:T(8,128)(2,1)} copy(bf16[8,4,128,128]{2,1,0,3:T(4,128)(2,1)} %reshape.370) | data formatting | bytes 2097152 | tf_op jit(solution)/shard_map/reshape | solution.py:101
  121.9 4.2 %all-to-all-start.4 = ((bf16[4,8,128,128]{2,1,3,0:T(8,128)(2,1)}), bf16[4,8,128,128]{2,1,3,0:T(8,128)(2,1)}, u32[]{:S(2)}, u32[]{:S(2)}) async-start(bf16[4,8,128,128]{2,1,3,0:T(8,128)(2,1)} %bitcast.263), calls=%async_computation.4 | async-start | bytes 2097152 | tf_op jit(solution)/shard_map/all_to_all | solution.py:102
  126.2 1.9 fusion.2
  128.1 0.7 dynamic-slice_bitcast_fusion.8
  128.8 1.4 collective-permute-start.1
  130.2 4.1 %collective-permute-done.1 = bf16[128,512]{1,0:T(8,128)(2,1)} collective-permute-done((bf16[128,512]{1,0:T(8,128)(2,1)S(1)}, bf16[128,512]{1,0:T(8,128)(2,1)}, u32[]{:S(2)}, u32[]{:S(2)}) %collective-permute-start.1) | collective-permute-done | bytes 131104 | tf_op jit(solution)/shard_map/ppermute | solution.py:73
  134.3 0.9 fusion.30
  135.2 1.5 collective-permute-start.2
  136.7 1.9 fusion.42
  138.6 3.2 %all-to-all-done.4 = bf16[4,8,128,128]{2,1,3,0:T(8,128)(2,1)} async-done(((bf16[4,8,128,128]{2,1,3,0:T(8,128)(2,1)}), bf16[4,8,128,128]{2,1,3,0:T(8,128)(2,1)}, u32[]{:S(2)}, u32[]{:S(2)}) %all-to-all-start.4) | async-done | bytes 1048608 | tf_op jit(solution)/shard_map/all_to_all | solution.py:102
  141.8 2.2 %reduce_sum.88 = bf16[8,128,128]{1,0,2:T(8,128)(2,1)} reduce(bf16[4,8,128,128]{2,1,3,0:T(8,128)(2,1)} %all-to-all-done.4, bf16[]{:T(256)} %constant.109.clone.1), dimensions={0}, to_apply=%region_7.0 | reduce | flops 393216 | bytes 1310722 | tf_op jit(solution)/shard_map/reduce_sum | solution.py:103
  144.0 1.7 copy.141
  145.7 4.0 %all-to-all-start.5 = ((bf16[8,128,128]{1,2,0:T(8,128)(2,1)}), bf16[8,128,128]{1,2,0:T(8,128)(2,1)}, u32[]{:S(2)}, u32[]{:S(2)}) async-start(bf16[8,128,128]{1,2,0:T(8,128)(2,1)} %copy.141), calls=%async_computation.5 | async-start | bytes 524288 | tf_op jit(solution)/shard_map/all_to_all | solution.py:104
  149.7 0.8 collective-permute-start.4
  150.6 1.6 fusion.29
  152.2 1.3 collective-permute-start.3
  153.4 1.2 fusion.10
  154.7 0.8 copy.145
  155.4 5.2 %all-to-all-done.5 = bf16[8,128,128]{1,2,0:T(8,128)(2,1)} async-done(((bf16[8,128,128]{1,2,0:T(8,128)(2,1)}), bf16[8,128,128]{1,2,0:T(8,128)(2,1)}, u32[]{:S(2)}, u32[]{:S(2)}) %all-to-all-start.5) | async-done | bytes 262176 | tf_op jit(solution)/shard_map/all_to_all | solution.py:104
  160.6 1.6 reduce_sum.89
  162.2 1.7 fusion.28
  164.0 1.1 collective-permute-start.5
  165.1 1.7 copy_bitcast_fusion.2
  166.8 3.4 %all-to-all-start.6 = ((bf16[4,128,256]{1,2,0:T(8,128)(2,1)}), bf16[4,128,256]{1,2,0:T(8,128)(2,1)S(1)}, u32[]{:S(2)}, u32[]{:S(2)}) async-start(bf16[4,128,256]{1,2,0:T(8,128)(2,1)} %copy_bitcast_fusion.2), calls=%async_computation.7 | async-start | bytes 524288 | tf_op jit(solution)/shard_map/all_to_all | solution.py:93
  170.9 2.5 %collective-permute-start.6 = (bf16[128,512]{1,0:T(8,128)(2,1)}, bf16[128,512]{1,0:T(8,128)(2,1)}, u32[]{:S(2)}, u32[]{:S(2)}) collective-permute-start(bf16[128,512]{1,0:T(8,128)(2,1)} %fusion.26), channel_id=1, source_target_pairs={{0,6},{2,0},{4,2},{6,4},{1,7},{3,1},{5,3},{7,5},{8,14},{10,8},{12,... | collective-permute-start | bytes 393224 | tf_op jit(solution)/shard_map/ppermute | solution.py:74
  173.4 3.5 %all-to-all-done.6 = bf16[4,128,256]{1,2,0:T(8,128)(2,1)S(1)} async-done(((bf16[4,128,256]{1,2,0:T(8,128)(2,1)}), bf16[4,128,256]{1,2,0:T(8,128)(2,1)S(1)}, u32[]{:S(2)}, u32[]{:S(2)}) %all-to-all-start.6) | async-done | bytes 262176 | tf_op jit(solution)/shard_map/all_to_all | solution.py:93
  177.6 1.8 copy_bitcast_fusion.1
  179.4 3.5 %all-to-all-start.7 = ((bf16[4,128,384]{1,2,0:T(8,128)(2,1)}), bf16[4,128,384]{1,2,0:T(8,128)(2,1)S(1)}, u32[]{:S(2)}, u32[]{:S(2)}) async-start(bf16[4,128,384]{1,2,0:T(8,128)(2,1)} %copy_bitcast_fusion.1), calls=%async_computation.9 | async-start | bytes 786432 | tf_op jit(solution)/shard_map/all_to_all | solution.py:93
  182.9 0.9 fusion.25
  183.8 1.6 pad_maximum_fusion.1
  185.4 4.8 %all-to-all-done.7 = bf16[4,128,384]{1,2,0:T(8,128)(2,1)S(1)} async-done(((bf16[4,128,384]{1,2,0:T(8,128)(2,1)}), bf16[4,128,384]{1,2,0:T(8,128)(2,1)S(1)}, u32[]{:S(2)}, u32[]{:S(2)}) %all-to-all-start.7) | async-done | bytes 393248 | tf_op jit(solution)/shard_map/all_to_all | solution.py:93
  190.2 0.8 pad_maximum_fusion.3
  191.0 0.9 pad_maximum_fusion.2
  191.9 0.8 copy.146
  (81 shorter events, 6.6 us)
Async XLA Ops:
  7.2 1.6 copy-start
  13.3 24.5 %copy-start.17 = (s32[1,32]{1,0:T(1,128)S(1)}, s32[1,32]{1,0:T(1,128)}, u32[]{:S(2)}) copy-start(s32[1,32]{1,0:T(1,128)} %param.7) | copy-start | bytes 388
  13.5 25.3 %copy-start.2 = (bf16[256,768]{0,1:T(8,128)(2,1)}, bf16[256,768]{0,1:T(8,128)(2,1)S(1)}, u32[]{:S(2)}) copy-start(bf16[256,768]{0,1:T(8,128)(2,1)S(1)} %copy.106) | copy-start | bytes 1179652
  38.9 16.5 %all-to-all-start.1 = ((bf16[32,2,2,1,8,128]{5,4,2,3,1,0:T(8,128)(2,1)}), bf16[32,2,2,1,8,128]{5,4,2,3,1,0:T(8,128)(2,1)}, u32[]{:S(2)}, u32[]{:S(2)}) async-start(bf16[32,2,2,1,8,128]{5,4,2,3,1,0:T(8,128)(2,1)} %bitcast.16), calls=%async_computation.1 | async-start | bytes 524288 | tf_op jit(solution)/shard_map/all_to_all | solution.py:40
  43.5 121.7 %reduce-scatter.3.cloned.1.call-start = ((), (), s32[]{:S(2)}) async-start(), calls=%async_computation.10 | async-start | bytes 2359296 | tf_op jit(solution)/shard_map/reduce_scatter | solution.py:87
  44.3 1.2 copy-start.13
  44.3 1.2 copy-start.15
  55.4 1.5 copy-start.11
  56.4 3.2 %copy-start.10 = (bf16[32,2,2,1,8,128]{5,4,0,2,3,1:T(8,128)(2,1)}, bf16[32,2,2,1,8,128]{5,4,0,2,3,1:T(8,128)(2,1)S(1)}, u32[]{:S(2)}) copy-start(bf16[32,2,2,1,8,128]{5,4,0,2,3,1:T(8,128)(2,1)S(1)} %copy.192) | copy-start | bytes 786436
  56.7 0.8 copy-start.14
  56.7 0.8 copy-start.16
  58.7 0.7 copy-start.5
  58.7 0.9 copy-start.7
  62.0 0.9 copy-start.8
  62.0 1.2 copy-start.9
  64.2 17.9 %all-to-all-start.2 = ((bf16[32,2,2,1,8,128]{5,4,2,1,3,0:T(8,128)(2,1)}), bf16[32,2,2,1,8,128]{5,4,2,1,3,0:T(8,128)(2,1)S(1)}, u32[]{:S(2)}, u32[]{:S(2)}) async-start(bf16[32,2,2,1,8,128]{5,4,2,1,3,0:T(8,128)(2,1)} %copy_bitcast_fusion.3), calls=%async_computation.2 | async-start | bytes 524288 | tf_op jit(solution)/shard_map/all_to_all | solution.py:35
  68.0 35.5 %copy-start.6 = (bf16[2,256,256]{1,2,0:T(8,128)(2,1)S(1)}, bf16[2,256,256]{1,2,0:T(8,128)(2,1)}, u32[]{:S(2)}) copy-start(bf16[2,256,256]{1,2,0:T(8,128)(2,1)} %copy-done.5) | copy-start | bytes 786436
  68.1 109.5 %reduce-scatter.5.cloned.1.call-start = ((), (), s32[]{:S(2)}) async-start(), calls=%async_computation.11 | async-start | bytes 3538944 | tf_op jit(solution)/shard_map/reduce_scatter | solution.py:174
  82.3 22.5 %copy-start.3 = (bf16[2,256,256]{1,2,0:T(8,128)(2,1)S(1)}, bf16[2,256,256]{1,2,0:T(8,128)(2,1)}, u32[]{:S(2)}) copy-start(bf16[2,256,256]{1,2,0:T(8,128)(2,1)} %get-tuple-element.40) | copy-start | bytes 786436
  106.3 2.0 copy-start.1
  115.1 1.3 copy-start.12
  116.4 1.6 slice-start
  117.5 8.7 %collective-permute-start = (bf16[4,256,512]{2,1,0:T(8,128)(2,1)}, bf16[4,256,512]{2,1,0:T(8,128)(2,1)}, u32[]{:S(2)}, u32[]{:S(2)}) collective-permute-start(bf16[4,256,512]{2,1,0:T(8,128)(2,1)} %dynamic-slice_bitcast_fusion), channel_id=1, source_target_pairs={{0,1},{1,0},{2,3},{3,2},{4,5},{5,4},{6,7},{7,6},{8,9},{9,8},{10,11... | collective-permute-start | bytes 3145736 | tf_op jit(solution)/shard_map/ppermute | solution.py:60
  121.9 19.9 %all-to-all-start.4 = ((bf16[4,8,128,128]{2,1,3,0:T(8,128)(2,1)}), bf16[4,8,128,128]{2,1,3,0:T(8,128)(2,1)}, u32[]{:S(2)}, u32[]{:S(2)}) async-start(bf16[4,8,128,128]{2,1,3,0:T(8,128)(2,1)} %bitcast.263), calls=%async_computation.4 | async-start | bytes 2097152 | tf_op jit(solution)/shard_map/all_to_all | solution.py:102
  128.1 25.4 %copy-start.4 = (bf16[2,256,256]{1,2,0:T(8,128)(2,1)S(1)}, bf16[2,256,256]{1,2,0:T(8,128)(2,1)}, u32[]{:S(2)}) copy-start(bf16[2,256,256]{1,2,0:T(8,128)(2,1)} %get-tuple-element.40) | copy-start | bytes 786436
  128.8 5.5 %collective-permute-start.1 = (bf16[128,512]{1,0:T(8,128)(2,1)S(1)}, bf16[128,512]{1,0:T(8,128)(2,1)}, u32[]{:S(2)}, u32[]{:S(2)}) collective-permute-start(bf16[128,512]{1,0:T(8,128)(2,1)S(1)} %get-tuple-element.27), channel_id=1, source_target_pairs={{0,2},{2,4},{4,6},{6,0},{1,3},{3,5},{5,7},{7,1},{8,10},{10,12},{12... | collective-permute-start | bytes 393224 | tf_op jit(solution)/shard_map/ppermute | solution.py:73
  135.2 15.3 %collective-permute-start.2 = (bf16[128,512]{1,0:T(8,128)(2,1)S(1)}, bf16[128,512]{1,0:T(8,128)(2,1)}, u32[]{:S(2)}, u32[]{:S(2)}) collective-permute-start(bf16[128,512]{1,0:T(8,128)(2,1)S(1)} %fusion.30), channel_id=1, source_target_pairs={{0,2},{2,4},{4,6},{6,0},{1,3},{3,5},{5,7},{7,1},{8,10},{10,12},{12... | collective-permute-start | bytes 393224 | tf_op jit(solution)/shard_map/ppermute | solution.py:73
  145.7 14.9 %all-to-all-start.5 = ((bf16[8,128,128]{1,2,0:T(8,128)(2,1)}), bf16[8,128,128]{1,2,0:T(8,128)(2,1)}, u32[]{:S(2)}, u32[]{:S(2)}) async-start(bf16[8,128,128]{1,2,0:T(8,128)(2,1)} %copy.141), calls=%async_computation.5 | async-start | bytes 524288 | tf_op jit(solution)/shard_map/all_to_all | solution.py:104
  149.7 12.5 %collective-permute-start.4 = (bf16[128,512]{1,0:T(8,128)(2,1)}, bf16[128,512]{1,0:T(8,128)(2,1)}, u32[]{:S(2)}, u32[]{:S(2)}) collective-permute-start(bf16[128,512]{1,0:T(8,128)(2,1)} %get-tuple-element.28), channel_id=1, source_target_pairs={{0,6},{2,0},{4,2},{6,4},{1,7},{3,1},{5,3},{7,5},{8,14},{10,8},{12,... | collective-permute-start | bytes 393224 | tf_op jit(solution)/shard_map/ppermute | solution.py:74
  152.2 10.1 %collective-permute-start.3 = (bf16[128,512]{1,0:T(8,128)(2,1)}, bf16[128,512]{1,0:T(8,128)(2,1)}, u32[]{:S(2)}, u32[]{:S(2)}) collective-permute-start(bf16[128,512]{1,0:T(8,128)(2,1)} %fusion.29), channel_id=1, source_target_pairs={{0,2},{2,4},{4,6},{6,0},{1,3},{3,5},{5,7},{7,1},{8,10},{10,12},{12... | collective-permute-start | bytes 393224 | tf_op jit(solution)/shard_map/ppermute | solution.py:73
  164.0 6.3 %collective-permute-start.5 = (bf16[128,512]{1,0:T(8,128)(2,1)}, bf16[128,512]{1,0:T(8,128)(2,1)S(1)}, u32[]{:S(2)}, u32[]{:S(2)}) collective-permute-start(bf16[128,512]{1,0:T(8,128)(2,1)} %get-tuple-element.26), channel_id=1, source_target_pairs={{0,6},{2,0},{4,2},{6,4},{1,7},{3,1},{5,3},{7,5},{8,14},{10,8},{12,... | collective-permute-start | bytes 393224 | tf_op jit(solution)/shard_map/ppermute | solution.py:74
  166.8 10.1 %all-to-all-start.6 = ((bf16[4,128,256]{1,2,0:T(8,128)(2,1)}), bf16[4,128,256]{1,2,0:T(8,128)(2,1)S(1)}, u32[]{:S(2)}, u32[]{:S(2)}) async-start(bf16[4,128,256]{1,2,0:T(8,128)(2,1)} %copy_bitcast_fusion.2), calls=%async_computation.7 | async-start | bytes 524288 | tf_op jit(solution)/shard_map/all_to_all | solution.py:93
  170.9 11.9 %collective-permute-start.6 = (bf16[128,512]{1,0:T(8,128)(2,1)}, bf16[128,512]{1,0:T(8,128)(2,1)}, u32[]{:S(2)}, u32[]{:S(2)}) collective-permute-start(bf16[128,512]{1,0:T(8,128)(2,1)} %fusion.26), channel_id=1, source_target_pairs={{0,6},{2,0},{4,2},{6,4},{1,7},{3,1},{5,3},{7,5},{8,14},{10,8},{12,... | collective-permute-start | bytes 393224 | tf_op jit(solution)/shard_map/ppermute | solution.py:74
  179.4 10.8 %all-to-all-start.7 = ((bf16[4,128,384]{1,2,0:T(8,128)(2,1)}), bf16[4,128,384]{1,2,0:T(8,128)(2,1)S(1)}, u32[]{:S(2)}, u32[]{:S(2)}) async-start(bf16[4,128,384]{1,2,0:T(8,128)(2,1)} %copy_bitcast_fusion.1), calls=%async_computation.9 | async-start | bytes 786432 | tf_op jit(solution)/shard_map/all_to_all | solution.py:93
Sparse Core Ops, SparseCore 0:
  62.2 43.1 reduce-scatter.2
  110.5 45.8 reduce-scatter.4

commit v10 on v8

--- a/solution.py
+++ b/solution.py
@@ -89,9 +89,13 @@
 
 def reduce_x(part):
     n_x = lax.psum(1, "x")
+    i = lax.axis_index("x")
     pieces = part.reshape((n_x, part.shape[0] // n_x) + part.shape[1:])
-    gathered = lax.all_to_all(pieces, "x", 0, 0, tiled=True)
-    return jnp.sum(gathered.astype(jnp.float32), 0).astype(part.dtype)
+    total = lax.dynamic_index_in_dim(pieces, i, 0, keepdims=False).astype(jnp.float32)
+    for s in range(1, n_x):
+        outgoing = lax.dynamic_index_in_dim(pieces, (i + s) % n_x, 0, keepdims=False)
+        total = total + lax.ppermute(outgoing, "x", [(j, (j + s) % n_x) for j in range(n_x)]).astype(jnp.float32)
+    return total.astype(part.dtype)
 
 
 def per_device(activations, w_qkv, matching, dropout_bits, out_grad):

time: 188 us -> 189 us (level)
    all_to_all x2 -> x0, waiting for transfers between devices: 11 us -> none  [reduce_x(): gathered = lax.all_to_all(pieces, 'x', 0, 0, tiled=True)]
    ppermute x0 -> x6, waiting for transfers between devices: none -> 8.32 us  [reduce_x(): lax.ppermute(outgoing, 'x', [(j, (j + s) % n_x) for j in range(n_x)])]
    all_to_all x2 -> x0, starting transfers between devices: 7.51 us -> none  [reduce_x(): gathered = lax.all_to_all(pieces, 'x', 0, 0, tiled=True)]
    ppermute x0 -> x6, starting transfers between devices: none -> 6.97 us  [reduce_x(): lax.ppermute(outgoing, 'x', [(j, (j + s) % n_x) for j in range(n_x)])]
    unnamed x40 -> x38, local copies, waits for them, and re-layouts: 6.1 us -> 6.09 us
  transfers between devices with their start and end apart: 13 -> 17, of which waited for: 9 -> 13; matrix products, arithmetic and copies ran while one was open for 19% -> 20% of each run, Pallas kernels for 0% -> 0%
where the time goes in v10:
time: 189 us; the launch traced here: 187 us
  waiting for transfers between devices  48 us (25%)
  blocking collectives  41.5 us (22%)
  starting transfers between devices  26.6 us (14%)
  matrix products  23.7 us (13%)
  local copies, waits for them, and re-layouts  18.4 us (10%)
  between operations  14.6 us (8%)
  other arithmetic  13.8 us (7%)
    all_to_all x1, blocking collectives, route(): spread = lax.all_to_all(payload, CTX, 0, 0, tiled=True)  23.9 us
    all_to_all x1, blocking collectives, route(): return lax.all_to_all(chosen.reshape(spread.shape), CTX, 0, 0, tiled=True)  17.6 us
    all_to_all x1, waiting for transfers between devices, route(): spread = lax.all_to_all(payload, CTX, 0, 0, tiled=True)  13.2 us
    ppermute x3, waiting for transfers between devices, ring_rs(): got_a = lax.ppermute(acc_a, axis, cw)  12.3 us
    ppermute x6, waiting for transfers between devices, reduce_x(): lax.ppermute(outgoing, 'x', [(j, (j + s) % n_x) for j in range(n_x)])  8.32 us
    all_to_all x1, waiting for transfers between devices, route(): return lax.all_to_all(chosen.reshape(spread.shape), CTX, 0, 0, tiled=True)  7.38 us
    dot_general x12, matrix products, mm(): return jnp.einsum(form, left, right, preferred_element_type=f32)  7.3 us
    ppermute x6, starting transfers between devices, reduce_x(): lax.ppermute(outgoing, 'x', [(j, (j + s) % n_x) for j in range(n_x)])  6.97 us
  transfers between devices with their start and end apart: 17, of which 13 were waited for; matrix products, arithmetic and copies ran while one was open for 20% of the time, Pallas kernels for 0%

profile of v10, /device:TPU:8, one launch (start us, length us, event | category | flops | bytes accessed | tf_op | source)
XLA Modules:
  0.0 186.6 jit_solution(12080606986829701043)
XLA Ops:
  7.2 1.6 copy-done
  8.8 4.6 %convolution_convert_fusion.5 = bf16[256,768]{1,0:T(8,128)(2,1)S(1)} fusion(bf16[256,4096]{1,0:T(8,128)(2,1)S(1)} %copy-done, bf16[4096,768]{1,0:T(8,128)(2,1)} %param.6), kind=kOutput, calls=%fused_computation.10 | convolution fusion | flops 1610809344 | bytes 8781824 | tf_op jit(solution)/shard_map/dot_general | solution.py:107
  13.9 23.9 %all_to_all.20 = bf16[32,2,2,1,8,128]{5,4,2,3,1,0:T(8,128)(2,1)S(1)} all-to-all(bf16[32,2,2,1,8,128]{5,4,2,3,1,0:T(8,128)(2,1)S(1)} %copy.82), channel_id=1, replica_groups=mesh['z'=8,'x'=4,'y'=4,'c'=2] {'z','x'}, dimensions={0} | all-to-all | bytes 524288 | tf_op jit(solution)/shard_map/all_to_all | solution.py:35
  37.8 0.3 fusion.5
  38.1 0.7 copy.149
  38.9 4.6 %all-to-all-start.1 = ((bf16[32,2,2,1,8,128]{5,4,2,3,1,0:T(8,128)(2,1)}), bf16[32,2,2,1,8,128]{5,4,2,3,1,0:T(8,128)(2,1)}, u32[]{:S(2)}, u32[]{:S(2)}) async-start(bf16[32,2,2,1,8,128]{5,4,2,3,1,0:T(8,128)(2,1)} %bitcast.16), calls=%async_computation.1 | async-start | bytes 524288 | tf_op jit(solution)/shard_map/all_to_all | solution.py:40
  43.5 0.8 slice_bitcast_fusion.10
  44.4 1.0 copy.137
  45.5 1.0 fusion.20
  46.8 1.2 fusion.4
  48.0 7.4 %all-to-all-done.1 = bf16[32,2,2,1,8,128]{5,4,2,3,1,0:T(8,128)(2,1)} async-done(((bf16[32,2,2,1,8,128]{5,4,2,3,1,0:T(8,128)(2,1)}), bf16[32,2,2,1,8,128]{5,4,2,3,1,0:T(8,128)(2,1)}, u32[]{:S(2)}, u32[]{:S(2)}) %all-to-all-start.1) | async-done | bytes 262176 | tf_op jit(solution)/shard_map/all_to_all | solution.py:40
  55.4 1.1 copy.164
  56.9 0.3 multiply_reduce_fusion
  57.5 1.2 multiply_convert_fusion
  58.7 0.7 copy-done.3
  59.9 2.1 %fusion.1 = bf16[4096,256]{0,1:T(8,128)(2,1)} fusion(bf16[256,256]{0,1:T(8,128)(2,1)S(1)} %bitcast.284, bf16[256,4096]{1,0:T(8,128)(2,1)S(1)} %copy-done), kind=kOutput, calls=%fused_computation.4 | convolution fusion | flops 537919488 | bytes 4325376 | tf_op jit(solution)/shard_map/dot_general | solution.py:81
  62.0 0.9 copy-done.6
  63.4 0.8 copy_bitcast_fusion
  64.1 3.9 %all-to-all-start.2 = ((bf16[32,2,2,1,8,128]{5,4,2,1,3,0:T(8,128)(2,1)}), bf16[32,2,2,1,8,128]{5,4,2,1,3,0:T(8,128)(2,1)S(1)}, u32[]{:S(2)}, u32[]{:S(2)}) async-start(bf16[32,2,2,1,8,128]{5,4,2,1,3,0:T(8,128)(2,1)} %copy_bitcast_fusion), calls=%async_computation.2 | async-start | bytes 524288 | tf_op jit(solution)/shard_map/all_to_all | solution.py:35
  68.1 0.7 scatter_custom_fusion
  68.8 13.2 %all-to-all-done.2 = bf16[32,2,2,1,8,128]{5,4,2,1,3,0:T(8,128)(2,1)S(1)} async-done(((bf16[32,2,2,1,8,128]{5,4,2,1,3,0:T(8,128)(2,1)}), bf16[32,2,2,1,8,128]{5,4,2,1,3,0:T(8,128)(2,1)S(1)}, u32[]{:S(2)}, u32[]{:S(2)}) %all-to-all-start.2) | async-done | bytes 262176 | tf_op jit(solution)/shard_map/all_to_all | solution.py:35
  82.3 17.6 %all_to_all.21 = bf16[32,2,2,1,8,128]{5,4,2,3,1,0:T(8,128)(2,1)S(1)} all-to-all(bf16[32,2,2,1,8,128]{5,4,2,3,1,0:T(8,128)(2,1)S(1)} %bitcast.292), channel_id=1, replica_groups=mesh['z'=8,'x'=4,'y'=4,'c'=2] {'z','x'}, dimensions={0} | all-to-all | bytes 524288 | tf_op jit(solution)/shard_map/all_to_all | solution.py:40
  100.0 0.8 fusion.35
  100.8 1.8 copy.103
  102.6 1.1 copy.105
  103.7 1.2 fusion.14
  105.2 3.2 %fusion = bf16[4096,512]{0,1:T(8,128)(2,1)} fusion(bf16[256,512]{0,1:T(8,128)(2,1)S(1)} %bitcast.287, bf16[256,4096]{1,0:T(8,128)(2,1)S(1)} %copy-done), kind=kOutput, calls=%fused_computation.2 | convolution fusion | flops 1075838976 | bytes 6553600 | tf_op jit(solution)/shard_map/dot_general | solution.py:81
  108.5 6.0 %convolution_convert_fusion.4 = bf16[256,4,2,512]{3,0,2,1:T(8,128)(2,1)} fusion(bf16[256,768,1,1]{0,1,3,2:T(8,128)(2,1)S(1)} %bitcast.297, bf16[4,2,512,768]{3,2,1,0:T(8,128)(2,1)} %bitcast.301), kind=kOutput, calls=%fused_computation.9 | convolution fusion | flops 1611661312 | bytes 8781824 | tf_op jit(solution)/shard_map/tk,ycwk->cytw/dot_general | solution.py:168
  114.5 1.3 dynamic-slice_bitcast_fusion
  115.8 0.3 collective-permute-start
  116.2 2.7 %collective-permute-done = bf16[4,256,512]{2,1,0:T(8,128)(2,1)} collective-permute-done((bf16[4,256,512]{2,1,0:T(8,128)(2,1)S(1)}, bf16[4,256,512]{2,1,0:T(8,128)(2,1)}, u32[]{:S(2)}, u32[]{:S(2)}) %collective-permute-start) | collective-permute-done | bytes 1048608 | tf_op jit(solution)/shard_map/ppermute | solution.py:60
  118.9 1.9 %fusion.2 = bf16[4,256,512]{2,1,0:T(8,128)(2,1)S(1)} fusion(bf16[4,256,512]{2,1,0:T(8,128)(2,1)} %collective-permute-done, bf16[256,4,2,512]{3,0,2,1:T(8,128)(2,1)} %convolution_convert_fusion.4, s32[]{:T(128)S(6)} %select_n.107), kind=kLoop, calls=%fused_computation.8 | loop fusion | flops 2097152 | bytes 3145732 | tf_op jit(solution)/shard_map/convert_element_type | solution.py:61
  120.8 0.7 dynamic-slice_bitcast_fusion.8
  121.5 1.5 collective-permute-start.1
  123.0 4.3 %collective-permute-done.1 = bf16[128,512]{1,0:T(8,128)(2,1)} collective-permute-done((bf16[128,512]{1,0:T(8,128)(2,1)}, bf16[128,512]{1,0:T(8,128)(2,1)}, u32[]{:S(2)}, u32[]{:S(2)}) %collective-permute-start.1) | collective-permute-done | bytes 131104 | tf_op jit(solution)/shard_map/ppermute | solution.py:73
  127.3 1.6 fusion.33
  128.9 1.6 collective-permute-start.2
  130.5 0.5 collective-permute-start.4
  130.9 3.3 %collective-permute-done.2 = bf16[128,512]{1,0:T(8,128)(2,1)} collective-permute-done((bf16[128,512]{1,0:T(8,128)(2,1)}, bf16[128,512]{1,0:T(8,128)(2,1)}, u32[]{:S(2)}, u32[]{:S(2)}) %collective-permute-start.2) | collective-permute-done | bytes 131104 | tf_op jit(solution)/shard_map/ppermute | solution.py:73
  134.2 1.6 fusion.32
  135.8 1.6 collective-permute-start.3
  137.4 4.7 %collective-permute-done.3 = bf16[128,512]{1,0:T(8,128)(2,1)} collective-permute-done((bf16[128,512]{1,0:T(8,128)(2,1)}, bf16[128,512]{1,0:T(8,128)(2,1)}, u32[]{:S(2)}, u32[]{:S(2)}) %collective-permute-start.3) | collective-permute-done | bytes 131104 | tf_op jit(solution)/shard_map/ppermute | solution.py:73
  142.1 1.7 fusion.31
  143.8 3.2 %collective-permute-start.5 = (bf16[128,512]{1,0:T(8,128)(2,1)}, bf16[128,512]{1,0:T(8,128)(2,1)S(1)}, u32[]{:S(2)}, u32[]{:S(2)}) collective-permute-start(bf16[128,512]{1,0:T(8,128)(2,1)} %get-tuple-element.23), channel_id=1, source_target_pairs={{0,6},{2,0},{4,2},{6,4},{1,7},{3,1},{5,3},{7,5},{8,14},{10,8},{12,... | collective-permute-start | bytes 393224 | tf_op jit(solution)/shard_map/ppermute | solution.py:74
  147.0 3.3 %collective-permute-done.5 = bf16[128,512]{1,0:T(8,128)(2,1)S(1)} collective-permute-done((bf16[128,512]{1,0:T(8,128)(2,1)}, bf16[128,512]{1,0:T(8,128)(2,1)S(1)}, u32[]{:S(2)}, u32[]{:S(2)}) %collective-permute-start.5) | collective-permute-done | bytes 131104 | tf_op jit(solution)/shard_map/ppermute | solution.py:74
  150.4 2.5 %collective-permute-start.6 = (bf16[128,512]{1,0:T(8,128)(2,1)S(1)}, bf16[128,512]{1,0:T(8,128)(2,1)S(1)}, u32[]{:S(2)}, u32[]{:S(2)}) collective-permute-start(bf16[128,512]{1,0:T(8,128)(2,1)S(1)} %fusion.29), channel_id=1, source_target_pairs={{0,6},{2,0},{4,2},{6,4},{1,7},{3,1},{5,3},{7,5},{8,14},{10,8},{12,... | collective-permute-start | bytes 393224 | tf_op jit(solution)/shard_map/ppermute | solution.py:74
  152.9 1.9 %fusion.48 = f32[2,256,128]{1,2,0:T(8,128)} fusion(bf16[2,256,256]{1,2,0:T(8,128)(2,1)} %get-tuple-element.29, bf16[2,2,1,32,8,128]{5,4,3,1,2,0:T(8,128)(2,1)} %bitcast.280), kind=kOutput, calls=%fused_computation.111 | convolution fusion | flops 33554432 | bytes 655360 | tf_op jit(solution)/shard_map/hnqk,hnkd->hnqd/dot_general | solution.py:119
  154.8 0.7 collective-permute-done.6
  155.5 1.1 copy.142
  156.7 0.3 collective-permute-start.7
  157.0 3.0 %collective-permute-start.9 = (bf16[128,256]{1,0:T(8,128)(2,1)S(1)}, bf16[128,256]{1,0:T(8,128)(2,1)S(1)}, u32[]{:S(2)}, u32[]{:S(2)}) collective-permute-start(bf16[128,256]{1,0:T(8,128)(2,1)S(1)} %get-tuple-element.37), channel_id=1, source_target_pairs={{0,24},{8,0},{16,8},{24,16},{1,25},{9,1},{17,9},{25,17},{2,26},{10... | collective-permute-start | bytes 196616 | tf_op jit(solution)/shard_map/ppermute | solution.py:97
  160.0 0.4 collective-permute-start.8
  160.4 1.6 pad_maximum_fusion.1
  162.3 3.5 %collective-permute-done.8 = bf16[128,256]{1,0:T(8,128)(2,1)S(1)} collective-permute-done((bf16[128,256]{1,0:T(8,128)(2,1)S(1)}, bf16[128,256]{1,0:T(8,128)(2,1)S(1)}, u32[]{:S(2)}, u32[]{:S(2)}) %collective-permute-start.8) | collective-permute-done | bytes 65568 | tf_op jit(solution)/shard_map/ppermute | solution.py:97
  165.9 1.3 copy.143
  167.1 0.7 dynamic-slice_bitcast_fusion.11
  167.8 3.2 %collective-permute-start.12 = (bf16[128,512]{1,0:T(8,128)(2,1)}, bf16[128,512]{1,0:T(8,128)(2,1)}, u32[]{:S(2)}, u32[]{:S(2)}) collective-permute-start(bf16[128,512]{1,0:T(8,128)(2,1)} %get-tuple-element.31), channel_id=1, source_target_pairs={{0,24},{8,0},{16,8},{24,16},{1,25},{9,1},{17,9},{25,17},{2,26},{10... | collective-permute-start | bytes 393224 | tf_op jit(solution)/shard_map/ppermute | solution.py:97
  171.1 1.1 fusion.10
  172.2 0.8 copy.120
  173.1 1.9 %collective-permute-done.10 = bf16[128,512]{1,0:T(8,128)(2,1)} collective-permute-done((bf16[128,512]{1,0:T(8,128)(2,1)}, bf16[128,512]{1,0:T(8,128)(2,1)}, u32[]{:S(2)}, u32[]{:S(2)}) %collective-permute-start.10) | collective-permute-done | bytes 131104 | tf_op jit(solution)/shard_map/ppermute | solution.py:97
  175.0 0.3 collective-permute-done.12
  175.3 2.3 %collective-permute-done.11 = bf16[128,512]{1,0:T(8,128)(2,1)} collective-permute-done((bf16[128,512]{1,0:T(8,128)(2,1)S(1)}, bf16[128,512]{1,0:T(8,128)(2,1)}, u32[]{:S(2)}, u32[]{:S(2)}) %collective-permute-start.11) | collective-permute-done | bytes 131104 | tf_op jit(solution)/shard_map/ppermute | solution.py:97
  177.7 1.1 fusion.27
  178.9 0.8 copy.121
  (76 shorter events, 4.0 us)
Async XLA Ops:
  7.2 1.6 copy-start
  13.3 24.5 %copy-start.15 = (s32[1,32]{1,0:T(1,128)S(1)}, s32[1,32]{1,0:T(1,128)}, u32[]{:S(2)}) copy-start(s32[1,32]{1,0:T(1,128)} %param.7) | copy-start | bytes 388
  13.5 25.3 %copy-start.1 = (bf16[256,768]{0,1:T(8,128)(2,1)}, bf16[256,768]{0,1:T(8,128)(2,1)S(1)}, u32[]{:S(2)}) copy-start(bf16[256,768]{0,1:T(8,128)(2,1)S(1)} %copy.77) | copy-start | bytes 1179652
  38.9 16.5 %all-to-all-start.1 = ((bf16[32,2,2,1,8,128]{5,4,2,3,1,0:T(8,128)(2,1)}), bf16[32,2,2,1,8,128]{5,4,2,3,1,0:T(8,128)(2,1)}, u32[]{:S(2)}, u32[]{:S(2)}) async-start(bf16[32,2,2,1,8,128]{5,4,2,3,1,0:T(8,128)(2,1)} %bitcast.16), calls=%async_computation.1 | async-start | bytes 524288 | tf_op jit(solution)/shard_map/all_to_all | solution.py:40
  43.5 112.1 %reduce-scatter.3.cloned.1.call-start = ((), (), s32[]{:S(2)}) async-start(), calls=%async_computation.6 | async-start | bytes 2359296 | tf_op jit(solution)/shard_map/reduce_scatter | solution.py:87
  44.3 2.5 %copy-start.11 = (s32[2,256,16]{1,2,0:T(8,128)}, s32[2,256,16]{1,2,0:T(8,128)S(1)}, u32[]{:S(2)}) copy-start(s32[2,256,16]{1,2,0:T(8,128)S(1)} %get-tuple-element.41) | copy-start | bytes 98308
  44.3 2.5 %copy-start.13 = (s32[2,256,16]{1,2,0:T(8,128)}, s32[2,256,16]{1,2,0:T(8,128)S(1)}, u32[]{:S(2)}) copy-start(s32[2,256,16]{1,2,0:T(8,128)S(1)} %get-tuple-element.42) | copy-start | bytes 98308
  55.4 1.5 copy-start.9
  56.4 3.5 %copy-start.8 = (bf16[32,2,2,1,8,128]{5,4,0,2,3,1:T(8,128)(2,1)}, bf16[32,2,2,1,8,128]{5,4,0,2,3,1:T(8,128)(2,1)S(1)}, u32[]{:S(2)}) copy-start(bf16[32,2,2,1,8,128]{5,4,0,2,3,1:T(8,128)(2,1)S(1)} %copy.164) | copy-start | bytes 786436
  56.7 0.8 copy-start.12
  56.7 0.8 copy-start.14
  58.7 0.7 copy-start.3
  58.7 0.9 copy-start.5
  62.0 0.9 copy-start.6
  62.0 1.2 copy-start.7
  64.1 17.9 %all-to-all-start.2 = ((bf16[32,2,2,1,8,128]{5,4,2,1,3,0:T(8,128)(2,1)}), bf16[32,2,2,1,8,128]{5,4,2,1,3,0:T(8,128)(2,1)S(1)}, u32[]{:S(2)}, u32[]{:S(2)}) async-start(bf16[32,2,2,1,8,128]{5,4,2,1,3,0:T(8,128)(2,1)} %copy_bitcast_fusion), calls=%async_computation.2 | async-start | bytes 524288 | tf_op jit(solution)/shard_map/all_to_all | solution.py:35
  68.0 35.7 %copy-start.4 = (bf16[2,256,256]{1,2,0:T(8,128)(2,1)S(1)}, bf16[2,256,256]{1,2,0:T(8,128)(2,1)}, u32[]{:S(2)}) copy-start(bf16[2,256,256]{1,2,0:T(8,128)(2,1)} %copy-done.3) | copy-start | bytes 786436
  68.0 97.8 %reduce-scatter.5.cloned.1.call-start = ((), (), s32[]{:S(2)}) async-start(), calls=%async_computation.7 | async-start | bytes 4718592 | tf_op jit(solution)/shard_map/reduce_scatter | solution.py:164
  82.3 22.6 %copy-start.2 = (bf16[2,256,256]{1,2,0:T(8,128)(2,1)S(1)}, bf16[2,256,256]{1,2,0:T(8,128)(2,1)}, u32[]{:S(2)}) copy-start(bf16[2,256,256]{1,2,0:T(8,128)(2,1)} %get-tuple-element.43) | copy-start | bytes 786436
  115.8 3.1 %collective-permute-start = (bf16[4,256,512]{2,1,0:T(8,128)(2,1)S(1)}, bf16[4,256,512]{2,1,0:T(8,128)(2,1)}, u32[]{:S(2)}, u32[]{:S(2)}) collective-permute-start(bf16[4,256,512]{2,1,0:T(8,128)(2,1)S(1)} %dynamic-slice_bitcast_fusion), channel_id=1, source_target_pairs={{0,1},{1,0},{2,3},{3,2},{4,5},{5,4},{6,7},{7,6},{8,9},{9,8},{10,11... | collective-permute-start | bytes 3145736 | tf_op jit(solution)/shard_map/ppermute | solution.py:60
  121.5 5.9 %collective-permute-start.1 = (bf16[128,512]{1,0:T(8,128)(2,1)}, bf16[128,512]{1,0:T(8,128)(2,1)}, u32[]{:S(2)}, u32[]{:S(2)}) collective-permute-start(bf16[128,512]{1,0:T(8,128)(2,1)} %get-tuple-element.24), channel_id=1, source_target_pairs={{0,2},{2,4},{4,6},{6,0},{1,3},{3,5},{5,7},{7,1},{8,10},{10,12},{12... | collective-permute-start | bytes 393224 | tf_op jit(solution)/shard_map/ppermute | solution.py:73
  128.9 5.3 %collective-permute-start.2 = (bf16[128,512]{1,0:T(8,128)(2,1)}, bf16[128,512]{1,0:T(8,128)(2,1)}, u32[]{:S(2)}, u32[]{:S(2)}) collective-permute-start(bf16[128,512]{1,0:T(8,128)(2,1)} %fusion.33), channel_id=1, source_target_pairs={{0,2},{2,4},{4,6},{6,0},{1,3},{3,5},{5,7},{7,1},{8,10},{10,12},{12... | collective-permute-start | bytes 393224 | tf_op jit(solution)/shard_map/ppermute | solution.py:73
  130.5 6.9 %collective-permute-start.4 = (bf16[128,512]{1,0:T(8,128)(2,1)S(1)}, bf16[128,512]{1,0:T(8,128)(2,1)}, u32[]{:S(2)}, u32[]{:S(2)}) collective-permute-start(bf16[128,512]{1,0:T(8,128)(2,1)S(1)} %get-tuple-element.25), channel_id=1, source_target_pairs={{0,6},{2,0},{4,2},{6,4},{1,7},{3,1},{5,3},{7,5},{8,14},{10,8},{12,... | collective-permute-start | bytes 393224 | tf_op jit(solution)/shard_map/ppermute | solution.py:74
  135.8 6.3 %collective-permute-start.3 = (bf16[128,512]{1,0:T(8,128)(2,1)}, bf16[128,512]{1,0:T(8,128)(2,1)}, u32[]{:S(2)}, u32[]{:S(2)}) collective-permute-start(bf16[128,512]{1,0:T(8,128)(2,1)} %fusion.32), channel_id=1, source_target_pairs={{0,2},{2,4},{4,6},{6,0},{1,3},{3,5},{5,7},{7,1},{8,10},{10,12},{12... | collective-permute-start | bytes 393224 | tf_op jit(solution)/shard_map/ppermute | solution.py:73
  143.8 6.6 %collective-permute-start.5 = (bf16[128,512]{1,0:T(8,128)(2,1)}, bf16[128,512]{1,0:T(8,128)(2,1)S(1)}, u32[]{:S(2)}, u32[]{:S(2)}) collective-permute-start(bf16[128,512]{1,0:T(8,128)(2,1)} %get-tuple-element.23), channel_id=1, source_target_pairs={{0,6},{2,0},{4,2},{6,4},{1,7},{3,1},{5,3},{7,5},{8,14},{10,8},{12,... | collective-permute-start | bytes 393224 | tf_op jit(solution)/shard_map/ppermute | solution.py:74
  150.4 5.0 %collective-permute-start.6 = (bf16[128,512]{1,0:T(8,128)(2,1)S(1)}, bf16[128,512]{1,0:T(8,128)(2,1)S(1)}, u32[]{:S(2)}, u32[]{:S(2)}) collective-permute-start(bf16[128,512]{1,0:T(8,128)(2,1)S(1)} %fusion.29), channel_id=1, source_target_pairs={{0,6},{2,0},{4,2},{6,4},{1,7},{3,1},{5,3},{7,5},{8,14},{10,8},{12,... | collective-permute-start | bytes 393224 | tf_op jit(solution)/shard_map/ppermute | solution.py:74
  155.5 15.6 %copy-start.10 = (f32[2,256,128]{1,2,0:T(8,128)S(1)}, f32[2,256,128]{1,2,0:T(8,128)}, u32[]{:S(2)}) copy-start(f32[2,256,128]{1,2,0:T(8,128)} %fusion.48) | copy-start | bytes 786436
  156.7 5.6 %collective-permute-start.7 = (bf16[128,256]{1,0:T(8,128)(2,1)S(1)}, bf16[128,256]{1,0:T(8,128)(2,1)S(1)}, u32[]{:S(2)}, u32[]{:S(2)}) collective-permute-start(bf16[128,256]{1,0:T(8,128)(2,1)S(1)} %get-tuple-element.36), channel_id=1, source_target_pairs={{0,8},{8,16},{16,24},{24,0},{1,9},{9,17},{17,25},{25,1},{2,10},{10... | collective-permute-start | bytes 196616 | tf_op jit(solution)/shard_map/ppermute | solution.py:97
  157.0 5.2 %collective-permute-start.9 = (bf16[128,256]{1,0:T(8,128)(2,1)S(1)}, bf16[128,256]{1,0:T(8,128)(2,1)S(1)}, u32[]{:S(2)}, u32[]{:S(2)}) collective-permute-start(bf16[128,256]{1,0:T(8,128)(2,1)S(1)} %get-tuple-element.37), channel_id=1, source_target_pairs={{0,24},{8,0},{16,8},{24,16},{1,25},{9,1},{17,9},{25,17},{2,26},{10... | collective-permute-start | bytes 196616 | tf_op jit(solution)/shard_map/ppermute | solution.py:97
  160.0 5.8 %collective-permute-start.8 = (bf16[128,256]{1,0:T(8,128)(2,1)S(1)}, bf16[128,256]{1,0:T(8,128)(2,1)S(1)}, u32[]{:S(2)}, u32[]{:S(2)}) collective-permute-start(bf16[128,256]{1,0:T(8,128)(2,1)S(1)} %get-tuple-element.38), channel_id=1, source_target_pairs={{0,16},{8,24},{16,0},{24,8},{1,17},{9,25},{17,1},{25,9},{2,18},{10... | collective-permute-start | bytes 196616 | tf_op jit(solution)/shard_map/ppermute | solution.py:97
  167.8 7.1 %collective-permute-start.10 = (bf16[128,512]{1,0:T(8,128)(2,1)}, bf16[128,512]{1,0:T(8,128)(2,1)}, u32[]{:S(2)}, u32[]{:S(2)}) collective-permute-start(bf16[128,512]{1,0:T(8,128)(2,1)} %get-tuple-element.30), channel_id=1, source_target_pairs={{0,8},{8,16},{16,24},{24,0},{1,9},{9,17},{17,25},{25,1},{2,10},{10... | collective-permute-start | bytes 393224 | tf_op jit(solution)/shard_map/ppermute | solution.py:97
  167.8 7.5 %collective-permute-start.12 = (bf16[128,512]{1,0:T(8,128)(2,1)}, bf16[128,512]{1,0:T(8,128)(2,1)}, u32[]{:S(2)}, u32[]{:S(2)}) collective-permute-start(bf16[128,512]{1,0:T(8,128)(2,1)} %get-tuple-element.31), channel_id=1, source_target_pairs={{0,24},{8,0},{16,8},{24,16},{1,25},{9,1},{17,9},{25,17},{2,26},{10... | collective-permute-start | bytes 393224 | tf_op jit(solution)/shard_map/ppermute | solution.py:97
  171.1 6.6 %collective-permute-start.11 = (bf16[128,512]{1,0:T(8,128)(2,1)S(1)}, bf16[128,512]{1,0:T(8,128)(2,1)}, u32[]{:S(2)}, u32[]{:S(2)}) collective-permute-start(bf16[128,512]{1,0:T(8,128)(2,1)S(1)} %get-tuple-element.32), channel_id=1, source_target_pairs={{0,16},{8,24},{16,0},{24,8},{1,17},{9,25},{17,1},{25,9},{2,18},{10... | collective-permute-start | bytes 393224 | tf_op jit(solution)/shard_map/ppermute | solution.py:97
Sparse Core Ops, SparseCore 0:
  62.1 43.2 reduce-scatter.2
  108.5 54.2 reduce-scatter.4

commit v11 on v8

--- a/solution.py
+++ b/solution.py
@@ -100,11 +100,13 @@
     head_count = out_grad.shape[1] // HD
     score_scale = HD ** (-0.5)
     n_ctx = matching.shape[1]
-    projected = jnp.dot(activations, w_qkv, preferred_element_type=f32).astype(jnp.bfloat16)
-    projected = projected.reshape(local_tokens, head_count, 3, HD)
-    query = to_blocks(projected[:, :, 0].reshape(local_tokens, head_count * HD), HD)
-    key_own = to_blocks(projected[:, :, 1].reshape(local_tokens, head_count * HD), HD)
-    value_own = to_blocks(projected[:, :, 2].reshape(local_tokens, head_count * HD), HD)
+    w_heads = w_qkv.reshape(w_qkv.shape[0], head_count, 3, HD)
+    kv_proj = jnp.einsum("tk,khcd->thcd", activations, w_heads[:, :, 1:], preferred_element_type=f32)
+    kv_proj = kv_proj.astype(jnp.bfloat16)
+    key_own = to_blocks(kv_proj[:, :, 0].reshape(local_tokens, head_count * HD), HD)
+    value_own = to_blocks(kv_proj[:, :, 1].reshape(local_tokens, head_count * HD), HD)
+    q_proj = jnp.einsum("tk,khd->thd", activations, w_heads[:, :, 0], preferred_element_type=f32)
+    query = to_blocks(q_proj.astype(jnp.bfloat16).reshape(local_tokens, head_count * HD), HD)
     order = matching[0]
     inverse = jnp.zeros_like(order).at[order].set(jnp.arange(n_ctx, dtype=order.dtype))
     own_kv = jnp.stack([key_own, value_own], 0)

time: 188 us -> 197 us (1.048)
  blocking collectives: 41.4 us -> 17.6 us
  waiting for transfers between devices: 49.6 us -> 63.1 us
  starting transfers between devices: 26.9 us -> 38.9 us
  local copies, waits for them, and re-layouts: 18.7 us -> 24.1 us
    all_to_all x1 -> x0, blocking collectives: 23.9 us -> none  [route(): spread = lax.all_to_all(payload, CTX, 0, 0, tiled=True)]
    all_to_all x1 -> x2, starting transfers between devices: 3.87 us -> 15.2 us  [route(): spread = lax.all_to_all(payload, CTX, 0, 0, tiled=True)]
    all_to_all x1 -> x2, waiting for transfers between devices: 13.2 us -> 23.6 us  [route(): spread = lax.all_to_all(payload, CTX, 0, 0, tiled=True)]
    unnamed x40 -> x51, local copies, waits for them, and re-layouts: 6.1 us -> 15 us
    all_to_all x1, waiting for transfers between devices: 7.39 us -> 9.73 us  [route(): return lax.all_to_all(chosen.reshape(spread.shape), CTX, 0, 0, tiled=True)]
    dot_general x1 -> x2, matrix products: 4.57 us -> 5.85 us  [the longest x1 3.48 us: per_device(): jnp.einsum('tk,khcd->thcd', activations, w_heads[:, :, 1:], preferred_ele...]
  transfers between devices with their start and end apart: 13 -> 14, of which waited for: 9 -> 10; matrix products, arithmetic and copies ran while one was open for 19% -> 17% of each run, Pallas kernels for 0% -> 0%
where the time goes in v11:
time: 197 us; the launch traced here: 196 us
  waiting for transfers between devices  63.1 us (32%)
  starting transfers between devices  38.9 us (20%)
  local copies, waits for them, and re-layouts  24.1 us (12%)
  matrix products  22 us (11%)
  blocking collectives  17.6 us (9%)
  other arithmetic  15.4 us (8%)
  between operations  14.6 us (7%)
    all_to_all x2, waiting for transfers between devices, route(): spread = lax.all_to_all(payload, CTX, 0, 0, tiled=True)  23.6 us
    all_to_all x1, blocking collectives, route(): return lax.all_to_all(chosen.reshape(spread.shape), CTX, 0, 0, tiled=True)  17.6 us
    all_to_all x2, starting transfers between devices, route(): spread = lax.all_to_all(payload, CTX, 0, 0, tiled=True)  15.2 us
    unnamed x51, local copies, waits for them, and re-layouts  15 us
    ppermute x3, waiting for transfers between devices, ring_rs(): got_a = lax.ppermute(acc_a, axis, cw)  12.5 us
    all_to_all x2, waiting for transfers between devices, reduce_x(): gathered = lax.all_to_all(pieces, 'x', 0, 0, tiled=True)  11.9 us
    all_to_all x1, waiting for transfers between devices, route(): return lax.all_to_all(chosen.reshape(spread.shape), CTX, 0, 0, tiled=True)  9.73 us
    all_to_all x2, starting transfers between devices, reduce_x(): gathered = lax.all_to_all(pieces, 'x', 0, 0, tiled=True)  8.17 us
  transfers between devices with their start and end apart: 14, of which 10 were waited for; matrix products, arithmetic and copies ran while one was open for 17% of the time, Pallas kernels for 0%

profile of v11, /device:TPU:8, one launch (start us, length us, event | category | flops | bytes accessed | tf_op | source)
XLA Modules:
  0.0 195.7 jit_solution(6929894962955576947)
XLA Ops:
  7.2 8.9 %copy.62 = bf16[4096,768]{0,1:T(8,128)(2,1)} copy(bf16[4096,768]{1,0:T(8,128)(2,1)} %param.6) | data formatting | bytes 12582912 | tf_op args[1]
  16.1 3.5 %fusion.10 = bf16[256,2,2,128]{3,0,2,1:T(8,128)(2,1)S(1)} fusion(bf16[4096,2,3,128]{0,3,2,1:T(8,128)(2,1)} %bitcast.274, bf16[256,4096]{1,0:T(8,128)(2,1)S(1)} %copy-done), kind=kOutput, calls=%fused_computation.22 | convolution fusion | flops 1073872896 | bytes 6553600 | tf_op jit(solution)/shard_map/tk,khcd->thcd/dot_general | solution.py:104
  19.6 0.8 copy_bitcast_fusion.3
  20.3 11.3 %all-to-all-start = ((bf16[32,2,2,1,8,128]{5,4,2,1,3,0:T(8,128)(2,1)}), bf16[32,2,2,1,8,128]{5,4,2,1,3,0:T(8,128)(2,1)S(1)}, u32[]{:S(2)}, u32[]{:S(2)}) async-start(bf16[32,2,2,1,8,128]{5,4,2,1,3,0:T(8,128)(2,1)} %copy_bitcast_fusion.3), calls=%async_computation | async-start | bytes 524288 | tf_op jit(solution)/shard_map/all_to_all | solution.py:35
  31.7 2.4 %fusion.28 = bf16[2,256,128]{2,1,0:T(8,128)(2,1)S(1)} fusion(bf16[4096,2,3,128]{0,3,2,1:T(8,128)(2,1)} %bitcast.275, bf16[256,4096]{1,0:T(8,128)(2,1)S(1)} %copy-done), kind=kOutput, calls=%fused_computation.40 | convolution fusion | flops 536936448 | bytes 4325376 | tf_op jit(solution)/shard_map/tk,khd->thd/dot_general | solution.py:108
  34.1 10.4 %all-to-all-done = bf16[32,2,2,1,8,128]{5,4,2,1,3,0:T(8,128)(2,1)S(1)} async-done(((bf16[32,2,2,1,8,128]{5,4,2,1,3,0:T(8,128)(2,1)}), bf16[32,2,2,1,8,128]{5,4,2,1,3,0:T(8,128)(2,1)S(1)}, u32[]{:S(2)}, u32[]{:S(2)}) %all-to-all-start) | async-done | bytes 262176 | tf_op jit(solution)/shard_map/all_to_all | solution.py:35
  44.4 0.3 fusion.15
  44.7 0.7 copy.125
  45.5 4.6 %all-to-all-start.1 = ((bf16[32,2,2,1,8,128]{5,4,2,3,1,0:T(8,128)(2,1)}), bf16[32,2,2,1,8,128]{5,4,2,3,1,0:T(8,128)(2,1)}, u32[]{:S(2)}, u32[]{:S(2)}) async-start(bf16[32,2,2,1,8,128]{5,4,2,3,1,0:T(8,128)(2,1)} %bitcast.20), calls=%async_computation.1 | async-start | bytes 524288 | tf_op jit(solution)/shard_map/all_to_all | solution.py:40
  50.4 0.4 copy-done.16
  50.8 1.0 fusion.36
  51.8 0.2 fusion.64
  52.3 9.7 %all-to-all-done.1 = bf16[32,2,2,1,8,128]{5,4,2,3,1,0:T(8,128)(2,1)} async-done(((bf16[32,2,2,1,8,128]{5,4,2,3,1,0:T(8,128)(2,1)}), bf16[32,2,2,1,8,128]{5,4,2,3,1,0:T(8,128)(2,1)}, u32[]{:S(2)}, u32[]{:S(2)}) %all-to-all-start.1) | async-done | bytes 262176 | tf_op jit(solution)/shard_map/all_to_all | solution.py:40
  62.0 1.1 copy.143
  63.1 1.2 fusion.65
  64.5 0.3 multiply_reduce_fusion
  65.1 1.1 multiply_convert_fusion
  66.2 0.7 copy-done.3
  67.4 2.1 %fusion.1 = bf16[4096,256]{0,1:T(8,128)(2,1)} fusion(bf16[256,256]{0,1:T(8,128)(2,1)S(1)} %bitcast.284, bf16[256,4096]{1,0:T(8,128)(2,1)S(1)} %copy-done), kind=kOutput, calls=%fused_computation.4 | convolution fusion | flops 537919488 | bytes 4325376 | tf_op jit(solution)/shard_map/dot_general | solution.py:81
  69.5 0.9 copy-done.6
  70.9 0.7 copy_bitcast_fusion.2
  71.7 3.9 %all-to-all-start.2 = ((bf16[32,2,2,1,8,128]{5,4,2,1,3,0:T(8,128)(2,1)}), bf16[32,2,2,1,8,128]{5,4,2,1,3,0:T(8,128)(2,1)S(1)}, u32[]{:S(2)}, u32[]{:S(2)}) async-start(bf16[32,2,2,1,8,128]{5,4,2,1,3,0:T(8,128)(2,1)} %copy_bitcast_fusion.2), calls=%async_computation.2 | async-start | bytes 524288 | tf_op jit(solution)/shard_map/all_to_all | solution.py:35
  75.6 0.7 scatter_custom_fusion
  76.3 13.2 %all-to-all-done.2 = bf16[32,2,2,1,8,128]{5,4,2,1,3,0:T(8,128)(2,1)S(1)} async-done(((bf16[32,2,2,1,8,128]{5,4,2,1,3,0:T(8,128)(2,1)}), bf16[32,2,2,1,8,128]{5,4,2,1,3,0:T(8,128)(2,1)S(1)}, u32[]{:S(2)}, u32[]{:S(2)}) %all-to-all-start.2) | async-done | bytes 262176 | tf_op jit(solution)/shard_map/all_to_all | solution.py:35
  89.6 0.3 fusion.16
  89.9 17.6 %all_to_all.30 = bf16[32,2,2,1,8,128]{5,4,2,3,1,0:T(8,128)(2,1)S(1)} all-to-all(bf16[32,2,2,1,8,128]{5,4,2,3,1,0:T(8,128)(2,1)S(1)} %bitcast.290), channel_id=1, replica_groups=mesh['z'=8,'x'=4,'y'=4,'c'=2] {'z','x'}, dimensions={0} | all-to-all | bytes 524288 | tf_op jit(solution)/shard_map/all_to_all | solution.py:40
  107.5 0.7 fusion.48
  108.3 1.8 copy.89
  110.1 0.8 copy.87
  110.9 1.2 fusion.27
  112.1 1.2 fusion.26
  113.3 3.2 %fusion = bf16[4096,512]{0,1:T(8,128)(2,1)} fusion(bf16[256,512]{0,1:T(8,128)(2,1)S(1)} %bitcast.287, bf16[256,4096]{1,0:T(8,128)(2,1)S(1)} %copy-done), kind=kOutput, calls=%fused_computation.2 | convolution fusion | flops 1075838976 | bytes 6553600 | tf_op jit(solution)/shard_map/dot_general | solution.py:81
  116.7 4.6 %convolution_convert_fusion.4 = bf16[256,4,2,512]{3,0,2,1:T(8,128)(2,1)S(1)} fusion(bf16[256,768,1,1]{0,1,3,2:T(8,128)(2,1)S(1)} %bitcast.294, bf16[4,2,512,768]{3,2,1,0:T(8,128)(2,1)} %bitcast.273), kind=kOutput, calls=%fused_computation.15 | convolution fusion | flops 1611661312 | bytes 8781824 | tf_op jit(solution)/shard_map/tk,ycwk->cytw/dot_general | solution.py:166
  121.3 1.4 copy-done.13
  122.8 0.3 collective-permute-start
  123.1 2.7 %collective-permute-done = bf16[4,256,512]{2,1,0:T(8,128)(2,1)} collective-permute-done((bf16[4,256,512]{2,1,0:T(8,128)(2,1)S(1)}, bf16[4,256,512]{2,1,0:T(8,128)(2,1)}, u32[]{:S(2)}, u32[]{:S(2)}) %collective-permute-start) | collective-permute-done | bytes 1048608 | tf_op jit(solution)/shard_map/ppermute | solution.py:60
  125.8 2.1 %fusion.5 = bf16[4,256,512]{2,1,0:T(8,128)(2,1)S(1)} fusion(bf16[4,256,512]{2,1,0:T(8,128)(2,1)} %collective-permute-done, bf16[256,4,2,512]{3,0,2,1:T(8,128)(2,1)} %copy-done.13, s32[]{:T(128)S(6)} %select_n.71), kind=kLoop, calls=%fused_computation.12 | loop fusion | flops 2097152 | bytes 3145732 | tf_op jit(solution)/shard_map/convert_element_type | solution.py:61
  127.9 0.7 dynamic-slice_bitcast_fusion.8
  128.6 1.4 collective-permute-start.1
  130.0 4.5 %collective-permute-done.1 = bf16[128,512]{1,0:T(8,128)(2,1)} collective-permute-done((bf16[128,512]{1,0:T(8,128)(2,1)}, bf16[128,512]{1,0:T(8,128)(2,1)}, u32[]{:S(2)}, u32[]{:S(2)}) %collective-permute-start.1) | collective-permute-done | bytes 131104 | tf_op jit(solution)/shard_map/ppermute | solution.py:73
  134.4 1.6 fusion.46
  136.0 1.4 collective-permute-start.2
  137.4 0.6 collective-permute-start.4
  138.1 3.3 %collective-permute-done.2 = bf16[128,512]{1,0:T(8,128)(2,1)} collective-permute-done((bf16[128,512]{1,0:T(8,128)(2,1)}, bf16[128,512]{1,0:T(8,128)(2,1)}, u32[]{:S(2)}, u32[]{:S(2)}) %collective-permute-start.2) | collective-permute-done | bytes 131104 | tf_op jit(solution)/shard_map/ppermute | solution.py:73
  141.3 1.6 fusion.45
  142.9 1.4 collective-permute-start.3
  144.3 4.8 %collective-permute-done.3 = bf16[128,512]{1,0:T(8,128)(2,1)} collective-permute-done((bf16[128,512]{1,0:T(8,128)(2,1)}, bf16[128,512]{1,0:T(8,128)(2,1)}, u32[]{:S(2)}, u32[]{:S(2)}) %collective-permute-start.3) | collective-permute-done | bytes 131104 | tf_op jit(solution)/shard_map/ppermute | solution.py:73
  149.1 1.0 fusion.44
  150.1 3.3 %collective-permute-start.5 = (bf16[128,512]{1,0:T(8,128)(2,1)S(1)}, bf16[128,512]{1,0:T(8,128)(2,1)S(1)}, u32[]{:S(2)}, u32[]{:S(2)}) collective-permute-start(bf16[128,512]{1,0:T(8,128)(2,1)S(1)} %get-tuple-element.23), channel_id=1, source_target_pairs={{0,6},{2,0},{4,2},{6,4},{1,7},{3,1},{5,3},{7,5},{8,14},{10,8},{12,... | collective-permute-start | bytes 393224 | tf_op jit(solution)/shard_map/ppermute | solution.py:74
  153.4 2.5 %collective-permute-done.5 = bf16[128,512]{1,0:T(8,128)(2,1)S(1)} collective-permute-done((bf16[128,512]{1,0:T(8,128)(2,1)S(1)}, bf16[128,512]{1,0:T(8,128)(2,1)S(1)}, u32[]{:S(2)}, u32[]{:S(2)}) %collective-permute-start.5) | collective-permute-done | bytes 131104 | tf_op jit(solution)/shard_map/ppermute | solution.py:74
  156.0 0.7 fusion.42
  156.6 2.4 %collective-permute-start.6 = (bf16[128,512]{1,0:T(8,128)(2,1)}, bf16[128,512]{1,0:T(8,128)(2,1)}, u32[]{:S(2)}, u32[]{:S(2)}) collective-permute-start(bf16[128,512]{1,0:T(8,128)(2,1)} %fusion.42), channel_id=1, source_target_pairs={{0,6},{2,0},{4,2},{6,4},{1,7},{3,1},{5,3},{7,5},{8,14},{10,8},{12,... | collective-permute-start | bytes 393224 | tf_op jit(solution)/shard_map/ppermute | solution.py:74
  159.1 1.7 copy_bitcast_fusion.1
  160.8 4.0 %all-to-all-start.4 = ((bf16[4,128,256]{1,2,0:T(8,128)(2,1)}), bf16[4,128,256]{1,2,0:T(8,128)(2,1)}, u32[]{:S(2)}, u32[]{:S(2)}) async-start(bf16[4,128,256]{1,2,0:T(8,128)(2,1)} %copy_bitcast_fusion.1), calls=%async_computation.5 | async-start | bytes 524288 | tf_op jit(solution)/shard_map/all_to_all | solution.py:93
  164.9 0.9 fusion.41
  165.8 0.7 pad_maximum_fusion.2
  166.6 5.0 %all-to-all-done.4 = bf16[4,128,256]{1,2,0:T(8,128)(2,1)} async-done(((bf16[4,128,256]{1,2,0:T(8,128)(2,1)}), bf16[4,128,256]{1,2,0:T(8,128)(2,1)}, u32[]{:S(2)}, u32[]{:S(2)}) %all-to-all-start.4) | async-done | bytes 262176 | tf_op jit(solution)/shard_map/all_to_all | solution.py:93
  171.6 1.0 reduce_sum.64
  172.6 1.9 copy_bitcast_fusion
  174.6 4.1 %all-to-all-start.5 = ((bf16[4,128,512]{1,2,0:T(8,128)(2,1)}), bf16[4,128,512]{1,2,0:T(8,128)(2,1)}, u32[]{:S(2)}, u32[]{:S(2)}) async-start(bf16[4,128,512]{1,2,0:T(8,128)(2,1)} %copy_bitcast_fusion), calls=%async_computation.7 | async-start | bytes 1048576 | tf_op jit(solution)/shard_map/all_to_all | solution.py:93
  179.2 0.8 copy.97
  180.0 6.9 %all-to-all-done.5 = bf16[4,128,512]{1,2,0:T(8,128)(2,1)} async-done(((bf16[4,128,512]{1,2,0:T(8,128)(2,1)}), bf16[4,128,512]{1,2,0:T(8,128)(2,1)}, u32[]{:S(2)}, u32[]{:S(2)}) %all-to-all-start.5) | async-done | bytes 524320 | tf_op jit(solution)/shard_map/all_to_all | solution.py:93
  186.8 1.1 reduce_sum.65
  188.0 0.8 copy.98
  (76 shorter events, 2.8 us)
Async XLA Ops:
  7.2 8.9 %copy-start = (bf16[256,4096]{1,0:T(8,128)(2,1)S(1)}, bf16[256,4096]{1,0:T(8,128)(2,1)}, u32[]{:S(2)}) copy-start(bf16[256,4096]{1,0:T(8,128)(2,1)} %param.5) | copy-start | bytes 6291460
  19.5 32.5 %copy-start.7 = (bf16[256,2,2,128]{3,0,2,1:T(8,128)(2,1)}, bf16[256,2,2,128]{3,0,2,1:T(8,128)(2,1)S(1)}, u32[]{:S(2)}) copy-start(bf16[256,2,2,128]{3,0,2,1:T(8,128)(2,1)S(1)} %fusion.10) | copy-start | bytes 786436
  20.3 24.1 %all-to-all-start = ((bf16[32,2,2,1,8,128]{5,4,2,1,3,0:T(8,128)(2,1)}), bf16[32,2,2,1,8,128]{5,4,2,1,3,0:T(8,128)(2,1)S(1)}, u32[]{:S(2)}, u32[]{:S(2)}) async-start(bf16[32,2,2,1,8,128]{5,4,2,1,3,0:T(8,128)(2,1)} %copy_bitcast_fusion.3), calls=%async_computation | async-start | bytes 524288 | tf_op jit(solution)/shard_map/all_to_all | solution.py:35
  31.6 12.8 %copy-start.22 = (s32[1,32]{1,0:T(1,128)S(1)}, s32[1,32]{1,0:T(1,128)}, u32[]{:S(2)}) copy-start(s32[1,32]{1,0:T(1,128)} %param.7) | copy-start | bytes 388
  31.7 18.5 %copy-start.21 = (s32[256,64]{0,1:T(8,128)S(1)}, s32[256,64]{0,1:T(8,128)}, u32[]{:S(2)}) copy-start(s32[256,64]{0,1:T(8,128)} %param.8) | copy-start | bytes 196612
  31.7 18.6 %copy-start.20 = (bf16[256,256]{1,0:T(8,128)(2,1)S(1)}, bf16[256,256]{1,0:T(8,128)(2,1)}, u32[]{:S(2)}) copy-start(bf16[256,256]{1,0:T(8,128)(2,1)} %param.9) | copy-start | bytes 393220
  34.1 18.0 %copy-start.14 = (bf16[2,256,128]{2,1,0:T(8,128)(2,1)}, bf16[2,256,128]{2,1,0:T(8,128)(2,1)S(1)}, u32[]{:S(2)}) copy-start(bf16[2,256,128]{2,1,0:T(8,128)(2,1)S(1)} %fusion.28) | copy-start | bytes 393220
  45.5 16.5 %all-to-all-start.1 = ((bf16[32,2,2,1,8,128]{5,4,2,3,1,0:T(8,128)(2,1)}), bf16[32,2,2,1,8,128]{5,4,2,3,1,0:T(8,128)(2,1)}, u32[]{:S(2)}, u32[]{:S(2)}) async-start(bf16[32,2,2,1,8,128]{5,4,2,3,1,0:T(8,128)(2,1)} %bitcast.20), calls=%async_computation.1 | async-start | bytes 524288 | tf_op jit(solution)/shard_map/all_to_all | solution.py:40
  50.1 109.0 %reduce-scatter.3.cloned.1.call-start = ((), (), s32[]{:S(2)}) async-start(), calls=%async_computation.8 | async-start | bytes 2359296 | tf_op jit(solution)/shard_map/reduce_scatter | solution.py:87
  50.1 0.6 copy-start.16
  50.2 0.6 copy-start.18
  62.0 2.5 %copy-start.12 = (f32[2,256,256]{1,2,0:T(8,128)S(1)}, f32[2,256,256]{1,2,0:T(8,128)}, u32[]{:S(2)}) copy-start(f32[2,256,256]{1,2,0:T(8,128)} %get-tuple-element.39) | copy-start | bytes 1572868
  63.0 4.1 %copy-start.10 = (bf16[32,2,2,1,8,128]{5,4,0,2,3,1:T(8,128)(2,1)}, bf16[32,2,2,1,8,128]{5,4,0,2,3,1:T(8,128)(2,1)S(1)}, u32[]{:S(2)}) copy-start(bf16[32,2,2,1,8,128]{5,4,0,2,3,1:T(8,128)(2,1)S(1)} %copy.143) | copy-start | bytes 786436
  64.3 0.8 copy-start.17
  64.3 0.8 copy-start.19
  64.8 2.1 %copy-start.8 = (bf16[256,2,2,128]{3,0,2,1:T(8,128)(2,1)S(1)}, bf16[256,2,2,128]{3,0,2,1:T(8,128)(2,1)}, u32[]{:S(2)}) copy-start(bf16[256,2,2,128]{3,0,2,1:T(8,128)(2,1)} %copy-done.7) | copy-start | bytes 786436
  66.2 0.7 copy-start.3
  66.2 1.0 copy-start.5
  69.5 0.9 copy-start.6
  69.5 1.0 copy-start.15
  71.7 17.9 %all-to-all-start.2 = ((bf16[32,2,2,1,8,128]{5,4,2,1,3,0:T(8,128)(2,1)}), bf16[32,2,2,1,8,128]{5,4,2,1,3,0:T(8,128)(2,1)S(1)}, u32[]{:S(2)}, u32[]{:S(2)}) async-start(bf16[32,2,2,1,8,128]{5,4,2,1,3,0:T(8,128)(2,1)} %copy_bitcast_fusion.2), calls=%async_computation.2 | async-start | bytes 524288 | tf_op jit(solution)/shard_map/all_to_all | solution.py:35
  75.6 35.3 %copy-start.4 = (bf16[2,256,256]{1,2,0:T(8,128)(2,1)S(1)}, bf16[2,256,256]{1,2,0:T(8,128)(2,1)}, u32[]{:S(2)}) copy-start(bf16[2,256,256]{1,2,0:T(8,128)(2,1)} %copy-done.3) | copy-start | bytes 786436
  75.6 97.0 %reduce-scatter.5.cloned.1.call-start = ((), (), s32[]{:S(2)}) async-start(), calls=%async_computation.9 | async-start | bytes 4718592 | tf_op jit(solution)/shard_map/reduce_scatter | solution.py:162
  89.8 22.3 %copy-start.1 = (bf16[2,256,256]{1,2,0:T(8,128)(2,1)S(1)}, bf16[2,256,256]{1,2,0:T(8,128)(2,1)}, u32[]{:S(2)}) copy-start(bf16[2,256,256]{1,2,0:T(8,128)(2,1)} %get-tuple-element.36) | copy-start | bytes 786436
  121.3 1.4 copy-start.13
  122.8 3.1 %collective-permute-start = (bf16[4,256,512]{2,1,0:T(8,128)(2,1)S(1)}, bf16[4,256,512]{2,1,0:T(8,128)(2,1)}, u32[]{:S(2)}, u32[]{:S(2)}) collective-permute-start(bf16[4,256,512]{2,1,0:T(8,128)(2,1)S(1)} %dynamic-slice_bitcast_fusion), channel_id=1, source_target_pairs={{0,1},{1,0},{2,3},{3,2},{4,5},{5,4},{6,7},{7,6},{8,9},{9,8},{10,11... | collective-permute-start | bytes 3145736 | tf_op jit(solution)/shard_map/ppermute | solution.py:60
  128.6 5.9 %collective-permute-start.1 = (bf16[128,512]{1,0:T(8,128)(2,1)}, bf16[128,512]{1,0:T(8,128)(2,1)}, u32[]{:S(2)}, u32[]{:S(2)}) collective-permute-start(bf16[128,512]{1,0:T(8,128)(2,1)} %get-tuple-element.24), channel_id=1, source_target_pairs={{0,2},{2,4},{4,6},{6,0},{1,3},{3,5},{5,7},{7,1},{8,10},{10,12},{12... | collective-permute-start | bytes 393224 | tf_op jit(solution)/shard_map/ppermute | solution.py:73
  136.0 5.3 %collective-permute-start.2 = (bf16[128,512]{1,0:T(8,128)(2,1)}, bf16[128,512]{1,0:T(8,128)(2,1)}, u32[]{:S(2)}, u32[]{:S(2)}) collective-permute-start(bf16[128,512]{1,0:T(8,128)(2,1)} %fusion.46), channel_id=1, source_target_pairs={{0,2},{2,4},{4,6},{6,0},{1,3},{3,5},{5,7},{7,1},{8,10},{10,12},{12... | collective-permute-start | bytes 393224 | tf_op jit(solution)/shard_map/ppermute | solution.py:73
  137.4 6.9 %collective-permute-start.4 = (bf16[128,512]{1,0:T(8,128)(2,1)S(1)}, bf16[128,512]{1,0:T(8,128)(2,1)}, u32[]{:S(2)}, u32[]{:S(2)}) collective-permute-start(bf16[128,512]{1,0:T(8,128)(2,1)S(1)} %get-tuple-element.25), channel_id=1, source_target_pairs={{0,6},{2,0},{4,2},{6,4},{1,7},{3,1},{5,3},{7,5},{8,14},{10,8},{12,... | collective-permute-start | bytes 393224 | tf_op jit(solution)/shard_map/ppermute | solution.py:74
  142.9 6.2 %collective-permute-start.3 = (bf16[128,512]{1,0:T(8,128)(2,1)}, bf16[128,512]{1,0:T(8,128)(2,1)}, u32[]{:S(2)}, u32[]{:S(2)}) collective-permute-start(bf16[128,512]{1,0:T(8,128)(2,1)} %fusion.45), channel_id=1, source_target_pairs={{0,2},{2,4},{4,6},{6,0},{1,3},{3,5},{5,7},{7,1},{8,10},{10,12},{12... | collective-permute-start | bytes 393224 | tf_op jit(solution)/shard_map/ppermute | solution.py:73
  150.1 5.8 %collective-permute-start.5 = (bf16[128,512]{1,0:T(8,128)(2,1)S(1)}, bf16[128,512]{1,0:T(8,128)(2,1)S(1)}, u32[]{:S(2)}, u32[]{:S(2)}) collective-permute-start(bf16[128,512]{1,0:T(8,128)(2,1)S(1)} %get-tuple-element.23), channel_id=1, source_target_pairs={{0,6},{2,0},{4,2},{6,4},{1,7},{3,1},{5,3},{7,5},{8,14},{10,8},{12,... | collective-permute-start | bytes 393224 | tf_op jit(solution)/shard_map/ppermute | solution.py:74
  156.6 8.2 %collective-permute-start.6 = (bf16[128,512]{1,0:T(8,128)(2,1)}, bf16[128,512]{1,0:T(8,128)(2,1)}, u32[]{:S(2)}, u32[]{:S(2)}) collective-permute-start(bf16[128,512]{1,0:T(8,128)(2,1)} %fusion.42), channel_id=1, source_target_pairs={{0,6},{2,0},{4,2},{6,4},{1,7},{3,1},{5,3},{7,5},{8,14},{10,8},{12,... | collective-permute-start | bytes 393224 | tf_op jit(solution)/shard_map/ppermute | solution.py:74
  160.8 10.8 %all-to-all-start.4 = ((bf16[4,128,256]{1,2,0:T(8,128)(2,1)}), bf16[4,128,256]{1,2,0:T(8,128)(2,1)}, u32[]{:S(2)}, u32[]{:S(2)}) async-start(bf16[4,128,256]{1,2,0:T(8,128)(2,1)} %copy_bitcast_fusion.1), calls=%async_computation.5 | async-start | bytes 524288 | tf_op jit(solution)/shard_map/all_to_all | solution.py:93
  165.8 12.9 %copy-start.2 = (bf16[2,256,256]{1,2,0:T(8,128)(2,1)S(1)}, bf16[2,256,256]{1,2,0:T(8,128)(2,1)}, u32[]{:S(2)}) copy-start(bf16[2,256,256]{1,2,0:T(8,128)(2,1)} %get-tuple-element.36) | copy-start | bytes 786436
  165.8 12.9 %copy-start.9 = (bf16[256,2,2,128]{3,0,2,1:T(8,128)(2,1)S(1)}, bf16[256,2,2,128]{3,0,2,1:T(8,128)(2,1)}, u32[]{:S(2)}) copy-start(bf16[256,2,2,128]{3,0,2,1:T(8,128)(2,1)} %copy-done.7) | copy-start | bytes 786436
  165.8 13.1 %copy-start.11 = (bf16[32,2,2,1,8,128]{5,4,0,2,3,1:T(8,128)(2,1)S(1)}, bf16[32,2,2,1,8,128]{5,4,0,2,3,1:T(8,128)(2,1)}, u32[]{:S(2)}) copy-start(bf16[32,2,2,1,8,128]{5,4,0,2,3,1:T(8,128)(2,1)} %copy-done.10) | copy-start | bytes 786436
  174.6 12.3 %all-to-all-start.5 = ((bf16[4,128,512]{1,2,0:T(8,128)(2,1)}), bf16[4,128,512]{1,2,0:T(8,128)(2,1)}, u32[]{:S(2)}, u32[]{:S(2)}) async-start(bf16[4,128,512]{1,2,0:T(8,128)(2,1)} %copy_bitcast_fusion), calls=%async_computation.7 | async-start | bytes 1048576 | tf_op jit(solution)/shard_map/all_to_all | solution.py:93
Sparse Core Ops, SparseCore 0:
  69.7 43.2 reduce-scatter.2
  116.7 53.5 reduce-scatter.4
